TPU v7x, 128 devices: a whole 4x4x4 slice. The times are simulated.
128 devices in a mesh: blk: 4 (over x_hi, core), aux: 32 (over x_lo, y, z).
Axes of the slice: x: 4 (x_hi: 2, x_lo: 2; x = x_hi * 2 + x_lo), y: 4, z: 4, core: 2. Of those that a mesh axis runs over, the one named last changes fastest.
Arguments:
- tensor: bfloat16 [512, 512, 4096], P('blk', None, 'aux'), may hold values from -0.25 to 0.25
- greens: bfloat16 [2, 512, 512], P(None, None, 'blk'), may hold values from -0.25 to 0.25
- pattern: int32 [4, 4, 32], P('blk', None, 'aux'), may hold values from 0 to 1, as said below
- block_sizes: int32 [4], replicated, may hold values from 64 to 128, as said below
- trial_vectors: bfloat16 [4096, 32], P('aux'), may hold values from -0.09375 to 0.09375
Outputs:
- response: float32 [32, 4096], P('blk', 'aux')
Inputs may be any that keep to these rules, and one draw needn't show every extreme that they name: pattern[mu, nu, p] is 1 exactly where |mu - nu| is at most a reach drawn for auxiliary block p, so every diagonal entry is 1. The first block_sizes[b] basis functions of atom block b are live, the rest are padding; some block is full and some block has exactly half of its functions live.
All inputs are finite; a program needn't handle non-finite values.
Results may differ from a plain program's by a relative error of at most 0.0049.
Values may be sent and summed in bfloat16 or wider, within the bound.
No kernel may reach another device: no remote copies, remote signals or barrier semaphores. Data moves between devices by JAX's collectives and lax.ppermute only.
A program may use at most 256 MiB of HBM per device.

v0:
```python
import jax
import jax.numpy as jnp
from jax import lax
from jax.sharding import PartitionSpec as P

BS = 128
PS = 128
MB_DEV = 1
PB_DEV = 1


def combine_terms(
    projected, left_moved, group_count, owner_count, shard_rows, piece_rows, vector_share, aux_local
):
    projected = projected.reshape(group_count, shard_rows, piece_rows, group_count, vector_share)
    left_moved = left_moved.reshape(group_count, owner_count, piece_rows, shard_rows, aux_local)
    terms = jnp.einsum(
        "bricd,bairp->cadp", projected, left_moved, preferred_element_type=jnp.float32
    )
    return terms.reshape(group_count * owner_count * vector_share, aux_local)


def per_device(tensor, greens, pattern, block_sizes, trial_vectors):
    shard_rows = tensor.shape[0]
    basis_count = tensor.shape[1]
    aux_local = tensor.shape[2]
    group_count = lax.axis_size("blk")
    owner_count = lax.axis_size("aux")
    piece_rows = shard_rows // owner_count
    block_count = block_sizes.shape[0]
    live_mask = (jnp.arange(BS)[None, :] < block_sizes[:, None]).reshape(basis_count)
    row_live = lax.dynamic_slice_in_dim(live_mask, lax.axis_index("blk") * shard_rows, shard_rows)
    tile_mask = jnp.broadcast_to(
        pattern[:, None, :, None, :, None] > 0, (MB_DEV, BS, block_count, BS, PB_DEV, PS)
    )
    keep_mask = tile_mask.reshape(shard_rows, basis_count, aux_local)
    keep_mask = keep_mask & row_live[:, None, None] & live_mask[None, :, None]
    screened = jnp.where(keep_mask, tensor, jnp.zeros_like(tensor))
    products = jnp.einsum(
        "rsp,gsc->gcrp",
        screened,
        lax.all_gather(greens, "blk", axis=2, tiled=True),
        preferred_element_type=jnp.float32,
    )
    halves = products.astype(jnp.bfloat16)
    left_half = halves[0]
    right_half = halves[1]
    vector_count = trial_vectors.shape[1]
    vector_share = vector_count // group_count
    left_moved = lax.all_to_all(left_half, ("blk", "aux"), split_axis=0, concat_axis=0, tiled=True)
    right_moved = lax.all_to_all(right_half, "aux", split_axis=1, concat_axis=2, tiled=True)
    all_vectors = lax.all_gather(trial_vectors, "aux", axis=0, tiled=True)
    projected = jnp.einsum(
        "niq,qk->nik", right_moved, all_vectors, preferred_element_type=jnp.float32
    )
    projected = projected.astype(jnp.bfloat16)
    terms = combine_terms(
        projected,
        left_moved,
        group_count,
        owner_count,
        shard_rows,
        piece_rows,
        vector_share,
        aux_local,
    )
    return lax.psum_scatter(terms, ("blk", "aux"), scatter_dimension=0, tiled=True)


def solution(mesh):
    placed = (
        P("blk", None, "aux"),
        P(None, None, "blk"),
        P("blk", None, "aux"),
        P(),
        P("aux", None),
    )
    return jax.shard_map(
        per_device, mesh=mesh, in_specs=placed, out_specs=P("blk", "aux"), check_vma=False
    )
```

profile of v0, /device:TPU:1, one launch (start us, length us, event | category | flops | bytes accessed | tf_op | source)
XLA Modules:
  0.0 917.2 jit_solution(2484546159178420518)
XLA Ops:
  6.5 0.0 all-gather.2.cloned.1.call-start
  6.5 0.7 all-gather.2.cloned.1.call-update
  7.3 0.7 compare_bitcast_fusion
  7.9 0.7 fusion.11
  8.6 0.1 dynamic_slice.3
  8.7 24.7 %all-gather.2.cloned.1.call-done = bf16[2,512,512]{2,1,0:T(8,128)(2,1)} async-done(((bf16[2,512,128]{2,1,0:T(8,128)(2,1)}), bf16[2,512,512]{2,1,0:T(8,128)(2,1)}) %all-gather.2.cloned.1.call-update) | async-done | bytes 1048592 | tf_op jit(solution)/shard_map/all_gather | solution.py:42
  33.5 28.2 %convert_bitcast_fusion = bf16[2,512,128,128]{1,3,0,2:T(8,128)(2,1)} fusion(bf16[128,512,128]{2,1,0:T(8,128)(2,1)} %param.5, pred[512]{0:T(512)(128)(4,1)S(1)} %get-tuple-element.7, pred[128]{0:T(512)(128)(4,1)S(1)} %dynamic_slice.3, pred[512]{0:T(512)(128)(4,1)S(1)} %get-tuple-element.8, bf16[2,512,512]{2,1,0:T(8,128)(2,1)} %all-gather.2.cloned.1.call-done), kind=kOutput, calls=%fused_computation | convolution fusion | flops 17221812224 | bytes 51381376 | tf_op jit(solution)/shard_map/rsp,gsc->gcrp/dot_general | solution.py:39
  61.6 23.0 %slice_bitcast_fusion = (bf16[512,128,128]{0,2,1:T(8,128)(2,1)}, bf16[512,128,128]{0,2,1:T(8,128)(2,1)}) fusion(bf16[2,512,128,128]{1,3,0,2:T(8,128)(2,1)} %convert_bitcast_fusion), kind=kLoop, calls=%fused_computation.3 | loop fusion | bytes 67108864 | tf_op jit(solution)/shard_map/squeeze | solution.py:47
  84.7 7.1 all-to-all-start.1
  91.8 23.7 %copy.17 = bf16[512,128,128]{2,1,0:T(8,128)(2,1)} copy(bf16[512,128,128]{0,2,1:T(8,128)(2,1)} %get-tuple-element.6) | data formatting | bytes 33554432 | tf_op jit(solution)/shard_map/squeeze | solution.py:46
  115.5 277.0 %all-to-all-done.1 = bf16[512,128,128]{0,2,1:T(8,128)(2,1)} async-done(((bf16[512,128,128]{0,2,1:T(8,128)(2,1)}), bf16[512,128,128]{0,2,1:T(8,128)(2,1)}, u32[]{:S(2)}, u32[]{:S(2)}) %all-to-all-start.1) | async-done | bytes 16777248 | tf_op jit(solution)/shard_map/all_to_all | solution.py:51
  392.5 6.1 all-to-all-start
  398.6 0.0 all-reduce.3.cloned.1.call-start
  398.6 0.0 copy-done
  398.7 269.0 %all_gather.7 = bf16[4096,32]{0,1:T(8,128)(2,1)S(1)} all-gather(bf16[128,32]{0,1:T(8,128)(2,1)S(1)} %copy-done), channel_id=1, replica_groups=mesh['blk'=4,'aux'=32] {'aux'}, dimensions={0}, use_global_device_ids=true | all-gather | bytes 270336 | tf_op jit(solution)/shard_map/all_gather | solution.py:52
  667.7 28.6 %copy.18 = bf16[512,4,32,128]{3,2,0,1:T(8,128)(2,1)} copy(bf16[512,4,32,128]{0,3,1,2:T(8,128)(2,1)} %bitcast.12) | data formatting | bytes 33554432 | tf_op jit(solution)/shard_map/all_to_all | solution.py:51
  696.2 25.3 %all_to_all.20 = bf16[512,4,4096]{2,0,1:T(8,128)(2,1)} reshape(bf16[512,4,32,128]{3,2,0,1:T(8,128)(2,1)} %copy.18) | data formatting | bytes 33554432 | tf_op jit(solution)/shard_map/all_to_all | solution.py:51
  721.6 10.8 %fusion.6 = bf16[4,128,4,4,8,1]{1,4,0,3,2,5:T(8,128)(2,1)S(1)} fusion(bf16[512,4,4096]{2,0,1:T(8,128)(2,1)} %all_to_all.20, bf16[4096,32]{0,1:T(8,128)(2,1)S(1)} %all_gather.7), kind=kOutput, calls=%fused_computation.10 | convolution fusion | flops 536936448 | bytes 17170432 | tf_op jit(solution)/shard_map/niq,qk->nik/dot_general | solution.py:53
  732.4 0.0 all-to-all-done
  732.4 7.3 fusion.9
  739.6 0.8 copy.23
  740.4 0.0 all-reduce.3.cloned.1.call-update
  740.5 168.6 %all-reduce.3.cloned.1.call-done = f32[1024,128]{1,0:T(8,128)} async-done(((f32[1024,128]{1,0:T(8,128)}), f32[1024,128]{1,0:T(8,128)}) %all-reduce.3.cloned.1.call-update) | async-done | bytes 524304
  909.1 1.3 constant_dynamic-slice_fusion
  (1 shorter events, 0.0 us)
Async XLA Ops:
  6.5 26.9 %all-gather.2.cloned.1.call-start = ((), (), s32[]{:S(2)}) async-start(), calls=%async_computation.2 | async-start | bytes 1310720 | tf_op jit(solution)/shard_map/all_gather | solution.py:42
  84.7 307.8 %all-to-all-start.1 = ((bf16[512,128,128]{0,2,1:T(8,128)(2,1)}), bf16[512,128,128]{0,2,1:T(8,128)(2,1)}, u32[]{:S(2)}, u32[]{:S(2)}) async-start(bf16[512,128,128]{0,2,1:T(8,128)(2,1)} %get-tuple-element.5), calls=%async_computation.1 | async-start | bytes 33554432 | tf_op jit(solution)/shard_map/all_to_all | solution.py:51
  115.5 283.1 %copy-start = (bf16[128,32]{0,1:T(8,128)(2,1)S(1)}, bf16[128,32]{0,1:T(8,128)(2,1)}, u32[]{:S(2)}) copy-start(bf16[128,32]{0,1:T(8,128)(2,1)} %param.9) | copy-start | bytes 24580
  392.5 339.9 %all-to-all-start = ((bf16[512,128,128]{2,1,0:T(8,128)(2,1)}), bf16[512,128,128]{2,1,0:T(8,128)(2,1)}, u32[]{:S(2)}, u32[]{:S(2)}) async-start(bf16[512,128,128]{2,1,0:T(8,128)(2,1)} %copy.17), calls=%async_computation | async-start | bytes 33554432 | tf_op jit(solution)/shard_map/all_to_all | solution.py:50
  398.6 510.5 %all-reduce.3.cloned.1.call-start = ((), (), s32[]{:S(2)}) async-start(), calls=%async_computation.3 | async-start | bytes 1048576
Sparse Core Ops, SparseCore 0:
  9.0 24.4 all-gather.1
  740.6 168.4 all-reduce.2
where the time goes:
time: 919 us; the launch traced here: 917 us
  waiting for transfers between devices  471 us (51%)
  blocking collectives  269 us (29%)
  local copies, waits for them, and re-layouts  103 us (11%)
  matrix products  46.2 us (5%)
  between operations  13.5 us (1%)
  starting transfers between devices  13.3 us (1%)
    all_to_all x1, waiting for transfers between devices, per_device(): lax.all_to_all(right_half, 'aux', split_axis=1, concat_axis=2, tiled=True)  277 us
    all_gather x1, blocking collectives, per_device(): all_vectors = lax.all_gather(trial_vectors, 'aux', axis=0, tiled=True)  269 us
    unnamed x3, waiting for transfers between devices  169 us
    all_to_all x2, local copies, waits for them, and re-layouts, per_device(): lax.all_to_all(right_half, 'aux', split_axis=1, concat_axis=2, tiled=True)  53.9 us
    dot_general x1, matrix products, per_device(): jnp.einsum('rsp,gsc->gcrp', screened, lax.all_gather(greens, 'blk', axis=...  28.2 us
    all_gather x1, waiting for transfers between devices, per_device(): lax.all_gather(greens, 'blk', axis=2, tiled=True)  24.7 us
    squeeze x1, local copies, waits for them, and re-layouts, per_device(): left_half = halves[0]  23.7 us
    squeeze x1, local copies, waits for them, and re-layouts, per_device(): right_half = halves[1]  23 us
  transfers between devices with their start and end apart: 4, of which 3 were waited for; matrix products, arithmetic and copies ran while one was open for 7% of the time, Pallas kernels for 0%

commit v1 on v0

v1 whole, which is shorter than its diff:
```python
import jax
import jax.numpy as jnp
from jax import lax
from jax.sharding import PartitionSpec as P

BS = 128
PS = 128
MB_DEV = 1
PB_DEV = 1
HI = lax.Precision.HIGHEST


def per_device(tensor, greens, pattern, block_sizes, trial_vectors):
    shard_rows = tensor.shape[0]
    basis_count = tensor.shape[1]
    aux_local = tensor.shape[2]
    block_count = block_sizes.shape[0]
    live_mask = (jnp.arange(BS)[None, :] < block_sizes[:, None]).reshape(basis_count)
    row_live = lax.dynamic_slice_in_dim(live_mask, lax.axis_index("blk") * shard_rows, shard_rows)
    tile_mask = jnp.broadcast_to(
        pattern[:, None, :, None, :, None] > 0, (MB_DEV, BS, block_count, BS, PB_DEV, PS)
    )
    keep_mask = tile_mask.reshape(shard_rows, basis_count, aux_local)
    keep_mask = keep_mask & row_live[:, None, None] & live_mask[None, :, None]
    screened = jnp.where(keep_mask, tensor, jnp.zeros_like(tensor))

    weighted = jnp.einsum(
        "rsp,pk->krs", screened, trial_vectors, preferred_element_type=jnp.float32
    )
    weighted = lax.psum_scatter(weighted, "aux", scatter_dimension=0, tiled=True)[0]
    virtual = lax.all_gather(greens[1], "blk", axis=1, tiled=True).astype(jnp.float32)
    occupied_cols = greens[0].astype(jnp.float32)
    projected = jnp.dot(weighted, virtual, precision=HI)
    z_part = jnp.einsum("ln,sl->ns", projected, occupied_cols, precision=HI)
    z_rows = lax.psum_scatter(z_part, "blk", scatter_dimension=0, tiled=True)
    z_all = lax.all_gather(z_rows.astype(jnp.bfloat16), "aux", axis=0, tiled=False)
    terms = jnp.einsum(
        "nsp,kns->kp", screened, z_all, preferred_element_type=jnp.float32
    )
    return lax.psum_scatter(terms, "blk", scatter_dimension=0, tiled=True)


def solution(mesh):
    placed = (
        P("blk", None, "aux"),
        P(None, None, "blk"),
        P("blk", None, "aux"),
        P(),
        P("aux", None),
    )
    return jax.shard_map(
        per_device, mesh=mesh, in_specs=placed, out_specs=P("blk", "aux"), check_vma=False
    )
```

time: 919 us -> 444 us (0.48)
  blocking collectives: 269 us -> 42.4 us
  waiting for transfers between devices: 471 us -> 337 us
  local copies, waits for them, and re-layouts: 103 us -> 15.9 us
  matrix products: 46.2 us -> 19.3 us
  other arithmetic: 1.39 us -> 15 us
  starting transfers between devices: 13.3 us -> 0.27 us
    all_to_all x2 -> x0, waiting for transfers between devices: 277 us -> none  [the longest x1 277 us: per_device(): lax.all_to_all(right_half, 'aux', split_axis=1, concat_axis=2, tiled=True)]
    all_gather x1, blocking collectives: 269 us -> 10 us  [per_device(): lax.all_gather(greens[1], 'blk', axis=1, tiled=True).astype(jnp.float32)]
    reduce_scatter x0 -> x2, waiting for transfers between devices: none -> 202 us  [the longest x1 150 us: per_device(): lax.psum_scatter(weighted, 'aux', scatter_dimension=0, tiled=True)[0]]
    unnamed x3, waiting for transfers between devices: 169 us -> 0.05 us
    all_gather x1, waiting for transfers between devices: 24.7 us -> 135 us  [per_device(): lax.all_gather(z_rows.astype(jnp.bfloat16), 'aux', axis=0, tiled=False)]
    all_to_all x2 -> x0, local copies, waits for them, and re-layouts: 53.9 us -> none  [per_device(): lax.all_to_all(right_half, 'aux', split_axis=1, concat_axis=2, tiled=True)]
    squeeze x2 -> x0, local copies, waits for them, and re-layouts: 46.7 us -> none  [the longest x1 23.7 us: per_device(): left_half = halves[0]]
    unnamed x0 -> x1, blocking collectives: none -> 32.3 us
  transfers between devices with their start and end apart: 4 -> 3, of which waited for: 3 -> 3; matrix products, arithmetic and copies ran while one was open for 7% -> 0% of each run, Pallas kernels for 0% -> 0%
where the time goes in v1:
time: 444 us; the launch traced here: 443 us
  waiting for transfers between devices  337 us (76%)
  blocking collectives  42.4 us (10%)
  matrix products  19.3 us (4%)
  local copies, waits for them, and re-layouts  15.9 us (4%)
  other arithmetic  15 us (3%)
  between operations  13.8 us (3%)
    reduce_scatter x1, waiting for transfers between devices, per_device(): lax.psum_scatter(weighted, 'aux', scatter_dimension=0, tiled=True)[0]  150 us
    all_gather x1, waiting for transfers between devices, per_device(): lax.all_gather(z_rows.astype(jnp.bfloat16), 'aux', axis=0, tiled=False)  135 us
    reduce_scatter x1, waiting for transfers between devices, per_device(): z_rows = lax.psum_scatter(z_part, 'blk', scatter_dimension=0, tiled=True)  51.7 us
    unnamed x1, blocking collectives  32.3 us
    select_n x1, other arithmetic, per_device(): screened = jnp.where(keep_mask, tensor, jnp.zeros_like(tensor))  12 us
    dot_general x1, matrix products, per_device(): jnp.einsum('nsp,kns->kp', screened, z_all, preferred_element_type=jnp.flo...  10.5 us
    all_gather x1, blocking collectives, per_device(): lax.all_gather(greens[1], 'blk', axis=1, tiled=True).astype(jnp.float32)  10 us
  transfers between devices with their start and end apart: 3, of which 3 were waited for; matrix products, arithmetic and copies ran while one was open for 0% of the time, Pallas kernels for 0%

profile of v1, /device:TPU:1, one launch (start us, length us, event | category | flops | bytes accessed | tf_op | source)
XLA Modules:
  0.0 443.3 jit_solution(16713091900998686100)
XLA Ops:
  6.5 0.7 compare_bitcast_fusion
  7.2 0.7 fusion.12
  7.9 0.1 dynamic_slice.3
  8.0 12.0 %and_select_fusion = bf16[128,512,128]{2,1,0:T(8,128)(2,1)S(1)} fusion(bf16[128,512,128]{2,1,0:T(8,128)(2,1)} %param.5, pred[512]{0:T(512)(128)(4,1)S(1)} %get-tuple-element.5, pred[128]{0:T(512)(128)(4,1)S(1)} %dynamic_slice.3, pred[512]{0:T(512)(128)(4,1)S(1)} %get-tuple-element.6), kind=kLoop, calls=%fused_computation | loop fusion | flops 25165824 | bytes 33555584 | tf_op jit(solution)/shard_map/jit(_where)/select_n | solution.py:25
  20.0 5.7 %copy-done.1 = bf16[128,512,128]{2,1,0:T(8,128)(2,1)} copy-done((bf16[128,512,128]{2,1,0:T(8,128)(2,1)}, bf16[128,512,128]{2,1,0:T(8,128)(2,1)S(1)}, u32[]{:S(2)}) %copy-start.1) | copy-done | bytes 16777240
  25.7 5.8 %convolution_bitcast_fusion = f32[32,128,512]{2,0,1:T(8,128)S(1)} fusion(bf16[128,512,128]{2,1,0:T(8,128)(2,1)S(1)} %and_select_fusion, bf16[128,32]{0,1:T(8,128)(2,1)S(1)} %copy-done), kind=kOutput, calls=%fused_computation.3 | convolution fusion | flops 536870912 | bytes 25174016 | tf_op jit(solution)/shard_map/rsp,pk->krs/dot_general | solution.py:27
  31.6 8.1 %copy.7 = f32[32,128,512]{2,1,0:T(8,128)} copy(f32[32,128,512]{2,0,1:T(8,128)S(1)} %convolution_bitcast_fusion) | data formatting | bytes 16777216 | tf_op jit(solution)/shard_map/rsp,pk->krs/dot_general | solution.py:27
  39.7 0.0 reduce-scatter.3.cloned.1.call-update
  39.7 0.0 reduce-scatter.5.cloned.1.call-start
  39.8 0.8 slice-done
  40.6 10.0 %all-gather = bf16[1,512,512]{2,1,0:T(8,128)(2,1)S(1)} all-gather(bf16[1,512,128]{2,1,0:T(8,128)(2,1)S(1)} %slice-done), channel_id=2, replica_groups=mesh['blk'=4,'aux'=32] {'blk'}, dimensions={2}, use_global_device_ids=true | all-gather | bytes 655360 | tf_op jit(solution)/shard_map/all_gather | solution.py:31
  50.6 149.9 %reduce-scatter.3.cloned.1.call-done = f32[1,128,512]{2,1,0:T(8,128)} async-done(((f32[32,128,512]{2,1,0:T(8,128)}), f32[1,128,512]{2,1,0:T(8,128)}) %reduce-scatter.3.cloned.1.call-update) | async-done | bytes 262160 | tf_op jit(solution)/shard_map/reduce_scatter | solution.py:30
  200.6 1.3 fusion.5
  201.9 1.6 fusion.8
  203.5 0.0 reduce-scatter.5.cloned.1.call-update
  203.5 0.2 all-gather.4.cloned.1.call-start
  203.7 51.7 %reduce-scatter.5.cloned.1.call-done = f32[128,512]{1,0:T(8,128)} async-done(((f32[512,512]{1,0:T(8,128)}), f32[128,512]{1,0:T(8,128)}) %reduce-scatter.5.cloned.1.call-update) | async-done | bytes 262160 | tf_op jit(solution)/shard_map/reduce_scatter | solution.py:35
  255.5 1.6 convert_element_type.2
  257.1 0.0 all-gather.4.cloned.1.call-update
  257.1 0.6 dynamic-slice
  258.3 135.0 %all-gather.4.cloned.1.call-done = bf16[4096,512]{1,0:T(8,128)(2,1)} async-done(((bf16[128,512]{1,0:T(8,128)(2,1)}), bf16[4096,512]{1,0:T(8,128)(2,1)}) %all-gather.4.cloned.1.call-update) | async-done | bytes 4194320 | tf_op jit(solution)/shard_map/all_gather | solution.py:36
  393.4 10.5 %fusion.2 = f32[32,128]{1,0:T(8,128)S(1)} fusion(bf16[128,512,128]{2,1,0:T(8,128)(2,1)} %copy-done.1, bf16[32,128,512]{2,1,0:T(8,128)(2,1)} %bitcast.27), kind=kOutput, calls=%fused_computation.4 | convolution fusion | flops 536870912 | bytes 20987904 | tf_op jit(solution)/shard_map/nsp,kns->kp/dot_general | solution.py:37
  403.9 32.3 %all-reduce = f32[32,128]{1,0:T(8,128)S(1)} all-reduce(f32[32,128]{1,0:T(8,128)S(1)} %fusion.2), channel_id=6, replica_groups=mesh['blk'=4,'aux'=32] {'blk'}, use_global_device_ids=true, to_apply=%region_2.3.clone | all-reduce | flops 4096 | bytes 32768
  436.2 0.6 constant_dynamic-slice_fusion
  (9 shorter events, 0.0 us)
Async XLA Ops:
  6.5 19.2 %copy-start = (bf16[128,32]{0,1:T(8,128)(2,1)S(1)}, bf16[128,32]{0,1:T(8,128)(2,1)}, u32[]{:S(2)}) copy-start(bf16[128,32]{0,1:T(8,128)(2,1)} %param.9) | copy-start | bytes 24580
  6.5 194.0 %reduce-scatter.3.cloned.1.call-start = ((), (), s32[]{:S(2)}) async-start(), calls=%async_computation.2 | async-start | bytes 8650752 | tf_op jit(solution)/shard_map/reduce_scatter | solution.py:30
  20.0 5.7 %copy-start.1 = (bf16[128,512,128]{2,1,0:T(8,128)(2,1)}, bf16[128,512,128]{2,1,0:T(8,128)(2,1)S(1)}, u32[]{:S(2)}) copy-start(bf16[128,512,128]{2,1,0:T(8,128)(2,1)S(1)} %and_select_fusion) | copy-start | bytes 50331652
  39.7 0.9 slice-start
  39.7 162.2 %copy-start.2 = (bf16[2,512,128]{2,1,0:T(8,128)(2,1)S(1)}, bf16[2,512,128]{2,1,0:T(8,128)(2,1)}, u32[]{:S(2)}) copy-start(bf16[2,512,128]{2,1,0:T(8,128)(2,1)} %param.6) | copy-start | bytes 786436
  39.7 217.4 %copy-start.3 = (u32[128]{0:T(128)S(1)}, u32[128]{0:T(128)}, u32[]{:S(2)}) copy-start(u32[128]{0:T(128)} %constant.18) | copy-start | bytes 1540
  39.7 215.7 %reduce-scatter.5.cloned.1.call-start = ((), (), s32[]{:S(2)}) async-start(), calls=%async_computation.3 | async-start | bytes 1310720 | tf_op jit(solution)/shard_map/reduce_scatter | solution.py:35
  203.5 189.8 %all-gather.4.cloned.1.call-start = ((), (), s32[]{:S(2)}) async-start(), calls=%async_computation.4 | async-start | bytes 4325376 | tf_op jit(solution)/shard_map/all_gather | solution.py:36
Sparse Core Ops, SparseCore 0:
  39.8 160.6 reduce-scatter.2
  203.6 51.7 reduce-scatter.4
  257.2 136.1 all-gather.3

commit v2 on v1

--- a/solution.py
+++ b/solution.py
@@ -27,13 +27,16 @@
     weighted = jnp.einsum(
         "rsp,pk->krs", screened, trial_vectors, preferred_element_type=jnp.float32
     )
-    weighted = lax.psum_scatter(weighted, "aux", scatter_dimension=0, tiled=True)[0]
+    weighted = lax.all_to_all(weighted, "aux", split_axis=0, concat_axis=0, tiled=True)
+    weighted = jnp.sum(weighted, axis=0)
     virtual = lax.all_gather(greens[1], "blk", axis=1, tiled=True).astype(jnp.float32)
     occupied_cols = greens[0].astype(jnp.float32)
     projected = jnp.dot(weighted, virtual, precision=HI)
     z_part = jnp.einsum("ln,sl->ns", projected, occupied_cols, precision=HI)
     z_rows = lax.psum_scatter(z_part, "blk", scatter_dimension=0, tiled=True)
-    z_all = lax.all_gather(z_rows.astype(jnp.bfloat16), "aux", axis=0, tiled=False)
+    aux_count = lax.axis_size("aux")
+    z_copies = jnp.broadcast_to(z_rows.astype(jnp.bfloat16)[None], (aux_count,) + z_rows.shape)
+    z_all = lax.all_to_all(z_copies, "aux", split_axis=0, concat_axis=0, tiled=True)
     terms = jnp.einsum(
         "nsp,kns->kp", screened, z_all, preferred_element_type=jnp.float32
     )

time: 444 us -> 312 us (0.70); the launches traced: 443 us -> 306 us
  waiting for transfers between devices: 337 us -> 78.7 us
  blocking collectives: 42.4 us -> 141 us
  starting transfers between devices: 0.27 us -> 17.2 us
    reduce_scatter x1 -> x0, waiting for transfers between devices: 150 us -> none  [per_device(): lax.psum_scatter(weighted, 'aux', scatter_dimension=0, tiled=True)[0]]
    all_gather x1 -> x0, waiting for transfers between devices: 135 us -> none  [per_device(): lax.all_gather(z_rows.astype(jnp.bfloat16), 'aux', axis=0, tiled=False)]
    all_gather x1, blocking collectives: 10 us -> 128 us  [per_device(): lax.all_gather(greens[1], 'blk', axis=1, tiled=True).astype(jnp.float32)]
    all_to_all x0 -> x2, waiting for transfers between devices: none -> 48.4 us  [the longest x1 48.4 us: per_device(): lax.all_to_all(z_copies, 'aux', split_axis=0, concat_axis=0, tiled=True)]
    reduce_scatter x1, waiting for transfers between devices: 51.7 us -> 30.3 us  [per_device(): z_rows = lax.psum_scatter(z_part, 'blk', scatter_dimension=0, tiled=True)]
    unnamed x1, blocking collectives: 32.3 us -> 13.6 us
    all_to_all x0 -> x2, starting transfers between devices: none -> 17.2 us  [the longest x1 10.1 us: per_device(): lax.all_to_all(weighted, 'aux', split_axis=0, concat_axis=0, tiled=True)]
  transfers between devices with their start and end apart: 3 -> 3, of which waited for: 3 -> 2; matrix products, arithmetic and copies ran while one was open for 0% -> 0% of each run, Pallas kernels for 0% -> 0%
where the time goes in v2:
time: 312 us; the launch traced here: 306 us
  blocking collectives  141 us (45%)
  waiting for transfers between devices  78.7 us (25%)
  other arithmetic  18.6 us (6%)
  matrix products  18.3 us (6%)
  local copies, waits for them, and re-layouts  17.5 us (6%)
  starting transfers between devices  17.2 us (6%)
  between operations  14.2 us (5%)
    all_gather x1, blocking collectives, per_device(): lax.all_gather(greens[1], 'blk', axis=1, tiled=True).astype(jnp.float32)  128 us
    all_to_all x1, waiting for transfers between devices, per_device(): lax.all_to_all(z_copies, 'aux', split_axis=0, concat_axis=0, tiled=True)  48.4 us
    reduce_scatter x1, waiting for transfers between devices, per_device(): z_rows = lax.psum_scatter(z_part, 'blk', scatter_dimension=0, tiled=True)  30.3 us
    unnamed x1, blocking collectives  13.6 us
    select_n x1, other arithmetic, per_device(): screened = jnp.where(keep_mask, tensor, jnp.zeros_like(tensor))  12 us
    dot_general x1, matrix products, per_device(): jnp.einsum('nsp,kns->kp', screened, z_all, preferred_element_type=jnp.flo...  10.5 us
    all_to_all x1, starting transfers between devices, per_device(): lax.all_to_all(weighted, 'aux', split_axis=0, concat_axis=0, tiled=True)  10.1 us
    dot_general x1, local copies, waits for them, and re-layouts, per_device(): jnp.einsum('rsp,pk->krs', screened, trial_vectors, preferred_element_type...  8.09 us
  transfers between devices with their start and end apart: 3, of which 2 were waited for; matrix products, arithmetic and copies ran while one was open for 0% of the time, Pallas kernels for 0%

profile of v2, /device:TPU:1, one launch (start us, length us, event | category | flops | bytes accessed | tf_op | source)
XLA Modules:
  0.0 306.0 jit_solution(1333223601976902297)
XLA Ops:
  6.5 0.7 compare_bitcast_fusion
  7.2 0.7 fusion.12
  7.9 0.1 dynamic_slice.3
  8.0 12.0 %and_select_fusion = bf16[128,512,128]{2,1,0:T(8,128)(2,1)S(1)} fusion(bf16[128,512,128]{2,1,0:T(8,128)(2,1)} %param.5, pred[512]{0:T(512)(128)(4,1)S(1)} %get-tuple-element.5, pred[128]{0:T(512)(128)(4,1)S(1)} %dynamic_slice.3, pred[512]{0:T(512)(128)(4,1)S(1)} %get-tuple-element.6), kind=kLoop, calls=%fused_computation | loop fusion | flops 25165824 | bytes 33555584 | tf_op jit(solution)/shard_map/jit(_where)/select_n | solution.py:25
  20.0 5.7 %copy-done.2 = bf16[128,512,128]{2,1,0:T(8,128)(2,1)} copy-done((bf16[128,512,128]{2,1,0:T(8,128)(2,1)}, bf16[128,512,128]{2,1,0:T(8,128)(2,1)S(1)}, u32[]{:S(2)}) %copy-start.2) | copy-done | bytes 16777240
  25.7 5.8 %fusion.10 = f32[128,512,32]{1,2,0:T(8,128)S(1)} fusion(bf16[128,512,128]{2,1,0:T(8,128)(2,1)S(1)} %and_select_fusion, bf16[128,32]{0,1:T(8,128)(2,1)S(1)} %copy-done), kind=kOutput, calls=%fused_computation.10 | convolution fusion | flops 536870912 | bytes 25174016 | tf_op jit(solution)/shard_map/rsp,pk->krs/dot_general | solution.py:27
  31.6 8.1 %copy.13 = f32[128,512,32]{1,0,2:T(8,128)} copy(f32[128,512,32]{1,2,0:T(8,128)S(1)} %fusion.10) | data formatting | bytes 16777216 | tf_op jit(solution)/shard_map/rsp,pk->krs/dot_general | solution.py:27
  39.7 10.1 %all-to-all-start = ((f32[32,128,512]{2,1,0:T(8,128)}), f32[32,128,512]{2,1,0:T(8,128)}, u32[]{:S(2)}, u32[]{:S(2)}) async-start(f32[32,128,512]{2,1,0:T(8,128)} %bitcast.25), calls=%async_computation | async-start | bytes 16777216 | tf_op jit(solution)/shard_map/all_to_all | solution.py:30
  49.8 0.0 reduce-scatter.2.cloned.1.call-start
  49.8 127.8 %all-gather = bf16[1,512,512]{2,1,0:T(8,128)(2,1)S(1)} all-gather(bf16[1,512,128]{2,1,0:T(8,128)(2,1)S(1)} %slice-done), channel_id=2, replica_groups=mesh['blk'=4,'aux'=32] {'blk'}, dimensions={2}, use_global_device_ids=true | all-gather | bytes 655360 | tf_op jit(solution)/shard_map/all_gather | solution.py:32
  177.6 4.3 %reduce_sum.9 = f32[128,512]{1,0:T(8,128)S(1)} reduce(f32[32,128,512]{2,1,0:T(8,128)} %all-to-all-done, f32[]{:T(128)} %constant.16.clone.1), dimensions={0}, to_apply=%region_0.1 | reduce | flops 2031616 | bytes 8650756 | tf_op jit(solution)/shard_map/reduce_sum | solution.py:31
  181.9 0.0 copy-start.4
  181.9 0.4 fusion.5
  182.3 1.6 fusion.7
  183.9 0.0 reduce-scatter.2.cloned.1.call-update
  183.9 30.3 %reduce-scatter.2.cloned.1.call-done = f32[128,512]{1,0:T(8,128)} async-done(((f32[512,512]{1,0:T(8,128)}), f32[128,512]{1,0:T(8,128)}) %reduce-scatter.2.cloned.1.call-update) | async-done | bytes 262160 | tf_op jit(solution)/shard_map/reduce_scatter | solution.py:36
  214.3 1.0 convert_element_type.2
  215.2 2.4 broadcast_in_dim.26
  217.7 7.1 %all-to-all-start.1 = ((bf16[32,128,512]{2,1,0:T(8,128)(2,1)}), bf16[32,128,512]{2,1,0:T(8,128)(2,1)}, u32[]{:S(2)}, u32[]{:S(2)}) async-start(bf16[32,128,512]{2,1,0:T(8,128)(2,1)} %broadcast_in_dim.26), calls=%async_computation.2 | async-start | bytes 8388608 | tf_op jit(solution)/shard_map/all_to_all | solution.py:39
  224.8 0.6 dynamic-slice
  226.1 48.4 %all-to-all-done.1 = bf16[32,128,512]{2,1,0:T(8,128)(2,1)} async-done(((bf16[32,128,512]{2,1,0:T(8,128)(2,1)}), bf16[32,128,512]{2,1,0:T(8,128)(2,1)}, u32[]{:S(2)}, u32[]{:S(2)}) %all-to-all-start.1) | async-done | bytes 4194336 | tf_op jit(solution)/shard_map/all_to_all | solution.py:39
  274.5 10.5 %fusion.2 = f32[32,128]{1,0:T(8,128)S(1)} fusion(bf16[128,512,128]{2,1,0:T(8,128)(2,1)} %copy-done.2, bf16[32,128,512]{2,1,0:T(8,128)(2,1)} %all-to-all-done.1), kind=kOutput, calls=%fused_computation.4 | convolution fusion | flops 536870912 | bytes 20987904 | tf_op jit(solution)/shard_map/nsp,kns->kp/dot_general | solution.py:40
  285.0 13.6 %all-reduce = f32[32,128]{1,0:T(8,128)S(1)} all-reduce(f32[32,128]{1,0:T(8,128)S(1)} %fusion.2), channel_id=4, replica_groups=mesh['blk'=4,'aux'=32] {'blk'}, use_global_device_ids=true, to_apply=%region_2.3.clone | all-reduce | flops 4096 | bytes 32768
  298.6 0.6 constant_dynamic-slice_fusion
  (11 shorter events, 0.0 us)
Async XLA Ops:
  6.5 19.2 %copy-start = (bf16[128,32]{0,1:T(8,128)(2,1)S(1)}, bf16[128,32]{0,1:T(8,128)(2,1)}, u32[]{:S(2)}) copy-start(bf16[128,32]{0,1:T(8,128)(2,1)} %param.9) | copy-start | bytes 24580
  20.0 5.7 %copy-start.2 = (bf16[128,512,128]{2,1,0:T(8,128)(2,1)}, bf16[128,512,128]{2,1,0:T(8,128)(2,1)S(1)}, u32[]{:S(2)}) copy-start(bf16[128,512,128]{2,1,0:T(8,128)(2,1)S(1)} %and_select_fusion) | copy-start | bytes 50331652
  39.7 10.1 %slice-start = ((bf16[2,512,128]{2,1,0:T(8,128)(2,1)}), bf16[1,512,128]{2,1,0:T(8,128)(2,1)S(1)}, s32[]{:S(2)}) async-start(bf16[2,512,128]{2,1,0:T(8,128)(2,1)} %param.6), calls=%async_computation.4 | async-start | bytes 262144 | tf_op jit(solution)/shard_map/slice | solution.py:32
  39.7 137.9 %all-to-all-start = ((f32[32,128,512]{2,1,0:T(8,128)}), f32[32,128,512]{2,1,0:T(8,128)}, u32[]{:S(2)}, u32[]{:S(2)}) async-start(f32[32,128,512]{2,1,0:T(8,128)} %bitcast.25), calls=%async_computation | async-start | bytes 16777216 | tf_op jit(solution)/shard_map/all_to_all | solution.py:30
  49.8 132.5 %copy-start.3 = (bf16[2,512,128]{2,1,0:T(8,128)(2,1)S(1)}, bf16[2,512,128]{2,1,0:T(8,128)(2,1)}, u32[]{:S(2)}) copy-start(bf16[2,512,128]{2,1,0:T(8,128)(2,1)} %param.6) | copy-start | bytes 786436
  49.8 164.5 %reduce-scatter.2.cloned.1.call-start = ((), (), s32[]{:S(2)}) async-start(), calls=%async_computation.3 | async-start | bytes 1310720 | tf_op jit(solution)/shard_map/reduce_scatter | solution.py:36
  181.9 42.9 %copy-start.4 = (u32[128]{0:T(128)S(1)}, u32[128]{0:T(128)}, u32[]{:S(2)}) copy-start(u32[128]{0:T(128)} %constant.20) | copy-start | bytes 1540
  217.7 56.8 %all-to-all-start.1 = ((bf16[32,128,512]{2,1,0:T(8,128)(2,1)}), bf16[32,128,512]{2,1,0:T(8,128)(2,1)}, u32[]{:S(2)}, u32[]{:S(2)}) async-start(bf16[32,128,512]{2,1,0:T(8,128)(2,1)} %broadcast_in_dim.26), calls=%async_computation.2 | async-start | bytes 8388608 | tf_op jit(solution)/shard_map/all_to_all | solution.py:39
  225.4 73.8 %copy-start.1 = (bf16[128,32]{0,1:T(8,128)(2,1)S(1)}, bf16[128,32]{0,1:T(8,128)(2,1)}, u32[]{:S(2)}) copy-start(bf16[128,32]{0,1:T(8,128)(2,1)} %param.9) | copy-start | bytes 24580
Sparse Core Ops, SparseCore 0:
  184.1 30.1 reduce-scatter.1

commit v3 on v2

--- a/solution.py
+++ b/solution.py
@@ -27,20 +27,25 @@
     weighted = jnp.einsum(
         "rsp,pk->krs", screened, trial_vectors, preferred_element_type=jnp.float32
     )
-    weighted = lax.all_to_all(weighted, "aux", split_axis=0, concat_axis=0, tiled=True)
-    weighted = jnp.sum(weighted, axis=0)
+    weighted = lax.all_to_all(
+        weighted.astype(jnp.bfloat16), "aux", split_axis=0, concat_axis=0, tiled=True
+    )
+    weighted = jnp.sum(weighted.astype(jnp.float32), axis=0)
     virtual = lax.all_gather(greens[1], "blk", axis=1, tiled=True).astype(jnp.float32)
     occupied_cols = greens[0].astype(jnp.float32)
     projected = jnp.dot(weighted, virtual, precision=HI)
     z_part = jnp.einsum("ln,sl->ns", projected, occupied_cols, precision=HI)
-    z_rows = lax.psum_scatter(z_part, "blk", scatter_dimension=0, tiled=True)
+    group_count = lax.axis_size("blk")
+    z_part = z_part.reshape((group_count, -1) + z_part.shape[1:])
+    z_rows = jnp.sum(lax.all_to_all(z_part, "blk", split_axis=0, concat_axis=0, tiled=True), axis=0)
     aux_count = lax.axis_size("aux")
     z_copies = jnp.broadcast_to(z_rows.astype(jnp.bfloat16)[None], (aux_count,) + z_rows.shape)
     z_all = lax.all_to_all(z_copies, "aux", split_axis=0, concat_axis=0, tiled=True)
     terms = jnp.einsum(
         "nsp,kns->kp", screened, z_all, preferred_element_type=jnp.float32
     )
-    return lax.psum_scatter(terms, "blk", scatter_dimension=0, tiled=True)
+    terms = terms.reshape((group_count, -1) + terms.shape[1:])
+    return jnp.sum(lax.all_to_all(terms, "blk", split_axis=0, concat_axis=0, tiled=True), axis=0)
 
 
 def solution(mesh):

time: 312 us -> 188 us (0.60); the launches traced: 306 us -> 187 us
  waiting for transfers between devices: 78.7 us -> 0.01 us
  between operations: 14.2 us -> 0.11 us
  local copies, waits for them, and re-layouts: 17.5 us -> 5.02 us
  starting transfers between devices: 17.2 us -> 10.1 us
    all_to_all x0 -> x3, blocking collectives: none -> 81.7 us  [the longest x1 53.9 us: per_device(): lax.all_to_all(z_copies, 'aux', split_axis=0, concat_axis=0, tiled=True)]
    all_gather x1, blocking collectives: 128 us -> 57.5 us  [per_device(): lax.all_gather(greens[1], 'blk', axis=1, tiled=True).astype(jnp.float32)]
    all_to_all x2 -> x1, waiting for transfers between devices: 48.4 us -> 0.01 us  [per_device(): lax.all_to_all(weighted.astype(jnp.bfloat16), 'aux', split_axis=0, concat...]
    reduce_scatter x1 -> x0, waiting for transfers between devices: 30.3 us -> none  [per_device(): z_rows = lax.psum_scatter(z_part, 'blk', scatter_dimension=0, tiled=True)]
    unnamed x1 -> x0, blocking collectives: 13.6 us -> none
    dot_general x1, local copies, waits for them, and re-layouts: 8.09 us -> 0.12 us  [per_device(): z_part = jnp.einsum('ln,sl->ns', projected, occupied_cols, precision=HI)]
    all_to_all x2 -> x1, starting transfers between devices: 17.2 us -> 10.1 us  [per_device(): lax.all_to_all(weighted.astype(jnp.bfloat16), 'aux', split_axis=0, concat...]
    unnamed x12 -> x6, local copies, waits for them, and re-layouts: 6.92 us -> 0.01 us
  transfers between devices with their start and end apart: 3 -> 1, of which waited for: 2 -> 0; matrix products, arithmetic and copies ran while one was open for 0% -> 0% of each run, Pallas kernels for 0% -> 0%
where the time goes in v3:
time: 188 us; the launch traced here: 187 us
  blocking collectives  139 us (74%)
  other arithmetic  16.7 us (9%)
  matrix products  16.2 us (9%)
  starting transfers between devices  10.1 us (5%)
  local copies, waits for them, and re-layouts  5.02 us (3%)
    all_gather x1, blocking collectives, per_device(): lax.all_gather(greens[1], 'blk', axis=1, tiled=True).astype(jnp.float32)  57.5 us
    all_to_all x1, blocking collectives, per_device(): lax.all_to_all(z_copies, 'aux', split_axis=0, concat_axis=0, tiled=True)  53.9 us
    all_to_all x1, blocking collectives, per_device(): lax.all_to_all(z_part, 'blk', split_axis=0, concat_axis=0, tiled=True)  17.5 us
    select_n x1, other arithmetic, per_device(): screened = jnp.where(keep_mask, tensor, jnp.zeros_like(tensor))  11.8 us
    all_to_all x1, blocking collectives, per_device(): lax.all_to_all(terms, 'blk', split_axis=0, concat_axis=0, tiled=True)  10.3 us
    all_to_all x1, starting transfers between devices, per_device(): lax.all_to_all(weighted.astype(jnp.bfloat16), 'aux', split_axis=0, concat...  10.1 us
    dot_general x1, matrix products, per_device(): jnp.einsum('nsp,kns->kp', screened, z_all, preferred_element_type=jnp.flo...  9.4 us
    dot_general x1, matrix products, per_device(): jnp.einsum('rsp,pk->krs', screened, trial_vectors, preferred_element_type...  5.85 us
  transfers between devices with their start and end apart: 1, of which 0 were waited for; matrix products, arithmetic and copies ran while one was open for 0% of the time, Pallas kernels for 0%

profile of v3, /device:TPU:1, one launch (start us, length us, event | category | flops | bytes accessed | tf_op | source)
XLA Modules:
  0.0 187.3 jit_solution(17248623093976729242)
XLA Ops:
  0.0 0.0 copy-start
  0.0 0.7 compare_bitcast_fusion
  0.7 0.7 fusion.10
  1.4 0.1 dynamic_slice.3
  1.5 11.8 %and_select_fusion = bf16[128,512,128]{2,1,0:T(8,128)(2,1)S(1)} fusion(bf16[128,512,128]{2,1,0:T(8,128)(2,1)} %param.5, pred[512]{0:T(512)(128)(4,1)S(1)} %get-tuple-element.5, pred[128]{0:T(512)(128)(4,1)S(1)} %dynamic_slice.3, pred[512]{0:T(512)(128)(4,1)S(1)} %get-tuple-element.6), kind=kLoop, calls=%fused_computation | loop fusion | flops 25165824 | bytes 33555584 | tf_op jit(solution)/shard_map/jit(_where)/select_n | solution.py:25
  13.3 5.8 %convert_bitcast_fusion = bf16[32,128,512]{2,0,1:T(8,128)(2,1)S(1)} fusion(bf16[128,512,128]{2,1,0:T(8,128)(2,1)S(1)} %and_select_fusion, bf16[128,32]{0,1:T(8,128)(2,1)S(1)} %copy-done), kind=kOutput, calls=%fused_computation.4 | convolution fusion | flops 538968064 | bytes 20979712 | tf_op jit(solution)/shard_map/rsp,pk->krs/dot_general | solution.py:27
  19.2 0.0 copy-done.1
  19.2 0.0 slice-start
  19.2 4.3 %copy.7 = bf16[32,128,512]{2,1,0:T(8,128)(2,1)} copy(bf16[32,128,512]{2,0,1:T(8,128)(2,1)S(1)} %convert_bitcast_fusion) | data formatting | bytes 8388608 | tf_op jit(solution)/shard_map/convert_element_type | solution.py:31
  23.6 10.1 %all-to-all-start = ((bf16[32,128,512]{2,1,0:T(8,128)(2,1)}), bf16[32,128,512]{2,1,0:T(8,128)(2,1)}, u32[]{:S(2)}, u32[]{:S(2)}) async-start(bf16[32,128,512]{2,1,0:T(8,128)(2,1)} %copy.7), calls=%async_computation | async-start | bytes 8388608 | tf_op jit(solution)/shard_map/all_to_all | solution.py:30
  33.6 0.0 slice-done
  33.6 57.5 %all-gather = bf16[1,512,512]{2,1,0:T(8,128)(2,1)S(1)} all-gather(bf16[1,512,128]{2,1,0:T(8,128)(2,1)S(1)} %slice-done), channel_id=2, replica_groups=mesh['blk'=4,'aux'=32] {'blk'}, dimensions={2}, use_global_device_ids=true | all-gather | bytes 655360 | tf_op jit(solution)/shard_map/all_gather | solution.py:34
  91.1 0.0 all-to-all-done
  91.1 2.8 %convert_reduce_fusion = f32[128,512]{1,0:T(8,128)S(1)} fusion(bf16[32,128,512]{2,1,0:T(8,128)(2,1)} %all-to-all-done), kind=kLoop, calls=%fused_computation.1 | loop fusion | flops 4128768 | bytes 4456448 | tf_op jit(solution)/shard_map/reduce_sum | solution.py:33
  93.9 0.4 convolution_bitcast_fusion
  94.3 0.1 copy.10
  94.4 0.6 fusion.6
  95.0 17.5 %all_to_all.20 = f32[4,128,512]{2,1,0:T(8,128)S(1)} all-to-all(f32[4,128,512]{2,1,0:T(8,128)S(1)} %fusion.6), channel_id=1, replica_groups=mesh['blk'=4,'aux'=32] {'blk'}, dimensions={0} | all-to-all | bytes 2097152 | tf_op jit(solution)/shard_map/all_to_all | solution.py:40
  112.5 0.1 reduce_sum.28
  112.6 0.5 broadcast_in_dim.26
  113.1 53.9 %all_to_all.21 = bf16[32,128,512]{2,1,0:T(8,128)(2,1)S(1)} all-to-all(bf16[32,128,512]{2,1,0:T(8,128)(2,1)S(1)} %broadcast_in_dim.26), channel_id=1, replica_groups=mesh['blk'=4,'aux'=32] {'aux'}, dimensions={0} | all-to-all | bytes 8388608 | tf_op jit(solution)/shard_map/all_to_all | solution.py:43
  167.0 9.4 %fusion.2 = f32[4,8,128]{2,1,0:T(8,128)S(1)} fusion(bf16[128,512,128]{2,1,0:T(8,128)(2,1)} %copy-done.1, bf16[32,128,512]{2,1,0:T(8,128)(2,1)S(1)} %all_to_all.21), kind=kOutput, calls=%fused_computation.6 | convolution fusion | flops 536870912 | bytes 20987904 | tf_op jit(solution)/shard_map/nsp,kns->kp/dot_general | solution.py:44
  176.4 10.3 %all_to_all.22 = f32[4,8,128]{2,1,0:T(8,128)S(1)} all-to-all(f32[4,8,128]{2,1,0:T(8,128)S(1)} %fusion.2), channel_id=1, replica_groups=mesh['blk'=4,'aux'=32] {'blk'}, dimensions={0} | all-to-all | bytes 32768 | tf_op jit(solution)/shard_map/all_to_all | solution.py:48
  186.7 0.6 reduce_sum.29
  (4 shorter events, 0.0 us)
Async XLA Ops:
  0.0 13.3 %copy-start = (bf16[128,32]{0,1:T(8,128)(2,1)S(1)}, bf16[128,32]{0,1:T(8,128)(2,1)}, u32[]{:S(2)}) copy-start(bf16[128,32]{0,1:T(8,128)(2,1)} %param.9) | copy-start | bytes 24580
  13.3 5.9 %copy-start.1 = (bf16[128,512,128]{2,1,0:T(8,128)(2,1)}, bf16[128,512,128]{2,1,0:T(8,128)(2,1)S(1)}, u32[]{:S(2)}) copy-start(bf16[128,512,128]{2,1,0:T(8,128)(2,1)S(1)} %and_select_fusion) | copy-start | bytes 50331652
  19.2 14.4 %slice-start = ((bf16[2,512,128]{2,1,0:T(8,128)(2,1)}), bf16[1,512,128]{2,1,0:T(8,128)(2,1)S(1)}, s32[]{:S(2)}) async-start(bf16[2,512,128]{2,1,0:T(8,128)(2,1)} %param.6), calls=%async_computation.4 | async-start | bytes 262144 | tf_op jit(solution)/shard_map/slice | solution.py:34
  23.6 70.9 %copy-start.2 = (bf16[2,512,128]{2,1,0:T(8,128)(2,1)S(1)}, bf16[2,512,128]{2,1,0:T(8,128)(2,1)}, u32[]{:S(2)}) copy-start(bf16[2,512,128]{2,1,0:T(8,128)(2,1)} %param.6) | copy-start | bytes 786436
  23.6 67.5 %all-to-all-start = ((bf16[32,128,512]{2,1,0:T(8,128)(2,1)}), bf16[32,128,512]{2,1,0:T(8,128)(2,1)}, u32[]{:S(2)}, u32[]{:S(2)}) async-start(bf16[32,128,512]{2,1,0:T(8,128)(2,1)} %copy.7), calls=%async_computation | async-start | bytes 8388608 | tf_op jit(solution)/shard_map/all_to_all | solution.py:30

commit v4 on v3

v4 whole, which is shorter than its diff:
```python
import jax
import jax.numpy as jnp
from jax import lax
from jax.sharding import PartitionSpec as P

BS = 128
HI = lax.Precision.HIGHEST


def per_device(tensor, greens, pattern, block_sizes, trial_vectors):
    shard_rows = tensor.shape[0]
    basis_count = tensor.shape[1]
    group_count = lax.axis_size("blk")
    aux_count = lax.axis_size("aux")
    block_count = block_sizes.shape[0]
    live_mask = (jnp.arange(BS)[None, :] < block_sizes[:, None]).reshape(basis_count)
    row_live = lax.dynamic_slice_in_dim(live_mask, lax.axis_index("blk") * shard_rows, shard_rows)
    col_keep = jnp.broadcast_to(pattern[0, :, 0][:, None] > 0, (block_count, BS)).reshape(basis_count)
    keep = row_live[:, None] & (col_keep & live_mask)[None, :]

    weighted = jnp.einsum(
        "rsp,pk->krs", tensor, trial_vectors, preferred_element_type=jnp.float32
    )
    weighted = jnp.where(keep[None], weighted, 0.0)
    weighted = lax.all_to_all(
        weighted.astype(jnp.bfloat16), "aux", split_axis=0, concat_axis=0, tiled=True
    )
    weighted = jnp.sum(weighted.astype(jnp.float32), axis=0)
    both = lax.all_gather(greens, "blk", axis=2, tiled=True).astype(jnp.float32)
    occupied = both[0]
    virtual = both[1]
    projected = jnp.dot(weighted, virtual, precision=HI)
    projected = projected.reshape(shard_rows, group_count, shard_rows).transpose(1, 0, 2)
    projected = lax.all_to_all(projected, "blk", split_axis=0, concat_axis=0, tiled=True)
    projected = projected.reshape(group_count * shard_rows, shard_rows)
    z_rows = jnp.einsum("ln,sl->ns", projected, occupied, precision=HI)
    z_copies = jnp.broadcast_to(z_rows.astype(jnp.bfloat16)[None], (aux_count,) + z_rows.shape)
    z_all = lax.all_to_all(z_copies, "aux", split_axis=0, concat_axis=0, tiled=True)
    z_all = jnp.where(keep[None], z_all, jnp.zeros_like(z_all))
    terms = jnp.einsum(
        "nsp,kns->kp", tensor, z_all, preferred_element_type=jnp.float32
    )
    terms = terms.reshape((group_count, -1) + terms.shape[1:])
    return jnp.sum(lax.all_to_all(terms, "blk", split_axis=0, concat_axis=0, tiled=True), axis=0)


def solution(mesh):
    placed = (
        P("blk", None, "aux"),
        P(None, None, "blk"),
        P("blk", None, "aux"),
        P(),
        P("aux", None),
    )
    return jax.shard_map(
        per_device, mesh=mesh, in_specs=placed, out_specs=P("blk", "aux"), check_vma=False
    )
```

time: 188 us -> 193 us (1.027)
  blocking collectives: 139 us -> 79.8 us
  waiting for transfers between devices: 0.01 us -> 51.4 us
  between operations: 0.11 us -> 13.5 us
  matrix products: 16.2 us -> 24.4 us
  other arithmetic: 16.7 us -> 12 us
  local copies, waits for them, and re-layouts: 5.02 us -> 1.92 us
    all_gather x1 -> x0, blocking collectives: 57.5 us -> none  [per_device(): lax.all_gather(greens[1], 'blk', axis=1, tiled=True).astype(jnp.float32)]
    all_gather x0 -> x1, waiting for transfers between devices: none -> 30.1 us  [per_device(): both = lax.all_gather(greens, 'blk', axis=2, tiled=True).astype(jnp.float32)]
    all_to_all x1, waiting for transfers between devices: 0.01 us -> 20.6 us  [per_device(): lax.all_to_all(weighted.astype(jnp.bfloat16), 'aux', split_axis=0, concat...]
    select_n x1, other arithmetic: 11.8 us -> 0.3 us  [per_device(): z_all = jnp.where(keep[None], z_all, jnp.zeros_like(z_all))]
    dot_general x3, matrix products: 15.8 us -> 23.7 us  [the longest x1 13.6 us: per_device(): jnp.einsum('rsp,pk->krs', tensor, trial_vectors, preferred_element_type=j...]
    convert_element_type x0 -> x1, other arithmetic: none -> 6.81 us  [per_device(): weighted.astype(jnp.bfloat16)]
    all_to_all x1, blocking collectives: 17.5 us -> 12.9 us  [per_device(): lax.all_to_all(projected, 'blk', split_axis=0, concat_axis=0, tiled=True)]
    convert_element_type x1 -> x0, local copies, waits for them, and re-layouts: 4.34 us -> none  [per_device(): weighted.astype(jnp.bfloat16)]
  transfers between devices with their start and end apart: 1 -> 2, of which waited for: 0 -> 2; matrix products, arithmetic and copies ran while one was open for 0% -> 1% of each run, Pallas kernels for 0% -> 0%
where the time goes in v4:
time: 193 us
  blocking collectives  79.8 us (41%)
  waiting for transfers between devices  51.4 us (27%)
  matrix products  24.4 us (13%)
  between operations  13.5 us (7%)
  other arithmetic  12 us (6%)
  starting transfers between devices  9.97 us (5%)
    all_to_all x1, blocking collectives, per_device(): lax.all_to_all(z_copies, 'aux', split_axis=0, concat_axis=0, tiled=True)  56.6 us
    all_gather x1, waiting for transfers between devices, per_device(): both = lax.all_gather(greens, 'blk', axis=2, tiled=True).astype(jnp.float32)  30.1 us
    all_to_all x1, waiting for transfers between devices, per_device(): lax.all_to_all(weighted.astype(jnp.bfloat16), 'aux', split_axis=0, concat...  20.6 us
    dot_general x1, matrix products, per_device(): jnp.einsum('rsp,pk->krs', tensor, trial_vectors, preferred_element_type=j...  13.6 us
    all_to_all x1, blocking collectives, per_device(): lax.all_to_all(projected, 'blk', split_axis=0, concat_axis=0, tiled=True)  12.9 us
    all_to_all x1, blocking collectives, per_device(): lax.all_to_all(terms, 'blk', split_axis=0, concat_axis=0, tiled=True)  10.3 us
    all_to_all x1, starting transfers between devices, per_device(): lax.all_to_all(weighted.astype(jnp.bfloat16), 'aux', split_axis=0, concat...  9.93 us
    dot_general x1, matrix products, per_device(): jnp.einsum('nsp,kns->kp', tensor, z_all, preferred_element_type=jnp.float32)  9.4 us
  transfers between devices with their start and end apart: 2, of which 2 were waited for; matrix products, arithmetic and copies ran while one was open for 1% of the time, Pallas kernels for 0%

profile of v4, /device:TPU:1, one launch (start us, length us, event | category | flops | bytes accessed | tf_op | source)
XLA Modules:
  0.0 192.9 jit_solution(13444749834055533799)
XLA Ops:
  6.5 0.0 copy-start
  6.5 0.7 compare_bitcast_fusion
  7.2 0.7 bitcast_and_fusion
  7.9 0.1 dynamic_slice.3
  8.0 0.1 broadcast_and_fusion
  8.1 13.6 %fusion.7 = bf16[32,128,512]{2,0,1:T(8,128)(2,1)} fusion(bf16[128,512,128]{2,1,0:T(8,128)(2,1)} %param.5, bf16[128,32]{0,1:T(8,128)(2,1)S(1)} %copy-done), kind=kOutput, calls=%fused_computation.13 | convolution fusion | flops 536870912 | bytes 20979712 | tf_op jit(solution)/shard_map/rsp,pk->krs/dot_general | solution.py:21
  21.7 6.8 %fusion = bf16[32,128,512]{2,1,0:T(8,128)(2,1)} fusion(bf16[32,128,512]{2,0,1:T(8,128)(2,1)} %fusion.7, pred[128,512]{1,0:T(8,128)(4,1)S(1)} %broadcast_and_fusion), kind=kLoop, calls=%fused_computation.1 | loop fusion | flops 2097152 | bytes 8454144 | tf_op jit(solution)/shard_map/convert_element_type | solution.py:26
  28.5 9.9 %all-to-all-start = ((bf16[32,128,512]{2,1,0:T(8,128)(2,1)}), bf16[32,128,512]{2,1,0:T(8,128)(2,1)}, u32[]{:S(2)}, u32[]{:S(2)}) async-start(bf16[32,128,512]{2,1,0:T(8,128)(2,1)} %fusion), calls=%async_computation | async-start | bytes 8388608 | tf_op jit(solution)/shard_map/all_to_all | solution.py:25
  38.5 0.0 all-gather.2.cloned.1.call-start
  38.5 0.7 all-gather.2.cloned.1.call-update
  39.2 30.1 %all-gather.2.cloned.1.call-done = bf16[2,512,512]{2,1,0:T(8,128)(2,1)} async-done(((bf16[2,512,128]{2,1,0:T(8,128)(2,1)}), bf16[2,512,512]{2,1,0:T(8,128)(2,1)}) %all-gather.2.cloned.1.call-update) | async-done | bytes 1048592 | tf_op jit(solution)/shard_map/all_gather | solution.py:29
  69.3 1.2 slice_bitcast_fusion.2
  70.5 0.2 copy.7
  70.7 20.6 %all-to-all-done = bf16[32,128,512]{2,1,0:T(8,128)(2,1)} async-done(((bf16[32,128,512]{2,1,0:T(8,128)(2,1)}), bf16[32,128,512]{2,1,0:T(8,128)(2,1)}, u32[]{:S(2)}, u32[]{:S(2)}) %all-to-all-start) | async-done | bytes 4194336 | tf_op jit(solution)/shard_map/all_to_all | solution.py:25
  91.3 2.8 %convert_reduce_fusion = f32[128,512]{1,0:T(8,128)S(1)} fusion(bf16[32,128,512]{2,1,0:T(8,128)(2,1)} %all-to-all-done), kind=kLoop, calls=%fused_computation.2 | loop fusion | flops 4128768 | bytes 4456448 | tf_op jit(solution)/shard_map/reduce_sum | solution.py:28
  94.1 0.6 convolution_bitcast_fusion
  94.8 12.9 %all_to_all.20 = f32[4,128,128]{2,1,0:T(8,128)S(1)} all-to-all(f32[4,128,128]{2,1,0:T(8,128)S(1)} %convolution_bitcast_fusion), channel_id=1, replica_groups=mesh['blk'=4,'aux'=32] {'blk'}, dimensions={0} | all-to-all | bytes 524288 | tf_op jit(solution)/shard_map/all_to_all | solution.py:34
  107.7 0.7 convolution_convert_fusion
  108.5 0.5 broadcast_in_dim.24
  108.9 56.6 %all_to_all.21 = bf16[32,128,512]{2,1,0:T(8,128)(2,1)S(1)} all-to-all(bf16[32,128,512]{2,1,0:T(8,128)(2,1)S(1)} %broadcast_in_dim.24), channel_id=1, replica_groups=mesh['blk'=4,'aux'=32] {'aux'}, dimensions={0} | all-to-all | bytes 8388608 | tf_op jit(solution)/shard_map/all_to_all | solution.py:38
  165.5 0.3 broadcast_select_fusion
  165.8 9.4 %fusion.3 = f32[4,8,128]{2,1,0:T(8,128)S(1)} fusion(bf16[128,512,128]{2,1,0:T(8,128)(2,1)} %param.5, bf16[32,128,512]{2,1,0:T(8,128)(2,1)S(1)} %broadcast_select_fusion), kind=kOutput, calls=%fused_computation.8 | convolution fusion | flops 536870912 | bytes 20987904 | tf_op jit(solution)/shard_map/nsp,kns->kp/dot_general | solution.py:40
  175.2 10.3 %all_to_all.22 = f32[4,8,128]{2,1,0:T(8,128)S(1)} all-to-all(f32[4,8,128]{2,1,0:T(8,128)S(1)} %fusion.3), channel_id=1, replica_groups=mesh['blk'=4,'aux'=32] {'blk'}, dimensions={0} | all-to-all | bytes 32768 | tf_op jit(solution)/shard_map/all_to_all | solution.py:44
  185.5 0.6 reduce_sum.19
  (3 shorter events, 0.0 us)
Async XLA Ops:
  6.5 1.6 copy-start
  28.5 62.8 %all-to-all-start = ((bf16[32,128,512]{2,1,0:T(8,128)(2,1)}), bf16[32,128,512]{2,1,0:T(8,128)(2,1)}, u32[]{:S(2)}, u32[]{:S(2)}) async-start(bf16[32,128,512]{2,1,0:T(8,128)(2,1)} %fusion), calls=%async_computation | async-start | bytes 8388608 | tf_op jit(solution)/shard_map/all_to_all | solution.py:25
  38.5 30.8 %all-gather.2.cloned.1.call-start = ((), (), s32[]{:S(2)}) async-start(), calls=%async_computation.4 | async-start | bytes 1310720 | tf_op jit(solution)/shard_map/all_gather | solution.py:29
  69.3 38.4 %copy-start.1 = (bf16[2,512,512]{2,1,0:T(8,128)(2,1)S(1)}, bf16[2,512,512]{2,1,0:T(8,128)(2,1)}, u32[]{:S(2)}) copy-start(bf16[2,512,512]{2,1,0:T(8,128)(2,1)} %all-gather.2.cloned.1.call-done) | copy-start | bytes 3145732
Sparse Core Ops, SparseCore 0:
  40.9 28.3 all-gather.1

commit v5 on v4

--- a/solution.py
+++ b/solution.py
@@ -5,6 +5,7 @@
 
 BS = 128
 HI = lax.Precision.HIGHEST
+W_CHUNKS = 2
 
 
 def per_device(tensor, greens, pattern, block_sizes, trial_vectors):
@@ -18,15 +19,22 @@
     col_keep = jnp.broadcast_to(pattern[0, :, 0][:, None] > 0, (block_count, BS)).reshape(basis_count)
     keep = row_live[:, None] & (col_keep & live_mask)[None, :]
 
-    weighted = jnp.einsum(
-        "rsp,pk->krs", tensor, trial_vectors, preferred_element_type=jnp.float32
-    )
-    weighted = jnp.where(keep[None], weighted, 0.0)
-    weighted = lax.all_to_all(
-        weighted.astype(jnp.bfloat16), "aux", split_axis=0, concat_axis=0, tiled=True
-    )
-    weighted = jnp.sum(weighted.astype(jnp.float32), axis=0)
-    both = lax.all_gather(greens, "blk", axis=2, tiled=True).astype(jnp.float32)
+    chunk_rows = shard_rows // W_CHUNKS
+    pieces = []
+    for c in range(W_CHUNKS):
+        rows = slice(c * chunk_rows, (c + 1) * chunk_rows)
+        part = jnp.einsum(
+            "rsp,pk->krs", tensor[rows], trial_vectors, preferred_element_type=jnp.float32
+        )
+        part = jnp.where(keep[None, rows], part, 0.0)
+        part = lax.all_to_all(
+            part.astype(jnp.bfloat16), "aux", split_axis=0, concat_axis=0, tiled=True
+        )
+        pieces.append(jnp.sum(part.astype(jnp.float32), axis=0))
+    weighted = jnp.concatenate(pieces, axis=0)
+    green_copies = jnp.broadcast_to(greens[None], (group_count,) + greens.shape)
+    both = lax.all_to_all(green_copies, "blk", split_axis=0, concat_axis=0, tiled=True)
+    both = jnp.concatenate(list(both), axis=2).astype(jnp.float32)
     occupied = both[0]
     virtual = both[1]
     projected = jnp.dot(weighted, virtual, precision=HI)

time: 193 us -> 181 us (0.938)
  between operations: 13.5 us -> 0.11 us
  starting transfers between devices: 9.97 us -> 21.5 us
  other arithmetic: 12 us -> 4.65 us
  local copies, waits for them, and re-layouts: 1.92 us -> 8.6 us
  waiting for transfers between devices: 51.4 us -> 44.9 us
  blocking collectives: 79.8 us -> 76.3 us
    all_gather x1 -> x0, waiting for transfers between devices: 30.1 us -> none  [per_device(): both = lax.all_gather(greens, 'blk', axis=2, tiled=True).astype(jnp.float32)]
    all_to_all x1 -> x3, waiting for transfers between devices: 20.6 us -> 44.9 us  [the longest x2 40.3 us: per_device(): lax.all_to_all(part.astype(jnp.bfloat16), 'aux', split_axis=0, concat_axi...]
    all_to_all x1 -> x3, starting transfers between devices: 9.93 us -> 21.5 us  [the longest x2 15.7 us: per_device(): lax.all_to_all(part.astype(jnp.bfloat16), 'aux', split_axis=0, concat_axi...]
    convert_element_type x1 -> x0, other arithmetic: 6.81 us -> none  [per_device(): weighted.astype(jnp.bfloat16)]
    convert_element_type x0 -> x2, local copies, waits for them, and re-layouts: none -> 4.98 us  [per_device(): part.astype(jnp.bfloat16)]
    all_to_all x1, blocking collectives: 56.6 us -> 52 us  [per_device(): lax.all_to_all(z_copies, 'aux', split_axis=0, concat_axis=0, tiled=True)]
    dot_general x1 -> x2, matrix products: 13.6 us -> 12.7 us  [per_device(): jnp.einsum('rsp,pk->krs', tensor[rows], trial_vectors, preferred_element_...]
  transfers between devices with their start and end apart: 2 -> 3, of which waited for: 2 -> 3; matrix products, arithmetic and copies ran while one was open for 1% -> 11% of each run, Pallas kernels for 0% -> 0%
where the time goes in v5:
time: 181 us; the launch traced here: 180 us
  blocking collectives  76.3 us (42%)
  waiting for transfers between devices  44.9 us (25%)
  matrix products  24.3 us (13%)
  starting transfers between devices  21.5 us (12%)
  local copies, waits for them, and re-layouts  8.6 us (5%)
  other arithmetic  4.65 us (3%)
    all_to_all x1, blocking collectives, per_device(): lax.all_to_all(z_copies, 'aux', split_axis=0, concat_axis=0, tiled=True)  52 us
    all_to_all x2, waiting for transfers between devices, per_device(): lax.all_to_all(part.astype(jnp.bfloat16), 'aux', split_axis=0, concat_axi...  40.3 us
    all_to_all x2, starting transfers between devices, per_device(): lax.all_to_all(part.astype(jnp.bfloat16), 'aux', split_axis=0, concat_axi...  15.7 us
    all_to_all x1, blocking collectives, per_device(): lax.all_to_all(projected, 'blk', split_axis=0, concat_axis=0, tiled=True)  14 us
    dot_general x2, matrix products, per_device(): jnp.einsum('rsp,pk->krs', tensor[rows], trial_vectors, preferred_element_...  12.7 us
    all_to_all x1, blocking collectives, per_device(): lax.all_to_all(terms, 'blk', split_axis=0, concat_axis=0, tiled=True)  10.3 us
    dot_general x1, matrix products, per_device(): jnp.einsum('nsp,kns->kp', tensor, z_all, preferred_element_type=jnp.float32)  9.4 us
    all_to_all x1, starting transfers between devices, per_device(): lax.all_to_all(green_copies, 'blk', split_axis=0, concat_axis=0, tiled=True)  5.78 us
  transfers between devices with their start and end apart: 3, of which 3 were waited for; matrix products, arithmetic and copies ran while one was open for 11% of the time, Pallas kernels for 0%

profile of v5, /device:TPU:1, one launch (start us, length us, event | category | flops | bytes accessed | tf_op | source)
XLA Modules:
  0.0 180.2 jit_solution(16410419662515489630)
XLA Ops:
  0.0 1.1 copy.15
  1.1 1.1 broadcast_in_dim.58
  2.2 5.8 %all-to-all-start.2 = ((bf16[4,2,512,128]{2,3,1,0:T(8,128)(2,1)}), bf16[4,2,512,128]{2,3,1,0:T(8,128)(2,1)S(1)}, u32[]{:S(2)}, u32[]{:S(2)}) async-start(bf16[4,2,512,128]{2,3,1,0:T(8,128)(2,1)} %broadcast_in_dim.58), calls=%async_computation.2 | async-start | bytes 2097152 | tf_op jit(solution)/shard_map/all_to_all | solution.py:36
  8.0 0.7 compare_bitcast_fusion
  8.6 0.7 bitcast_and_fusion
  9.6 6.4 %select_convert_fusion.1 = bf16[32,64,512]{2,0,1:T(8,128)(2,1)S(1)} fusion(pred[64,512]{1,0:T(8,128)(4,1)S(1)} %get-tuple-element.11, bf16[128,512,128]{2,1,0:T(8,128)(2,1)} %param.5, bf16[128,32]{0,1:T(8,128)(2,1)S(1)} %copy-done), kind=kOutput, calls=%fused_computation.9 | convolution fusion | flops 270532608 | bytes 10526720 | tf_op jit(solution)/shard_map/rsp,pk->krs/dot_general | solution.py:26
  15.9 2.5 %copy.13 = bf16[32,64,512]{2,1,0:T(8,128)(2,1)} copy(bf16[32,64,512]{2,0,1:T(8,128)(2,1)S(1)} %select_convert_fusion.1) | data formatting | bytes 4194304 | tf_op jit(solution)/shard_map/convert_element_type | solution.py:31
  18.4 4.5 %all-to-all-done.2 = bf16[4,2,512,128]{2,3,1,0:T(8,128)(2,1)S(1)} async-done(((bf16[4,2,512,128]{2,3,1,0:T(8,128)(2,1)}), bf16[4,2,512,128]{2,3,1,0:T(8,128)(2,1)S(1)}, u32[]{:S(2)}, u32[]{:S(2)}) %all-to-all-start.2) | async-done | bytes 1048608 | tf_op jit(solution)/shard_map/all_to_all | solution.py:36
  22.9 8.2 %all-to-all-start = ((bf16[32,64,512]{2,1,0:T(8,128)(2,1)}), bf16[32,64,512]{2,1,0:T(8,128)(2,1)S(1)}, u32[]{:S(2)}, u32[]{:S(2)}) async-start(bf16[32,64,512]{2,1,0:T(8,128)(2,1)} %copy.13), calls=%async_computation | async-start | bytes 4194304 | tf_op jit(solution)/shard_map/all_to_all | solution.py:30
  31.1 6.4 %select_convert_fusion = bf16[32,64,512]{2,0,1:T(8,128)(2,1)S(1)} fusion(pred[64,512]{1,0:T(8,128)(4,1)S(1)} %get-tuple-element.12, bf16[128,512,128]{2,1,0:T(8,128)(2,1)} %param.5, bf16[128,32]{0,1:T(8,128)(2,1)S(1)} %copy-done), kind=kOutput, calls=%fused_computation.7 | convolution fusion | flops 270532608 | bytes 10526720 | tf_op jit(solution)/shard_map/rsp,pk->krs/dot_general | solution.py:26
  37.5 2.5 %copy.14 = bf16[32,64,512]{2,1,0:T(8,128)(2,1)} copy(bf16[32,64,512]{2,0,1:T(8,128)(2,1)S(1)} %select_convert_fusion) | data formatting | bytes 4194304 | tf_op jit(solution)/shard_map/convert_element_type | solution.py:31
  40.0 16.5 %all-to-all-done = bf16[32,64,512]{2,1,0:T(8,128)(2,1)S(1)} async-done(((bf16[32,64,512]{2,1,0:T(8,128)(2,1)}), bf16[32,64,512]{2,1,0:T(8,128)(2,1)S(1)}, u32[]{:S(2)}, u32[]{:S(2)}) %all-to-all-start) | async-done | bytes 2097184 | tf_op jit(solution)/shard_map/all_to_all | solution.py:30
  56.5 7.5 %all-to-all-start.1 = ((bf16[32,64,512]{2,1,0:T(8,128)(2,1)}), bf16[32,64,512]{2,1,0:T(8,128)(2,1)}, u32[]{:S(2)}, u32[]{:S(2)}) async-start(bf16[32,64,512]{2,1,0:T(8,128)(2,1)} %copy.14), calls=%async_computation.1 | async-start | bytes 4194304 | tf_op jit(solution)/shard_map/all_to_all | solution.py:30
  64.2 0.8 slice.26
  65.3 23.8 %all-to-all-done.1 = bf16[32,64,512]{2,1,0:T(8,128)(2,1)} async-done(((bf16[32,64,512]{2,1,0:T(8,128)(2,1)}), bf16[32,64,512]{2,1,0:T(8,128)(2,1)}, u32[]{:S(2)}, u32[]{:S(2)}) %all-to-all-start.1) | async-done | bytes 2097184 | tf_op jit(solution)/shard_map/all_to_all | solution.py:30
  89.1 1.9 %convert_reduce_fusion = f32[64,512]{1,0:T(8,128)S(1)} fusion(bf16[32,64,512]{2,1,0:T(8,128)(2,1)} %all-to-all-done.1), kind=kLoop, calls=%fused_computation.6 | loop fusion | flops 2064384 | bytes 2228224 | tf_op jit(solution)/shard_map/reduce_sum | solution.py:33
  91.0 1.7 convolution_bitcast_fusion
  92.7 14.0 %all_to_all.30 = f32[4,128,128]{2,1,0:T(8,128)S(1)} all-to-all(f32[4,128,128]{2,1,0:T(8,128)S(1)} %convolution_bitcast_fusion), channel_id=1, replica_groups=mesh['blk'=4,'aux'=32] {'blk'}, dimensions={0} | all-to-all | bytes 524288 | tf_op jit(solution)/shard_map/all_to_all | solution.py:42
  106.7 0.5 convolution_convert_fusion
  107.2 0.5 broadcast_in_dim.59
  107.7 52.0 %all_to_all.31 = bf16[32,128,512]{2,1,0:T(8,128)(2,1)S(1)} all-to-all(bf16[32,128,512]{2,1,0:T(8,128)(2,1)S(1)} %broadcast_in_dim.59), channel_id=1, replica_groups=mesh['blk'=4,'aux'=32] {'aux'}, dimensions={0} | all-to-all | bytes 8388608 | tf_op jit(solution)/shard_map/all_to_all | solution.py:46
  159.9 9.4 %fusion.10 = f32[4,8,128]{2,1,0:T(8,128)S(1)} fusion(bf16[128,512,128]{2,1,0:T(8,128)(2,1)} %param.5, bf16[32,128,512]{2,1,0:T(8,128)(2,1)S(1)} %broadcast_select_fusion), kind=kOutput, calls=%fused_computation.13 | convolution fusion | flops 536870912 | bytes 20987904 | tf_op jit(solution)/shard_map/nsp,kns->kp/dot_general | solution.py:48
  169.4 10.3 %all_to_all.32 = f32[4,8,128]{2,1,0:T(8,128)S(1)} all-to-all(f32[4,8,128]{2,1,0:T(8,128)S(1)} %fusion.10), channel_id=1, replica_groups=mesh['blk'=4,'aux'=32] {'blk'}, dimensions={0} | all-to-all | bytes 32768 | tf_op jit(solution)/shard_map/all_to_all | solution.py:52
  179.6 0.6 reduce_sum.29
  (9 shorter events, 0.9 us)
Async XLA Ops:
  0.0 9.5 %copy-start = (bf16[128,32]{0,1:T(8,128)(2,1)S(1)}, bf16[128,32]{0,1:T(8,128)(2,1)}, u32[]{:S(2)}) copy-start(bf16[128,32]{0,1:T(8,128)(2,1)} %param.9) | copy-start | bytes 24580
  2.2 20.8 %all-to-all-start.2 = ((bf16[4,2,512,128]{2,3,1,0:T(8,128)(2,1)}), bf16[4,2,512,128]{2,3,1,0:T(8,128)(2,1)S(1)}, u32[]{:S(2)}, u32[]{:S(2)}) async-start(bf16[4,2,512,128]{2,3,1,0:T(8,128)(2,1)} %broadcast_in_dim.58), calls=%async_computation.2 | async-start | bytes 2097152 | tf_op jit(solution)/shard_map/all_to_all | solution.py:36
  22.9 33.6 %all-to-all-start = ((bf16[32,64,512]{2,1,0:T(8,128)(2,1)}), bf16[32,64,512]{2,1,0:T(8,128)(2,1)S(1)}, u32[]{:S(2)}, u32[]{:S(2)}) async-start(bf16[32,64,512]{2,1,0:T(8,128)(2,1)} %copy.13), calls=%async_computation | async-start | bytes 4194304 | tf_op jit(solution)/shard_map/all_to_all | solution.py:30
  56.5 32.6 %all-to-all-start.1 = ((bf16[32,64,512]{2,1,0:T(8,128)(2,1)}), bf16[32,64,512]{2,1,0:T(8,128)(2,1)}, u32[]{:S(2)}, u32[]{:S(2)}) async-start(bf16[32,64,512]{2,1,0:T(8,128)(2,1)} %copy.14), calls=%async_computation.1 | async-start | bytes 4194304 | tf_op jit(solution)/shard_map/all_to_all | solution.py:30

commit v6 on v5

--- a/solution.py
+++ b/solution.py
@@ -32,8 +32,11 @@
         )
         pieces.append(jnp.sum(part.astype(jnp.float32), axis=0))
     weighted = jnp.concatenate(pieces, axis=0)
-    green_copies = jnp.broadcast_to(greens[None], (group_count,) + greens.shape)
-    both = lax.all_to_all(green_copies, "blk", split_axis=0, concat_axis=0, tiled=True)
+    shifted = [greens] + [
+        lax.ppermute(greens, "blk", [(i, (i - s) % group_count) for i in range(group_count)])
+        for s in range(1, group_count)
+    ]
+    both = jnp.roll(jnp.stack(shifted), lax.axis_index("blk"), axis=0)
     both = jnp.concatenate(list(both), axis=2).astype(jnp.float32)
     occupied = both[0]
     virtual = both[1]

time: 181 us -> 180 us (level)
  waiting for transfers between devices: 44.9 us -> 33.2 us
  local copies, waits for them, and re-layouts: 8.6 us -> 17.1 us
  starting transfers between devices: 21.5 us -> 23.9 us
    all_to_all x2, waiting for transfers between devices: 40.3 us -> 18.9 us  [per_device(): lax.all_to_all(part.astype(jnp.bfloat16), 'aux', split_axis=0, concat_axi...]
    ppermute x0 -> x3, waiting for transfers between devices: none -> 14.3 us  [per_device(): lax.ppermute(greens, 'blk', [(i, (i - s) % group_count) for i in range(gr...]
    all_to_all x1 -> x0, starting transfers between devices: 5.78 us -> none  [per_device(): lax.all_to_all(green_copies, 'blk', split_axis=0, concat_axis=0, tiled=True)]
    ppermute x0 -> x3, starting transfers between devices: none -> 5.77 us  [per_device(): lax.ppermute(greens, 'blk', [(i, (i - s) % group_count) for i in range(gr...]
    all_to_all x1 -> x0, waiting for transfers between devices: 4.54 us -> none  [per_device(): lax.all_to_all(green_copies, 'blk', split_axis=0, concat_axis=0, tiled=True)]
    unnamed x3 -> x13, local copies, waits for them, and re-layouts: 1.1 us -> 5.11 us
    all_to_all x1, blocking collectives: 14 us -> 10.4 us  [per_device(): lax.all_to_all(projected, 'blk', split_axis=0, concat_axis=0, tiled=True)]
    dot_general x0 -> x2, local copies, waits for them, and re-layouts: none -> 2.92 us  [per_device(): projected = jnp.dot(weighted, virtual, precision=HI)]
  transfers between devices with their start and end apart: 3 -> 5, of which waited for: 3 -> 2; matrix products, arithmetic and copies ran while one was open for 11% -> 12% of each run, Pallas kernels for 0% -> 0%
where the time goes in v6:
time: 180 us; the launch traced here: 179 us
  blocking collectives  75 us (42%)
  waiting for transfers between devices  33.2 us (18%)
  matrix products  24.8 us (14%)
  starting transfers between devices  23.9 us (13%)
  local copies, waits for them, and re-layouts  17.1 us (10%)
  other arithmetic  4.71 us (3%)
    all_to_all x1, blocking collectives, per_device(): lax.all_to_all(z_copies, 'aux', split_axis=0, concat_axis=0, tiled=True)  54.3 us
    all_to_all x2, waiting for transfers between devices, per_device(): lax.all_to_all(part.astype(jnp.bfloat16), 'aux', split_axis=0, concat_axi...  18.9 us
    all_to_all x2, starting transfers between devices, per_device(): lax.all_to_all(part.astype(jnp.bfloat16), 'aux', split_axis=0, concat_axi...  18.1 us
    ppermute x3, waiting for transfers between devices, per_device(): lax.ppermute(greens, 'blk', [(i, (i - s) % group_count) for i in range(gr...  14.3 us
    dot_general x2, matrix products, per_device(): jnp.einsum('rsp,pk->krs', tensor[rows], trial_vectors, preferred_element_...  14.1 us
    all_to_all x1, blocking collectives, per_device(): lax.all_to_all(projected, 'blk', split_axis=0, concat_axis=0, tiled=True)  10.4 us
    all_to_all x1, blocking collectives, per_device(): lax.all_to_all(terms, 'blk', split_axis=0, concat_axis=0, tiled=True)  10.3 us
    dot_general x1, matrix products, per_device(): jnp.einsum('nsp,kns->kp', tensor, z_all, preferred_element_type=jnp.float32)  9.4 us
  transfers between devices with their start and end apart: 5, of which 2 were waited for; matrix products, arithmetic and copies ran while one was open for 12% of the time, Pallas kernels for 0%

profile of v6, /device:TPU:1, one launch (start us, length us, event | category | flops | bytes accessed | tf_op | source)
XLA Modules:
  0.0 178.8 jit_solution(8700074161092782401)
XLA Ops:
  0.7 0.7 bitcast_and_fusion
  1.6 6.4 %select_convert_fusion.1 = bf16[32,64,512]{2,0,1:T(8,128)(2,1)S(1)} fusion(pred[64,512]{1,0:T(8,128)(4,1)S(1)} %get-tuple-element.11, bf16[128,512,128]{2,1,0:T(8,128)(2,1)} %param.5, bf16[128,32]{0,1:T(8,128)(2,1)S(1)} %copy-done), kind=kOutput, calls=%fused_computation.9 | convolution fusion | flops 270532608 | bytes 10526720 | tf_op jit(solution)/shard_map/rsp,pk->krs/dot_general | solution.py:26
  8.0 2.5 %copy.13 = bf16[32,64,512]{2,1,0:T(8,128)(2,1)} copy(bf16[32,64,512]{2,0,1:T(8,128)(2,1)S(1)} %select_convert_fusion.1) | data formatting | bytes 4194304 | tf_op jit(solution)/shard_map/convert_element_type | solution.py:31
  10.5 9.9 %all-to-all-start = ((bf16[32,64,512]{2,1,0:T(8,128)(2,1)}), bf16[32,64,512]{2,1,0:T(8,128)(2,1)S(1)}, u32[]{:S(2)}, u32[]{:S(2)}) async-start(bf16[32,64,512]{2,1,0:T(8,128)(2,1)} %copy.13), calls=%async_computation | async-start | bytes 4194304 | tf_op jit(solution)/shard_map/all_to_all | solution.py:30
  20.4 1.0 collective-permute-start
  21.4 2.4 %collective-permute-start.2 = (bf16[2,512,128]{2,1,0:T(8,128)(2,1)S(1)}, bf16[2,512,128]{2,1,0:T(8,128)(2,1)S(1)}, u32[]{:S(2)}, u32[]{:S(2)}) collective-permute-start(bf16[2,512,128]{2,1,0:T(8,128)(2,1)S(1)} %copy-done.2), channel_id=1, source_target_pairs={{0,32},{32,64},{64,96},{96,0},{1,33},{33,65},{65,97},{97,1},{2,34}... | collective-permute-start | bytes 786440 | tf_op jit(solution)/shard_map/ppermute | solution.py:36
  23.8 2.3 %collective-permute-start.1 = (bf16[2,512,128]{2,1,0:T(8,128)(2,1)S(1)}, bf16[2,512,128]{2,1,0:T(8,128)(2,1)S(1)}, u32[]{:S(2)}, u32[]{:S(2)}) collective-permute-start(bf16[2,512,128]{2,1,0:T(8,128)(2,1)S(1)} %copy-done.2), channel_id=1, source_target_pairs={{0,64},{32,96},{64,0},{96,32},{1,65},{33,97},{65,1},{97,33},{2,66}... | collective-permute-start | bytes 786440 | tf_op jit(solution)/shard_map/ppermute | solution.py:36
  26.2 7.7 %select_convert_fusion = bf16[32,64,512]{2,0,1:T(8,128)(2,1)} fusion(pred[64,512]{1,0:T(8,128)(4,1)S(1)} %get-tuple-element.12, bf16[128,512,128]{2,1,0:T(8,128)(2,1)} %param.5, bf16[128,32]{0,1:T(8,128)(2,1)S(1)} %copy-done), kind=kOutput, calls=%fused_computation.7 | convolution fusion | flops 270532608 | bytes 10526720 | tf_op jit(solution)/shard_map/rsp,pk->krs/dot_general | solution.py:26
  34.6 4.1 %copy.14 = bf16[32,64,512]{2,1,0:T(8,128)(2,1)} copy(bf16[32,64,512]{2,0,1:T(8,128)(2,1)} %select_convert_fusion) | data formatting | bytes 4194304 | tf_op jit(solution)/shard_map/convert_element_type | solution.py:31
  38.7 14.3 %collective-permute-done = bf16[2,512,128]{2,1,0:T(8,128)(2,1)S(1)} collective-permute-done((bf16[2,512,128]{2,1,0:T(8,128)(2,1)S(1)}, bf16[2,512,128]{2,1,0:T(8,128)(2,1)S(1)}, u32[]{:S(2)}, u32[]{:S(2)}) %collective-permute-start) | collective-permute-done | bytes 262176 | tf_op jit(solution)/shard_map/ppermute | solution.py:36
  53.0 0.7 bitcast_dynamic-update-slice_fusion.4
  53.7 8.2 %all-to-all-start.1 = ((bf16[32,64,512]{2,1,0:T(8,128)(2,1)}), bf16[32,64,512]{2,1,0:T(8,128)(2,1)}, u32[]{:S(2)}, u32[]{:S(2)}) async-start(bf16[32,64,512]{2,1,0:T(8,128)(2,1)} %copy.14), calls=%async_computation.1 | async-start | bytes 4194304 | tf_op jit(solution)/shard_map/all_to_all | solution.py:30
  61.9 0.7 bitcast_dynamic-update-slice_fusion.2
  62.7 0.7 bitcast_dynamic-update-slice_fusion
  65.6 0.7 bitcast_dynamic-update-slice_fusion.1
  66.3 1.3 dynamic-slice_bitcast_fusion.3
  67.7 0.8 slice_bitcast_fusion.2
  68.5 2.1 %copy.15 = bf16[512,512]{1,0:T(8,128)(2,1)} copy(bf16[512,512]{0,1:T(8,128)(2,1)} %slice_bitcast_fusion.2) | data formatting | bytes 1048576 | tf_op jit(solution)/shard_map/dot_general | solution.py:43
  70.9 18.9 %all-to-all-done.1 = bf16[32,64,512]{2,1,0:T(8,128)(2,1)} async-done(((bf16[32,64,512]{2,1,0:T(8,128)(2,1)}), bf16[32,64,512]{2,1,0:T(8,128)(2,1)}, u32[]{:S(2)}, u32[]{:S(2)}) %all-to-all-start.1) | async-done | bytes 2097184 | tf_op jit(solution)/shard_map/all_to_all | solution.py:30
  89.8 1.9 %convert_reduce_fusion = f32[64,512]{1,0:T(8,128)S(1)} fusion(bf16[32,64,512]{2,1,0:T(8,128)(2,1)} %all-to-all-done.1), kind=kLoop, calls=%fused_computation.6 | loop fusion | flops 2064384 | bytes 2228224 | tf_op jit(solution)/shard_map/reduce_sum | solution.py:33
  92.3 10.4 %all_to_all.25 = f32[4,128,128]{2,1,0:T(8,128)S(1)} all-to-all(f32[4,128,128]{2,1,0:T(8,128)S(1)} %convolution_bitcast_fusion), channel_id=1, replica_groups=mesh['blk'=4,'aux'=32] {'blk'}, dimensions={0} | all-to-all | bytes 524288 | tf_op jit(solution)/shard_map/all_to_all | solution.py:45
  103.9 54.3 %all_to_all.26 = bf16[32,128,512]{2,1,0:T(8,128)(2,1)S(1)} all-to-all(bf16[32,128,512]{2,1,0:T(8,128)(2,1)S(1)} %broadcast_in_dim.52), channel_id=1, replica_groups=mesh['blk'=4,'aux'=32] {'aux'}, dimensions={0} | all-to-all | bytes 8388608 | tf_op jit(solution)/shard_map/all_to_all | solution.py:49
  158.5 9.4 %fusion.10 = f32[4,8,128]{2,1,0:T(8,128)S(1)} fusion(bf16[128,512,128]{2,1,0:T(8,128)(2,1)} %param.5, bf16[32,128,512]{2,1,0:T(8,128)(2,1)S(1)} %broadcast_select_fusion), kind=kOutput, calls=%fused_computation.13 | convolution fusion | flops 536870912 | bytes 20987904 | tf_op jit(solution)/shard_map/nsp,kns->kp/dot_general | solution.py:51
  168.0 10.3 %all_to_all.27 = f32[4,8,128]{2,1,0:T(8,128)S(1)} all-to-all(f32[4,8,128]{2,1,0:T(8,128)S(1)} %fusion.10), channel_id=1, replica_groups=mesh['blk'=4,'aux'=32] {'blk'}, dimensions={0} | all-to-all | bytes 32768 | tf_op jit(solution)/shard_map/all_to_all | solution.py:55
  (24 shorter events, 6.9 us)
Async XLA Ops:
  0.0 1.6 copy-start
  10.5 9.9 %copy-start.2 = (bf16[2,512,128]{2,1,0:T(8,128)(2,1)S(1)}, bf16[2,512,128]{2,1,0:T(8,128)(2,1)}, u32[]{:S(2)}) copy-start(bf16[2,512,128]{2,1,0:T(8,128)(2,1)} %param.6) | copy-start | bytes 786436
  10.5 43.3 %all-to-all-start = ((bf16[32,64,512]{2,1,0:T(8,128)(2,1)}), bf16[32,64,512]{2,1,0:T(8,128)(2,1)S(1)}, u32[]{:S(2)}, u32[]{:S(2)}) async-start(bf16[32,64,512]{2,1,0:T(8,128)(2,1)} %copy.13), calls=%async_computation | async-start | bytes 4194304 | tf_op jit(solution)/shard_map/all_to_all | solution.py:30
  20.4 32.6 %collective-permute-start = (bf16[2,512,128]{2,1,0:T(8,128)(2,1)S(1)}, bf16[2,512,128]{2,1,0:T(8,128)(2,1)S(1)}, u32[]{:S(2)}, u32[]{:S(2)}) collective-permute-start(bf16[2,512,128]{2,1,0:T(8,128)(2,1)S(1)} %copy-done.2), channel_id=1, source_target_pairs={{0,96},{32,0},{64,32},{96,64},{1,97},{33,1},{65,33},{97,65},{2,98}... | collective-permute-start | bytes 786440 | tf_op jit(solution)/shard_map/ppermute | solution.py:36
  21.4 41.2 %collective-permute-start.2 = (bf16[2,512,128]{2,1,0:T(8,128)(2,1)S(1)}, bf16[2,512,128]{2,1,0:T(8,128)(2,1)S(1)}, u32[]{:S(2)}, u32[]{:S(2)}) collective-permute-start(bf16[2,512,128]{2,1,0:T(8,128)(2,1)S(1)} %copy-done.2), channel_id=1, source_target_pairs={{0,32},{32,64},{64,96},{96,0},{1,33},{33,65},{65,97},{97,1},{2,34}... | collective-permute-start | bytes 786440 | tf_op jit(solution)/shard_map/ppermute | solution.py:36
  23.8 38.1 %collective-permute-start.1 = (bf16[2,512,128]{2,1,0:T(8,128)(2,1)S(1)}, bf16[2,512,128]{2,1,0:T(8,128)(2,1)S(1)}, u32[]{:S(2)}, u32[]{:S(2)}) collective-permute-start(bf16[2,512,128]{2,1,0:T(8,128)(2,1)S(1)} %copy-done.2), channel_id=1, source_target_pairs={{0,64},{32,96},{64,0},{96,32},{1,65},{33,97},{65,1},{97,33},{2,66}... | collective-permute-start | bytes 786440 | tf_op jit(solution)/shard_map/ppermute | solution.py:36
  53.7 36.0 %all-to-all-start.1 = ((bf16[32,64,512]{2,1,0:T(8,128)(2,1)}), bf16[32,64,512]{2,1,0:T(8,128)(2,1)}, u32[]{:S(2)}, u32[]{:S(2)}) async-start(bf16[32,64,512]{2,1,0:T(8,128)(2,1)} %copy.14), calls=%async_computation.1 | async-start | bytes 4194304 | tf_op jit(solution)/shard_map/all_to_all | solution.py:30
  70.9 20.8 %copy-start.1 = (bf16[512,512]{1,0:T(8,128)(2,1)S(1)}, bf16[512,512]{1,0:T(8,128)(2,1)}, u32[]{:S(2)}) copy-start(bf16[512,512]{1,0:T(8,128)(2,1)} %copy.15) | copy-start | bytes 1572868

commit v7 on v6

--- a/solution.py
+++ b/solution.py
@@ -42,7 +42,7 @@
     virtual = both[1]
     projected = jnp.dot(weighted, virtual, precision=HI)
     projected = projected.reshape(shard_rows, group_count, shard_rows).transpose(1, 0, 2)
-    projected = lax.all_to_all(projected, "blk", split_axis=0, concat_axis=0, tiled=True)
+    projected = _blk_exchange(projected, group_count)
     projected = projected.reshape(group_count * shard_rows, shard_rows)
     z_rows = jnp.einsum("ln,sl->ns", projected, occupied, precision=HI)
     z_copies = jnp.broadcast_to(z_rows.astype(jnp.bfloat16)[None], (aux_count,) + z_rows.shape)
@@ -52,7 +52,19 @@
         "nsp,kns->kp", tensor, z_all, preferred_element_type=jnp.float32
     )
     terms = terms.reshape((group_count, -1) + terms.shape[1:])
-    return jnp.sum(lax.all_to_all(terms, "blk", split_axis=0, concat_axis=0, tiled=True), axis=0)
+    return jnp.sum(_blk_exchange(terms, group_count), axis=0)
+
+
+def _blk_exchange(blocks, group_count):
+    me = lax.axis_index("blk")
+    got = [jnp.take(blocks, me, axis=0)]
+    for s in range(1, group_count):
+        sent = jnp.take(blocks, (me + s) % group_count, axis=0)
+        got.append(
+            lax.ppermute(sent, "blk", [(i, (i + s) % group_count) for i in range(group_count)])
+        )
+    ahead = jnp.stack([got[0]] + got[:0:-1])
+    return jnp.roll(ahead, me, axis=0)
 
 
 def solution(mesh):

time: 180 us -> 177 us (0.983)
  blocking collectives: 75 us -> 54.7 us
  starting transfers between devices: 23.9 us -> 36.6 us
  waiting for transfers between devices: 33.2 us -> 38.3 us
    all_to_all x2 -> x0, blocking collectives: 20.7 us -> none  [the longest x1 10.4 us: per_device(): lax.all_to_all(projected, 'blk', split_axis=0, concat_axis=0, tiled=True)]
    ppermute x0 -> x6, starting transfers between devices: none -> 12.7 us  [_blk_exchange(): lax.ppermute(sent, 'blk', [(i, (i + s) % group_count) for i in range(grou...]
    ppermute x0 -> x6, waiting for transfers between devices: none -> 5.08 us  [_blk_exchange(): lax.ppermute(sent, 'blk', [(i, (i + s) % group_count) for i in range(grou...]
    unnamed x13 -> x23, local copies, waits for them, and re-layouts: 5.11 us -> 5.15 us
  transfers between devices with their start and end apart: 5 -> 11, of which waited for: 2 -> 4; matrix products, arithmetic and copies ran while one was open for 12% -> 13% of each run, Pallas kernels for 0% -> 0%
where the time goes in v7:
time: 177 us
  blocking collectives  54.7 us (31%)
  waiting for transfers between devices  38.3 us (22%)
  starting transfers between devices  36.6 us (21%)
  matrix products  24.8 us (14%)
  local copies, waits for them, and re-layouts  17.2 us (10%)
  other arithmetic  4.79 us (3%)
    all_to_all x1, blocking collectives, per_device(): lax.all_to_all(z_copies, 'aux', split_axis=0, concat_axis=0, tiled=True)  54.7 us
    all_to_all x2, waiting for transfers between devices, per_device(): lax.all_to_all(part.astype(jnp.bfloat16), 'aux', split_axis=0, concat_axi...  18.9 us
    all_to_all x2, starting transfers between devices, per_device(): lax.all_to_all(part.astype(jnp.bfloat16), 'aux', split_axis=0, concat_axi...  18.1 us
    ppermute x3, waiting for transfers between devices, per_device(): lax.ppermute(greens, 'blk', [(i, (i - s) % group_count) for i in range(gr...  14.3 us
    dot_general x2, matrix products, per_device(): jnp.einsum('rsp,pk->krs', tensor[rows], trial_vectors, preferred_element_...  14.1 us
    ppermute x6, starting transfers between devices, _blk_exchange(): lax.ppermute(sent, 'blk', [(i, (i + s) % group_count) for i in range(grou...  12.7 us
    dot_general x1, matrix products, per_device(): jnp.einsum('nsp,kns->kp', tensor, z_all, preferred_element_type=jnp.float32)  9.4 us
    convert_element_type x2, local copies, waits for them, and re-layouts, per_device(): part.astype(jnp.bfloat16)  6.57 us
  transfers between devices with their start and end apart: 11, of which 4 were waited for; matrix products, arithmetic and copies ran while one was open for 13% of the time, Pallas kernels for 0%

profile of v7, /device:TPU:1, one launch (start us, length us, event | category | flops | bytes accessed | tf_op | source)
XLA Modules:
  0.0 176.6 jit_solution(13812802279848972442)
XLA Ops:
  1.6 6.4 %select_convert_fusion.1 = bf16[32,64,512]{2,0,1:T(8,128)(2,1)S(1)} fusion(pred[64,512]{1,0:T(8,128)(4,1)S(1)} %get-tuple-element.39, bf16[128,512,128]{2,1,0:T(8,128)(2,1)} %param.9, bf16[128,32]{0,1:T(8,128)(2,1)S(1)} %copy-done), kind=kOutput, calls=%fused_computation.9 | convolution fusion | flops 270532608 | bytes 10526720 | tf_op jit(solution)/shard_map/rsp,pk->krs/dot_general | solution.py:26
  8.0 2.5 %copy.13 = bf16[32,64,512]{2,1,0:T(8,128)(2,1)} copy(bf16[32,64,512]{2,0,1:T(8,128)(2,1)S(1)} %select_convert_fusion.1) | data formatting | bytes 4194304 | tf_op jit(solution)/shard_map/convert_element_type | solution.py:31
  10.5 9.9 %all-to-all-start = ((bf16[32,64,512]{2,1,0:T(8,128)(2,1)}), bf16[32,64,512]{2,1,0:T(8,128)(2,1)S(1)}, u32[]{:S(2)}, u32[]{:S(2)}) async-start(bf16[32,64,512]{2,1,0:T(8,128)(2,1)} %copy.13), calls=%async_computation | async-start | bytes 4194304 | tf_op jit(solution)/shard_map/all_to_all | solution.py:30
  20.4 1.0 collective-permute-start
  21.4 2.4 %collective-permute-start.2 = (bf16[2,512,128]{2,1,0:T(8,128)(2,1)S(1)}, bf16[2,512,128]{2,1,0:T(8,128)(2,1)S(1)}, u32[]{:S(2)}, u32[]{:S(2)}) collective-permute-start(bf16[2,512,128]{2,1,0:T(8,128)(2,1)S(1)} %copy-done.2), channel_id=1, source_target_pairs={{0,32},{32,64},{64,96},{96,0},{1,33},{33,65},{65,97},{97,1},{2,34}... | collective-permute-start | bytes 786440 | tf_op jit(solution)/shard_map/ppermute | solution.py:36
  23.9 2.3 %collective-permute-start.1 = (bf16[2,512,128]{2,1,0:T(8,128)(2,1)S(1)}, bf16[2,512,128]{2,1,0:T(8,128)(2,1)S(1)}, u32[]{:S(2)}, u32[]{:S(2)}) collective-permute-start(bf16[2,512,128]{2,1,0:T(8,128)(2,1)S(1)} %copy-done.2), channel_id=1, source_target_pairs={{0,64},{32,96},{64,0},{96,32},{1,65},{33,97},{65,1},{97,33},{2,66}... | collective-permute-start | bytes 786440 | tf_op jit(solution)/shard_map/ppermute | solution.py:36
  26.2 7.7 %select_convert_fusion = bf16[32,64,512]{2,0,1:T(8,128)(2,1)} fusion(pred[64,512]{1,0:T(8,128)(4,1)S(1)} %get-tuple-element.40, bf16[128,512,128]{2,1,0:T(8,128)(2,1)} %param.9, bf16[128,32]{0,1:T(8,128)(2,1)S(1)} %copy-done), kind=kOutput, calls=%fused_computation.7 | convolution fusion | flops 270532608 | bytes 10526720 | tf_op jit(solution)/shard_map/rsp,pk->krs/dot_general | solution.py:26
  34.6 4.1 %copy.14 = bf16[32,64,512]{2,1,0:T(8,128)(2,1)} copy(bf16[32,64,512]{2,0,1:T(8,128)(2,1)} %select_convert_fusion) | data formatting | bytes 4194304 | tf_op jit(solution)/shard_map/convert_element_type | solution.py:31
  38.7 14.3 %collective-permute-done = bf16[2,512,128]{2,1,0:T(8,128)(2,1)S(1)} collective-permute-done((bf16[2,512,128]{2,1,0:T(8,128)(2,1)S(1)}, bf16[2,512,128]{2,1,0:T(8,128)(2,1)S(1)}, u32[]{:S(2)}, u32[]{:S(2)}) %collective-permute-start) | collective-permute-done | bytes 262176 | tf_op jit(solution)/shard_map/ppermute | solution.py:36
  53.7 8.2 %all-to-all-start.1 = ((bf16[32,64,512]{2,1,0:T(8,128)(2,1)}), bf16[32,64,512]{2,1,0:T(8,128)(2,1)}, u32[]{:S(2)}, u32[]{:S(2)}) async-start(bf16[32,64,512]{2,1,0:T(8,128)(2,1)} %copy.14), calls=%async_computation.1 | async-start | bytes 4194304 | tf_op jit(solution)/shard_map/all_to_all | solution.py:30
  66.3 1.3 dynamic-slice_bitcast_fusion.3
  67.7 0.8 slice_bitcast_fusion.2
  68.5 2.0 %copy.15 = bf16[512,512]{1,0:T(8,128)(2,1)} copy(bf16[512,512]{0,1:T(8,128)(2,1)} %slice_bitcast_fusion.2) | data formatting | bytes 1048576 | tf_op jit(solution)/shard_map/dot_general | solution.py:43
  70.9 18.9 %all-to-all-done.1 = bf16[32,64,512]{2,1,0:T(8,128)(2,1)} async-done(((bf16[32,64,512]{2,1,0:T(8,128)(2,1)}), bf16[32,64,512]{2,1,0:T(8,128)(2,1)}, u32[]{:S(2)}, u32[]{:S(2)}) %all-to-all-start.1) | async-done | bytes 2097184 | tf_op jit(solution)/shard_map/all_to_all | solution.py:30
  89.8 1.9 %convert_reduce_fusion = f32[64,512]{1,0:T(8,128)S(1)} fusion(bf16[32,64,512]{2,1,0:T(8,128)(2,1)} %all-to-all-done.1), kind=kLoop, calls=%fused_computation.6 | loop fusion | flops 2064384 | bytes 2228224 | tf_op jit(solution)/shard_map/reduce_sum | solution.py:33
  92.5 3.2 %collective-permute-start.5 = (f32[128,128]{1,0:T(8,128)S(1)}, f32[128,128]{1,0:T(8,128)S(1)}, u32[]{:S(2)}, u32[]{:S(2)}) collective-permute-start(f32[128,128]{1,0:T(8,128)S(1)} %get-tuple-element.35), channel_id=1, source_target_pairs={{0,32},{32,64},{64,96},{96,0},{1,33},{33,65},{65,97},{97,1},{2,34}... | collective-permute-start | bytes 196616 | tf_op jit(solution)/shard_map/ppermute | solution.py:64
  95.7 2.4 %collective-permute-start.4 = (f32[128,128]{1,0:T(8,128)S(1)}, f32[128,128]{1,0:T(8,128)S(1)}, u32[]{:S(2)}, u32[]{:S(2)}) collective-permute-start(f32[128,128]{1,0:T(8,128)S(1)} %get-tuple-element.37), channel_id=1, source_target_pairs={{0,64},{32,96},{64,0},{96,32},{1,65},{33,97},{65,1},{97,33},{2,66}... | collective-permute-start | bytes 196616 | tf_op jit(solution)/shard_map/ppermute | solution.py:64
  98.1 3.2 %collective-permute-done.4 = f32[128,128]{1,0:T(8,128)S(1)} collective-permute-done((f32[128,128]{1,0:T(8,128)S(1)}, f32[128,128]{1,0:T(8,128)S(1)}, u32[]{:S(2)}, u32[]{:S(2)}) %collective-permute-start.4) | collective-permute-done | bytes 65568 | tf_op jit(solution)/shard_map/ppermute | solution.py:64
  102.6 54.7 %all_to_all.15 = bf16[32,128,512]{2,1,0:T(8,128)(2,1)S(1)} all-to-all(bf16[32,128,512]{2,1,0:T(8,128)(2,1)S(1)} %broadcast_in_dim.70), channel_id=1, replica_groups=mesh['blk'=4,'aux'=32] {'aux'}, dimensions={0} | all-to-all | bytes 8388608 | tf_op jit(solution)/shard_map/all_to_all | solution.py:49
  157.6 9.4 %fusion.10 = f32[4,8,128]{2,1,0:T(8,128)S(1)} fusion(bf16[128,512,128]{2,1,0:T(8,128)(2,1)} %param.9, bf16[32,128,512]{2,1,0:T(8,128)(2,1)S(1)} %broadcast_select_fusion), kind=kOutput, calls=%fused_computation.13 | convolution fusion | flops 536870912 | bytes 20987904 | tf_op jit(solution)/shard_map/nsp,kns->kp/dot_general | solution.py:51
  167.1 2.1 %collective-permute-start.6 = (f32[8,128]{1,0:T(8,128)S(1)}, f32[8,128]{1,0:T(8,128)S(1)}, u32[]{:S(2)}, u32[]{:S(2)}) collective-permute-start(f32[8,128]{1,0:T(8,128)S(1)} %get-tuple-element.44), channel_id=1, source_target_pairs={{0,96},{32,0},{64,32},{96,64},{1,97},{33,1},{65,33},{97,65},{2,98}... | collective-permute-start | bytes 12296 | tf_op jit(solution)/shard_map/ppermute | solution.py:64
  169.1 2.6 %collective-permute-start.8 = (f32[8,128]{1,0:T(8,128)S(1)}, f32[8,128]{1,0:T(8,128)S(1)}, u32[]{:S(2)}, u32[]{:S(2)}) collective-permute-start(f32[8,128]{1,0:T(8,128)S(1)} %get-tuple-element.41), channel_id=1, source_target_pairs={{0,32},{32,64},{64,96},{96,0},{1,33},{33,65},{65,97},{97,1},{2,34}... | collective-permute-start | bytes 12296 | tf_op jit(solution)/shard_map/ppermute | solution.py:64
  171.8 2.3 %collective-permute-start.7 = (f32[8,128]{1,0:T(8,128)S(1)}, f32[8,128]{1,0:T(8,128)S(1)}, u32[]{:S(2)}, u32[]{:S(2)}) collective-permute-start(f32[8,128]{1,0:T(8,128)S(1)} %get-tuple-element.43), channel_id=1, source_target_pairs={{0,64},{32,96},{64,0},{96,32},{1,65},{33,97},{65,1},{97,33},{2,66}... | collective-permute-start | bytes 12296 | tf_op jit(solution)/shard_map/ppermute | solution.py:64
  174.1 1.9 %collective-permute-done.7 = f32[8,128]{1,0:T(8,128)S(1)} collective-permute-done((f32[8,128]{1,0:T(8,128)S(1)}, f32[8,128]{1,0:T(8,128)S(1)}, u32[]{:S(2)}, u32[]{:S(2)}) %collective-permute-start.7) | collective-permute-done | bytes 4128 | tf_op jit(solution)/shard_map/ppermute | solution.py:64
  (51 shorter events, 10.8 us)
Async XLA Ops:
  0.0 1.6 copy-start
  10.5 9.9 %copy-start.2 = (bf16[2,512,128]{2,1,0:T(8,128)(2,1)S(1)}, bf16[2,512,128]{2,1,0:T(8,128)(2,1)}, u32[]{:S(2)}) copy-start(bf16[2,512,128]{2,1,0:T(8,128)(2,1)} %param.10) | copy-start | bytes 786436
  10.5 43.3 %all-to-all-start = ((bf16[32,64,512]{2,1,0:T(8,128)(2,1)}), bf16[32,64,512]{2,1,0:T(8,128)(2,1)S(1)}, u32[]{:S(2)}, u32[]{:S(2)}) async-start(bf16[32,64,512]{2,1,0:T(8,128)(2,1)} %copy.13), calls=%async_computation | async-start | bytes 4194304 | tf_op jit(solution)/shard_map/all_to_all | solution.py:30
  20.4 32.6 %collective-permute-start = (bf16[2,512,128]{2,1,0:T(8,128)(2,1)S(1)}, bf16[2,512,128]{2,1,0:T(8,128)(2,1)S(1)}, u32[]{:S(2)}, u32[]{:S(2)}) collective-permute-start(bf16[2,512,128]{2,1,0:T(8,128)(2,1)S(1)} %copy-done.2), channel_id=1, source_target_pairs={{0,96},{32,0},{64,32},{96,64},{1,97},{33,1},{65,33},{97,65},{2,98}... | collective-permute-start | bytes 786440 | tf_op jit(solution)/shard_map/ppermute | solution.py:36
  21.4 41.2 %collective-permute-start.2 = (bf16[2,512,128]{2,1,0:T(8,128)(2,1)S(1)}, bf16[2,512,128]{2,1,0:T(8,128)(2,1)S(1)}, u32[]{:S(2)}, u32[]{:S(2)}) collective-permute-start(bf16[2,512,128]{2,1,0:T(8,128)(2,1)S(1)} %copy-done.2), channel_id=1, source_target_pairs={{0,32},{32,64},{64,96},{96,0},{1,33},{33,65},{65,97},{97,1},{2,34}... | collective-permute-start | bytes 786440 | tf_op jit(solution)/shard_map/ppermute | solution.py:36
  23.9 38.1 %collective-permute-start.1 = (bf16[2,512,128]{2,1,0:T(8,128)(2,1)S(1)}, bf16[2,512,128]{2,1,0:T(8,128)(2,1)S(1)}, u32[]{:S(2)}, u32[]{:S(2)}) collective-permute-start(bf16[2,512,128]{2,1,0:T(8,128)(2,1)S(1)} %copy-done.2), channel_id=1, source_target_pairs={{0,64},{32,96},{64,0},{96,32},{1,65},{33,97},{65,1},{97,33},{2,66}... | collective-permute-start | bytes 786440 | tf_op jit(solution)/shard_map/ppermute | solution.py:36
  53.7 36.1 %all-to-all-start.1 = ((bf16[32,64,512]{2,1,0:T(8,128)(2,1)}), bf16[32,64,512]{2,1,0:T(8,128)(2,1)}, u32[]{:S(2)}, u32[]{:S(2)}) async-start(bf16[32,64,512]{2,1,0:T(8,128)(2,1)} %copy.14), calls=%async_computation.1 | async-start | bytes 4194304 | tf_op jit(solution)/shard_map/all_to_all | solution.py:30
  70.9 20.8 %copy-start.1 = (bf16[512,512]{1,0:T(8,128)(2,1)S(1)}, bf16[512,512]{1,0:T(8,128)(2,1)}, u32[]{:S(2)}) copy-start(bf16[512,512]{1,0:T(8,128)(2,1)} %copy.15) | copy-start | bytes 1572868
  92.4 5.7 %collective-permute-start.3 = (f32[128,128]{1,0:T(8,128)S(1)}, f32[128,128]{1,0:T(8,128)S(1)}, u32[]{:S(2)}, u32[]{:S(2)}) collective-permute-start(f32[128,128]{1,0:T(8,128)S(1)} %get-tuple-element.38), channel_id=1, source_target_pairs={{0,96},{32,0},{64,32},{96,64},{1,97},{33,1},{65,33},{97,65},{2,98}... | collective-permute-start | bytes 196616 | tf_op jit(solution)/shard_map/ppermute | solution.py:64
  92.5 8.9 %collective-permute-start.5 = (f32[128,128]{1,0:T(8,128)S(1)}, f32[128,128]{1,0:T(8,128)S(1)}, u32[]{:S(2)}, u32[]{:S(2)}) collective-permute-start(f32[128,128]{1,0:T(8,128)S(1)} %get-tuple-element.35), channel_id=1, source_target_pairs={{0,32},{32,64},{64,96},{96,0},{1,33},{33,65},{65,97},{97,1},{2,34}... | collective-permute-start | bytes 196616 | tf_op jit(solution)/shard_map/ppermute | solution.py:64
  95.7 5.6 %collective-permute-start.4 = (f32[128,128]{1,0:T(8,128)S(1)}, f32[128,128]{1,0:T(8,128)S(1)}, u32[]{:S(2)}, u32[]{:S(2)}) collective-permute-start(f32[128,128]{1,0:T(8,128)S(1)} %get-tuple-element.37), channel_id=1, source_target_pairs={{0,64},{32,96},{64,0},{96,32},{1,65},{33,97},{65,1},{97,33},{2,66}... | collective-permute-start | bytes 196616 | tf_op jit(solution)/shard_map/ppermute | solution.py:64
  167.1 7.0 %collective-permute-start.6 = (f32[8,128]{1,0:T(8,128)S(1)}, f32[8,128]{1,0:T(8,128)S(1)}, u32[]{:S(2)}, u32[]{:S(2)}) collective-permute-start(f32[8,128]{1,0:T(8,128)S(1)} %get-tuple-element.44), channel_id=1, source_target_pairs={{0,96},{32,0},{64,32},{96,64},{1,97},{33,1},{65,33},{97,65},{2,98}... | collective-permute-start | bytes 12296 | tf_op jit(solution)/shard_map/ppermute | solution.py:64
  169.1 6.8 %collective-permute-start.8 = (f32[8,128]{1,0:T(8,128)S(1)}, f32[8,128]{1,0:T(8,128)S(1)}, u32[]{:S(2)}, u32[]{:S(2)}) collective-permute-start(f32[8,128]{1,0:T(8,128)S(1)} %get-tuple-element.41), channel_id=1, source_target_pairs={{0,32},{32,64},{64,96},{96,0},{1,33},{33,65},{65,97},{97,1},{2,34}... | collective-permute-start | bytes 12296 | tf_op jit(solution)/shard_map/ppermute | solution.py:64
  171.8 4.2 %collective-permute-start.7 = (f32[8,128]{1,0:T(8,128)S(1)}, f32[8,128]{1,0:T(8,128)S(1)}, u32[]{:S(2)}, u32[]{:S(2)}) collective-permute-start(f32[8,128]{1,0:T(8,128)S(1)} %get-tuple-element.43), channel_id=1, source_target_pairs={{0,64},{32,96},{64,0},{96,32},{1,65},{33,97},{65,1},{97,33},{2,66}... | collective-permute-start | bytes 12296 | tf_op jit(solution)/shard_map/ppermute | solution.py:64

commit v8 on v7

--- a/solution.py
+++ b/solution.py
@@ -5,7 +5,7 @@
 
 BS = 128
 HI = lax.Precision.HIGHEST
-W_CHUNKS = 2
+W_CHUNKS = 1
 
 
 def per_device(tensor, greens, pattern, block_sizes, trial_vectors):

time: 177 us -> 181 us (1.023)
  waiting for transfers between devices: 38.3 us -> 56.7 us
  local copies, waits for them, and re-layouts: 17.2 us -> 1.23 us
  other arithmetic: 4.79 us -> 12.2 us
  starting transfers between devices: 36.6 us -> 30.8 us
    ppermute x3, waiting for transfers between devices: 14.3 us -> 54.2 us  [per_device(): lax.ppermute(greens, 'blk', [(i, (i - s) % group_count) for i in range(gr...]
    all_to_all x2 -> x1, waiting for transfers between devices: 18.9 us -> 0.01 us  [per_device(): lax.all_to_all(part.astype(jnp.bfloat16), 'aux', split_axis=0, concat_axi...]
    all_to_all x2 -> x1, starting transfers between devices: 18.1 us -> 10.1 us  [per_device(): lax.all_to_all(part.astype(jnp.bfloat16), 'aux', split_axis=0, concat_axi...]
    convert_element_type x0 -> x1, other arithmetic: none -> 6.83 us  [per_device(): part.astype(jnp.bfloat16)]
    convert_element_type x2 -> x0, local copies, waits for them, and re-layouts: 6.57 us -> none  [per_device(): part.astype(jnp.bfloat16)]
    unnamed x23 -> x21, local copies, waits for them, and re-layouts: 5.15 us -> 0.28 us
    dot_general x2, local copies, waits for them, and re-layouts: 2.88 us -> 0.25 us  [per_device(): projected = jnp.dot(weighted, virtual, precision=HI)]
    ppermute x6, waiting for transfers between devices: 5.08 us -> 2.58 us  [_blk_exchange(): lax.ppermute(sent, 'blk', [(i, (i + s) % group_count) for i in range(grou...]
  transfers between devices with their start and end apart: 11 -> 10, of which waited for: 4 -> 4; matrix products, arithmetic and copies ran while one was open for 13% -> 0% of each run, Pallas kernels for 0% -> 0%
where the time goes in v8:
time: 181 us; the launch traced here: 179 us
  waiting for transfers between devices  56.7 us (31%)
  blocking collectives  53.6 us (30%)
  starting transfers between devices  30.8 us (17%)
  matrix products  24.3 us (13%)
  other arithmetic  12.2 us (7%)
    ppermute x3, waiting for transfers between devices, per_device(): lax.ppermute(greens, 'blk', [(i, (i - s) % group_count) for i in range(gr...  54.2 us
    all_to_all x1, blocking collectives, per_device(): lax.all_to_all(z_copies, 'aux', split_axis=0, concat_axis=0, tiled=True)  53.6 us
    ppermute x6, starting transfers between devices, _blk_exchange(): lax.ppermute(sent, 'blk', [(i, (i + s) % group_count) for i in range(grou...  14.7 us
    dot_general x1, matrix products, per_device(): jnp.einsum('rsp,pk->krs', tensor[rows], trial_vectors, preferred_element_...  13.6 us
    all_to_all x1, starting transfers between devices, per_device(): lax.all_to_all(part.astype(jnp.bfloat16), 'aux', split_axis=0, concat_axi...  10.1 us
    dot_general x1, matrix products, per_device(): jnp.einsum('nsp,kns->kp', tensor, z_all, preferred_element_type=jnp.float32)  9.4 us
    convert_element_type x1, other arithmetic, per_device(): part.astype(jnp.bfloat16)  6.83 us
    ppermute x3, starting transfers between devices, per_device(): lax.ppermute(greens, 'blk', [(i, (i - s) % group_count) for i in range(gr...  6.05 us
  transfers between devices with their start and end apart: 10, of which 4 were waited for; matrix products, arithmetic and copies ran while one was open for 0% of the time, Pallas kernels for 0%

profile of v8, /device:TPU:1, one launch (start us, length us, event | category | flops | bytes accessed | tf_op | source)
XLA Modules:
  0.0 179.3 jit_solution(9366524956978269693)
XLA Ops:
  0.0 0.7 compare_bitcast_fusion
  0.7 0.7 bitcast_and_fusion
  1.6 13.6 %fusion.9 = bf16[32,128,512]{2,0,1:T(8,128)(2,1)} fusion(bf16[128,512,128]{2,1,0:T(8,128)(2,1)} %param.9, bf16[128,32]{0,1:T(8,128)(2,1)S(1)} %copy-done), kind=kOutput, calls=%fused_computation.47 | convolution fusion | flops 536870912 | bytes 20979712 | tf_op jit(solution)/shard_map/rsp,pk->krs/dot_general | solution.py:26
  15.2 6.8 %fusion = bf16[32,128,512]{2,1,0:T(8,128)(2,1)} fusion(bf16[32,128,512]{2,0,1:T(8,128)(2,1)} %fusion.9, pred[128,512]{1,0:T(8,128)(4,1)S(1)} %broadcast_and_fusion), kind=kLoop, calls=%fused_computation.1 | loop fusion | flops 2097152 | bytes 8454144 | tf_op jit(solution)/shard_map/convert_element_type | solution.py:31
  22.0 10.1 %all-to-all-start = ((bf16[32,128,512]{2,1,0:T(8,128)(2,1)}), bf16[32,128,512]{2,1,0:T(8,128)(2,1)}, u32[]{:S(2)}, u32[]{:S(2)}) async-start(bf16[32,128,512]{2,1,0:T(8,128)(2,1)} %fusion), calls=%async_computation | async-start | bytes 8388608 | tf_op jit(solution)/shard_map/all_to_all | solution.py:30
  32.1 1.0 collective-permute-start
  33.1 2.5 %collective-permute-start.1 = (bf16[2,512,128]{2,1,0:T(8,128)(2,1)S(1)}, bf16[2,512,128]{2,1,0:T(8,128)(2,1)S(1)}, u32[]{:S(2)}, u32[]{:S(2)}) collective-permute-start(bf16[2,512,128]{2,1,0:T(8,128)(2,1)S(1)} %copy-done.1), channel_id=1, source_target_pairs={{0,64},{32,96},{64,0},{96,32},{1,65},{33,97},{65,1},{97,33},{2,66}... | collective-permute-start | bytes 786440 | tf_op jit(solution)/shard_map/ppermute | solution.py:36
  35.6 2.6 %collective-permute-start.2 = (bf16[2,512,128]{2,1,0:T(8,128)(2,1)S(1)}, bf16[2,512,128]{2,1,0:T(8,128)(2,1)S(1)}, u32[]{:S(2)}, u32[]{:S(2)}) collective-permute-start(bf16[2,512,128]{2,1,0:T(8,128)(2,1)S(1)} %copy-done.1), channel_id=1, source_target_pairs={{0,32},{32,64},{64,96},{96,0},{1,33},{33,65},{65,97},{97,1},{2,34}... | collective-permute-start | bytes 786440 | tf_op jit(solution)/shard_map/ppermute | solution.py:36
  38.3 54.1 %collective-permute-done = bf16[2,512,128]{2,1,0:T(8,128)(2,1)S(1)} collective-permute-done((bf16[2,512,128]{2,1,0:T(8,128)(2,1)S(1)}, bf16[2,512,128]{2,1,0:T(8,128)(2,1)S(1)}, u32[]{:S(2)}, u32[]{:S(2)}) %collective-permute-start) | collective-permute-done | bytes 262176 | tf_op jit(solution)/shard_map/ppermute | solution.py:36
  93.2 2.8 %convert_reduce_fusion = f32[128,512]{1,0:T(8,128)S(1)} fusion(bf16[32,128,512]{2,1,0:T(8,128)(2,1)} %all-to-all-done), kind=kLoop, calls=%fused_computation.2 | loop fusion | flops 4128768 | bytes 4456448 | tf_op jit(solution)/shard_map/reduce_sum | solution.py:33
  96.0 0.6 convolution_bitcast_fusion
  96.7 4.8 %collective-permute-start.3 = (f32[128,128]{1,0:T(8,128)S(1)}, f32[128,128]{1,0:T(8,128)S(1)}, u32[]{:S(2)}, u32[]{:S(2)}) collective-permute-start(f32[128,128]{1,0:T(8,128)S(1)} %get-tuple-element.38), channel_id=1, source_target_pairs={{0,96},{32,0},{64,32},{96,64},{1,97},{33,1},{65,33},{97,65},{2,98}... | collective-permute-start | bytes 196616 | tf_op jit(solution)/shard_map/ppermute | solution.py:64
  101.5 0.5 collective-permute-start.4
  102.1 2.7 %collective-permute-start.5 = (f32[128,128]{1,0:T(8,128)S(1)}, f32[128,128]{1,0:T(8,128)S(1)}, u32[]{:S(2)}, u32[]{:S(2)}) collective-permute-start(f32[128,128]{1,0:T(8,128)S(1)} %get-tuple-element.35), channel_id=1, source_target_pairs={{0,32},{32,64},{64,96},{96,0},{1,33},{33,65},{65,97},{97,1},{2,34}... | collective-permute-start | bytes 196616 | tf_op jit(solution)/shard_map/ppermute | solution.py:64
  104.8 1.8 %collective-permute-done.4 = f32[128,128]{1,0:T(8,128)S(1)} collective-permute-done((f32[128,128]{1,0:T(8,128)S(1)}, f32[128,128]{1,0:T(8,128)S(1)}, u32[]{:S(2)}, u32[]{:S(2)}) %collective-permute-start.4) | collective-permute-done | bytes 65568 | tf_op jit(solution)/shard_map/ppermute | solution.py:64
  106.7 0.7 convolution_convert_fusion
  107.4 0.5 broadcast_in_dim.59
  107.9 53.6 %all_to_all.10 = bf16[32,128,512]{2,1,0:T(8,128)(2,1)S(1)} all-to-all(bf16[32,128,512]{2,1,0:T(8,128)(2,1)S(1)} %broadcast_in_dim.59), channel_id=1, replica_groups=mesh['blk'=4,'aux'=32] {'aux'}, dimensions={0} | all-to-all | bytes 8388608 | tf_op jit(solution)/shard_map/all_to_all | solution.py:49
  161.9 9.4 %fusion.3 = f32[4,8,128]{2,1,0:T(8,128)S(1)} fusion(bf16[128,512,128]{2,1,0:T(8,128)(2,1)} %param.9, bf16[32,128,512]{2,1,0:T(8,128)(2,1)S(1)} %broadcast_select_fusion), kind=kOutput, calls=%fused_computation.8 | convolution fusion | flops 536870912 | bytes 20987904 | tf_op jit(solution)/shard_map/nsp,kns->kp/dot_general | solution.py:51
  171.3 3.4 %collective-permute-start.6 = (f32[8,128]{1,0:T(8,128)S(1)}, f32[8,128]{1,0:T(8,128)S(1)}, u32[]{:S(2)}, u32[]{:S(2)}) collective-permute-start(f32[8,128]{1,0:T(8,128)S(1)} %get-tuple-element.42), channel_id=1, source_target_pairs={{0,96},{32,0},{64,32},{96,64},{1,97},{33,1},{65,33},{97,65},{2,98}... | collective-permute-start | bytes 12296 | tf_op jit(solution)/shard_map/ppermute | solution.py:64
  174.7 1.1 collective-permute-start.7
  175.8 2.2 %collective-permute-start.8 = (f32[8,128]{1,0:T(8,128)S(1)}, f32[8,128]{1,0:T(8,128)S(1)}, u32[]{:S(2)}, u32[]{:S(2)}) collective-permute-start(f32[8,128]{1,0:T(8,128)S(1)} %get-tuple-element.39), channel_id=1, source_target_pairs={{0,32},{32,64},{64,96},{96,0},{1,33},{33,65},{65,97},{97,1},{2,34}... | collective-permute-start | bytes 12296 | tf_op jit(solution)/shard_map/ppermute | solution.py:64
  177.9 0.7 collective-permute-done.7
  178.7 0.6 dynamic-slice_reduce_fusion
  (43 shorter events, 1.5 us)
Async XLA Ops:
  0.0 1.6 copy-start
  22.0 10.1 %copy-start.1 = (bf16[2,512,128]{2,1,0:T(8,128)(2,1)S(1)}, bf16[2,512,128]{2,1,0:T(8,128)(2,1)}, u32[]{:S(2)}) copy-start(bf16[2,512,128]{2,1,0:T(8,128)(2,1)} %param.10) | copy-start | bytes 786436
  22.0 71.2 %all-to-all-start = ((bf16[32,128,512]{2,1,0:T(8,128)(2,1)}), bf16[32,128,512]{2,1,0:T(8,128)(2,1)}, u32[]{:S(2)}, u32[]{:S(2)}) async-start(bf16[32,128,512]{2,1,0:T(8,128)(2,1)} %fusion), calls=%async_computation | async-start | bytes 8388608 | tf_op jit(solution)/shard_map/all_to_all | solution.py:30
  32.1 60.2 %collective-permute-start = (bf16[2,512,128]{2,1,0:T(8,128)(2,1)S(1)}, bf16[2,512,128]{2,1,0:T(8,128)(2,1)S(1)}, u32[]{:S(2)}, u32[]{:S(2)}) collective-permute-start(bf16[2,512,128]{2,1,0:T(8,128)(2,1)S(1)} %copy-done.1), channel_id=1, source_target_pairs={{0,96},{32,0},{64,32},{96,64},{1,97},{33,1},{65,33},{97,65},{2,98}... | collective-permute-start | bytes 786440 | tf_op jit(solution)/shard_map/ppermute | solution.py:36
  33.1 59.2 %collective-permute-start.1 = (bf16[2,512,128]{2,1,0:T(8,128)(2,1)S(1)}, bf16[2,512,128]{2,1,0:T(8,128)(2,1)S(1)}, u32[]{:S(2)}, u32[]{:S(2)}) collective-permute-start(bf16[2,512,128]{2,1,0:T(8,128)(2,1)S(1)} %copy-done.1), channel_id=1, source_target_pairs={{0,64},{32,96},{64,0},{96,32},{1,65},{33,97},{65,1},{97,33},{2,66}... | collective-permute-start | bytes 786440 | tf_op jit(solution)/shard_map/ppermute | solution.py:36
  35.6 56.9 %collective-permute-start.2 = (bf16[2,512,128]{2,1,0:T(8,128)(2,1)S(1)}, bf16[2,512,128]{2,1,0:T(8,128)(2,1)S(1)}, u32[]{:S(2)}, u32[]{:S(2)}) collective-permute-start(bf16[2,512,128]{2,1,0:T(8,128)(2,1)S(1)} %copy-done.1), channel_id=1, source_target_pairs={{0,32},{32,64},{64,96},{96,0},{1,33},{33,65},{65,97},{97,1},{2,34}... | collective-permute-start | bytes 786440 | tf_op jit(solution)/shard_map/ppermute | solution.py:36
  96.7 8.1 %collective-permute-start.3 = (f32[128,128]{1,0:T(8,128)S(1)}, f32[128,128]{1,0:T(8,128)S(1)}, u32[]{:S(2)}, u32[]{:S(2)}) collective-permute-start(f32[128,128]{1,0:T(8,128)S(1)} %get-tuple-element.38), channel_id=1, source_target_pairs={{0,96},{32,0},{64,32},{96,64},{1,97},{33,1},{65,33},{97,65},{2,98}... | collective-permute-start | bytes 196616 | tf_op jit(solution)/shard_map/ppermute | solution.py:64
  101.5 5.1 %collective-permute-start.4 = (f32[128,128]{1,0:T(8,128)S(1)}, f32[128,128]{1,0:T(8,128)S(1)}, u32[]{:S(2)}, u32[]{:S(2)}) collective-permute-start(f32[128,128]{1,0:T(8,128)S(1)} %get-tuple-element.37), channel_id=1, source_target_pairs={{0,64},{32,96},{64,0},{96,32},{1,65},{33,97},{65,1},{97,33},{2,66}... | collective-permute-start | bytes 196616 | tf_op jit(solution)/shard_map/ppermute | solution.py:64
  102.1 4.5 %collective-permute-start.5 = (f32[128,128]{1,0:T(8,128)S(1)}, f32[128,128]{1,0:T(8,128)S(1)}, u32[]{:S(2)}, u32[]{:S(2)}) collective-permute-start(f32[128,128]{1,0:T(8,128)S(1)} %get-tuple-element.35), channel_id=1, source_target_pairs={{0,32},{32,64},{64,96},{96,0},{1,33},{33,65},{65,97},{97,1},{2,34}... | collective-permute-start | bytes 196616 | tf_op jit(solution)/shard_map/ppermute | solution.py:64
  171.3 6.6 %collective-permute-start.6 = (f32[8,128]{1,0:T(8,128)S(1)}, f32[8,128]{1,0:T(8,128)S(1)}, u32[]{:S(2)}, u32[]{:S(2)}) collective-permute-start(f32[8,128]{1,0:T(8,128)S(1)} %get-tuple-element.42), channel_id=1, source_target_pairs={{0,96},{32,0},{64,32},{96,64},{1,97},{33,1},{65,33},{97,65},{2,98}... | collective-permute-start | bytes 12296 | tf_op jit(solution)/shard_map/ppermute | solution.py:64
  174.7 4.0 %collective-permute-start.7 = (f32[8,128]{1,0:T(8,128)S(1)}, f32[8,128]{1,0:T(8,128)S(1)}, u32[]{:S(2)}, u32[]{:S(2)}) collective-permute-start(f32[8,128]{1,0:T(8,128)S(1)} %get-tuple-element.41), channel_id=1, source_target_pairs={{0,64},{32,96},{64,0},{96,32},{1,65},{33,97},{65,1},{97,33},{2,66}... | collective-permute-start | bytes 12296 | tf_op jit(solution)/shard_map/ppermute | solution.py:64
  175.8 2.9 %collective-permute-start.8 = (f32[8,128]{1,0:T(8,128)S(1)}, f32[8,128]{1,0:T(8,128)S(1)}, u32[]{:S(2)}, u32[]{:S(2)}) collective-permute-start(f32[8,128]{1,0:T(8,128)S(1)} %get-tuple-element.39), channel_id=1, source_target_pairs={{0,32},{32,64},{64,96},{96,0},{1,33},{33,65},{65,97},{97,1},{2,34}... | collective-permute-start | bytes 12296 | tf_op jit(solution)/shard_map/ppermute | solution.py:64

commit v9 on v8

--- a/solution.py
+++ b/solution.py
@@ -5,7 +5,7 @@
 
 BS = 128
 HI = lax.Precision.HIGHEST
-W_CHUNKS = 1
+W_FIRST_SPLIT = 4
 
 
 def per_device(tensor, greens, pattern, block_sizes, trial_vectors):
@@ -19,10 +19,9 @@
     col_keep = jnp.broadcast_to(pattern[0, :, 0][:, None] > 0, (block_count, BS)).reshape(basis_count)
     keep = row_live[:, None] & (col_keep & live_mask)[None, :]
 
-    chunk_rows = shard_rows // W_CHUNKS
+    first_rows = shard_rows // W_FIRST_SPLIT
     pieces = []
-    for c in range(W_CHUNKS):
-        rows = slice(c * chunk_rows, (c + 1) * chunk_rows)
+    for rows in (slice(0, first_rows), slice(first_rows, shard_rows)):
         part = jnp.einsum(
             "rsp,pk->krs", tensor[rows], trial_vectors, preferred_element_type=jnp.float32
         )

time: 181 us -> 190 us (1.050)
  local copies, waits for them, and re-layouts: 1.23 us -> 22.8 us
  waiting for transfers between devices: 56.7 us -> 47.4 us
  other arithmetic: 12.2 us -> 4.42 us
  blocking collectives: 53.6 us -> 57.5 us
  starting transfers between devices: 30.8 us -> 33.1 us
    ppermute x3, waiting for transfers between devices: 54.2 us -> 39.4 us  [per_device(): lax.ppermute(greens, 'blk', [(i, (i - s) % group_count) for i in range(gr...]
    unnamed x21 -> x27, local copies, waits for them, and re-layouts: 0.28 us -> 11.4 us
    convert_element_type x1 -> x0, other arithmetic: 6.83 us -> none  [per_device(): part.astype(jnp.bfloat16)]
    all_to_all x1 -> x2, starting transfers between devices: 10.1 us -> 15.5 us  [per_device(): lax.all_to_all(part.astype(jnp.bfloat16), 'aux', split_axis=0, concat_axi...]
    convert_element_type x0 -> x2, local copies, waits for them, and re-layouts: none -> 5 us  [per_device(): part.astype(jnp.bfloat16)]
    all_to_all x1, blocking collectives: 53.6 us -> 57.5 us  [per_device(): lax.all_to_all(z_copies, 'aux', split_axis=0, concat_axis=0, tiled=True)]
    ppermute x6, waiting for transfers between devices: 2.58 us -> 5.53 us  [_blk_exchange(): lax.ppermute(sent, 'blk', [(i, (i + s) % group_count) for i in range(grou...]
    ppermute x6, starting transfers between devices: 14.7 us -> 11.9 us  [_blk_exchange(): lax.ppermute(sent, 'blk', [(i, (i + s) % group_count) for i in range(grou...]
  transfers between devices with their start and end apart: 10 -> 11, of which waited for: 4 -> 5; matrix products, arithmetic and copies ran while one was open for 0% -> 16% of each run, Pallas kernels for 0% -> 0%
where the time goes in v9:
time: 190 us; the launch traced here: 189 us
  blocking collectives  57.5 us (30%)
  waiting for transfers between devices  47.4 us (25%)
  starting transfers between devices  33.1 us (17%)
  matrix products  23.5 us (12%)
  local copies, waits for them, and re-layouts  22.8 us (12%)
  other arithmetic  4.42 us (2%)
    all_to_all x1, blocking collectives, per_device(): lax.all_to_all(z_copies, 'aux', split_axis=0, concat_axis=0, tiled=True)  57.5 us
    ppermute x3, waiting for transfers between devices, per_device(): lax.ppermute(greens, 'blk', [(i, (i - s) % group_count) for i in range(gr...  39.4 us
    all_to_all x2, starting transfers between devices, per_device(): lax.all_to_all(part.astype(jnp.bfloat16), 'aux', split_axis=0, concat_axi...  15.5 us
    dot_general x2, matrix products, per_device(): jnp.einsum('rsp,pk->krs', tensor[rows], trial_vectors, preferred_element_...  12.7 us
    ppermute x6, starting transfers between devices, _blk_exchange(): lax.ppermute(sent, 'blk', [(i, (i + s) % group_count) for i in range(grou...  11.9 us
    unnamed x27, local copies, waits for them, and re-layouts  11.4 us
    dot_general x1, matrix products, per_device(): jnp.einsum('nsp,kns->kp', tensor, z_all, preferred_element_type=jnp.float32)  9.4 us
    ppermute x3, starting transfers between devices, per_device(): lax.ppermute(greens, 'blk', [(i, (i - s) % group_count) for i in range(gr...  5.77 us
  transfers between devices with their start and end apart: 11, of which 5 were waited for; matrix products, arithmetic and copies ran while one was open for 16% of the time, Pallas kernels for 0%

profile of v9, /device:TPU:1, one launch (start us, length us, event | category | flops | bytes accessed | tf_op | source)
XLA Modules:
  0.0 189.0 jit_solution(13983890465264867431)
XLA Ops:
  1.6 3.7 %select_convert_fusion.1 = bf16[32,32,512]{2,0,1:T(8,128)(2,1)S(1)} fusion(bf16[128,512,128]{2,1,0:T(8,128)(2,1)} %param.9, pred[32,512]{1,0:T(8,128)(4,1)S(1)} %slice.42, bf16[128,32]{0,1:T(8,128)(2,1)S(1)} %copy-done), kind=kOutput, calls=%fused_computation.10 | convolution fusion | flops 135266304 | bytes 5267456 | tf_op jit(solution)/shard_map/rsp,pk->krs/dot_general | solution.py:25
  6.9 9.9 %all-to-all-start = ((bf16[32,32,512]{2,1,0:T(8,128)(2,1)}), bf16[32,32,512]{2,1,0:T(8,128)(2,1)}, u32[]{:S(2)}, u32[]{:S(2)}) async-start(bf16[32,32,512]{2,1,0:T(8,128)(2,1)} %copy.13), calls=%async_computation | async-start | bytes 2097152 | tf_op jit(solution)/shard_map/all_to_all | solution.py:29
  16.9 9.0 %select_convert_fusion = bf16[32,96,512]{2,0,1:T(8,128)(2,1)S(1)} fusion(pred[96,512]{1,0:T(8,128)(4,1)S(1)} %slice.43, bf16[128,512,128]{2,1,0:T(8,128)(2,1)} %param.9, bf16[128,32]{0,1:T(8,128)(2,1)S(1)} %copy-done), kind=kOutput, calls=%fused_computation.3 | convolution fusion | flops 405798912 | bytes 15785984 | tf_op jit(solution)/shard_map/rsp,pk->krs/dot_general | solution.py:25
  25.9 3.4 %copy.14 = bf16[32,96,512]{2,1,0:T(8,128)(2,1)} copy(bf16[32,96,512]{2,0,1:T(8,128)(2,1)S(1)} %select_convert_fusion) | data formatting | bytes 6291456 | tf_op jit(solution)/shard_map/convert_element_type | solution.py:30
  29.3 2.5 %all-to-all-done = bf16[32,32,512]{2,1,0:T(8,128)(2,1)} async-done(((bf16[32,32,512]{2,1,0:T(8,128)(2,1)}), bf16[32,32,512]{2,1,0:T(8,128)(2,1)}, u32[]{:S(2)}, u32[]{:S(2)}) %all-to-all-start) | async-done | bytes 1048608 | tf_op jit(solution)/shard_map/all_to_all | solution.py:29
  31.8 5.5 %all-to-all-start.1 = ((bf16[32,96,512]{2,1,0:T(8,128)(2,1)}), bf16[32,96,512]{2,1,0:T(8,128)(2,1)S(1)}, u32[]{:S(2)}, u32[]{:S(2)}) async-start(bf16[32,96,512]{2,1,0:T(8,128)(2,1)} %copy.14), calls=%async_computation.1 | async-start | bytes 6291456 | tf_op jit(solution)/shard_map/all_to_all | solution.py:29
  37.4 1.8 collective-permute-start
  39.2 2.4 %collective-permute-start.2 = (bf16[2,512,128]{2,1,0:T(8,128)(2,1)S(1)}, bf16[2,512,128]{2,1,0:T(8,128)(2,1)}, u32[]{:S(2)}, u32[]{:S(2)}) collective-permute-start(bf16[2,512,128]{2,1,0:T(8,128)(2,1)S(1)} %copy-done.4), channel_id=1, source_target_pairs={{0,32},{32,64},{64,96},{96,0},{1,33},{33,65},{65,97},{97,1},{2,34}... | collective-permute-start | bytes 786440 | tf_op jit(solution)/shard_map/ppermute | solution.py:35
  43.9 38.9 %collective-permute-done = bf16[2,512,128]{2,1,0:T(8,128)(2,1)} collective-permute-done((bf16[2,512,128]{2,1,0:T(8,128)(2,1)S(1)}, bf16[2,512,128]{2,1,0:T(8,128)(2,1)}, u32[]{:S(2)}, u32[]{:S(2)}) %collective-permute-start) | collective-permute-done | bytes 262176 | tf_op jit(solution)/shard_map/ppermute | solution.py:35
  82.8 1.7 bitcast_dynamic-update-slice_fusion.4
  84.9 1.7 bitcast_dynamic-update-slice_fusion.2
  89.0 1.7 bitcast_dynamic-update-slice_fusion.5
  90.6 1.7 bitcast_dynamic-update-slice_fusion.3
  92.3 1.7 bitcast_dynamic-update-slice_fusion.1
  97.2 2.0 %copy.15 = bf16[512,512]{1,0:T(8,128)(2,1)} copy(bf16[512,512]{0,1:T(8,128)(2,1)} %slice_bitcast_fusion.2) | data formatting | bytes 1048576 | tf_op jit(solution)/shard_map/dot_general | solution.py:42
  102.4 2.4 %collective-permute-start.3 = (f32[128,128]{1,0:T(8,128)S(1)}, f32[128,128]{1,0:T(8,128)S(1)}, u32[]{:S(2)}, u32[]{:S(2)}) collective-permute-start(f32[128,128]{1,0:T(8,128)S(1)} %get-tuple-element.38), channel_id=1, source_target_pairs={{0,96},{32,0},{64,32},{96,64},{1,97},{33,1},{65,33},{97,65},{2,98}... | collective-permute-start | bytes 196616 | tf_op jit(solution)/shard_map/ppermute | solution.py:63
  105.7 2.0 %collective-permute-start.4 = (f32[128,128]{1,0:T(8,128)S(1)}, f32[128,128]{1,0:T(8,128)S(1)}, u32[]{:S(2)}, u32[]{:S(2)}) collective-permute-start(f32[128,128]{1,0:T(8,128)S(1)} %get-tuple-element.37), channel_id=1, source_target_pairs={{0,64},{32,96},{64,0},{96,32},{1,65},{33,97},{65,1},{97,33},{2,66}... | collective-permute-start | bytes 196616 | tf_op jit(solution)/shard_map/ppermute | solution.py:63
  107.7 3.6 %collective-permute-done.4 = f32[128,128]{1,0:T(8,128)S(1)} collective-permute-done((f32[128,128]{1,0:T(8,128)S(1)}, f32[128,128]{1,0:T(8,128)S(1)}, u32[]{:S(2)}, u32[]{:S(2)}) %collective-permute-start.4) | collective-permute-done | bytes 65568 | tf_op jit(solution)/shard_map/ppermute | solution.py:63
  112.6 57.5 %all_to_all.15 = bf16[32,128,512]{2,1,0:T(8,128)(2,1)S(1)} all-to-all(bf16[32,128,512]{2,1,0:T(8,128)(2,1)S(1)} %broadcast_in_dim.77), channel_id=1, replica_groups=mesh['blk'=4,'aux'=32] {'aux'}, dimensions={0} | all-to-all | bytes 8388608 | tf_op jit(solution)/shard_map/all_to_all | solution.py:48
  170.4 9.4 %fusion.10 = f32[4,8,128]{2,1,0:T(8,128)S(1)} fusion(bf16[128,512,128]{2,1,0:T(8,128)(2,1)} %param.9, bf16[32,128,512]{2,1,0:T(8,128)(2,1)S(1)} %broadcast_select_fusion), kind=kOutput, calls=%fused_computation.13 | convolution fusion | flops 536870912 | bytes 20987904 | tf_op jit(solution)/shard_map/nsp,kns->kp/dot_general | solution.py:50
  179.8 2.4 %collective-permute-start.6 = (f32[8,128]{1,0:T(8,128)S(1)}, f32[8,128]{1,0:T(8,128)S(1)}, u32[]{:S(2)}, u32[]{:S(2)}) collective-permute-start(f32[8,128]{1,0:T(8,128)S(1)} %get-tuple-element.42), channel_id=1, source_target_pairs={{0,96},{32,0},{64,32},{96,64},{1,97},{33,1},{65,33},{97,65},{2,98}... | collective-permute-start | bytes 12296 | tf_op jit(solution)/shard_map/ppermute | solution.py:63
  182.3 1.8 collective-permute-start.8
  184.0 2.4 %collective-permute-start.7 = (f32[8,128]{1,0:T(8,128)S(1)}, f32[8,128]{1,0:T(8,128)S(1)}, u32[]{:S(2)}, u32[]{:S(2)}) collective-permute-start(f32[8,128]{1,0:T(8,128)S(1)} %get-tuple-element.41), channel_id=1, source_target_pairs={{0,64},{32,96},{64,0},{96,32},{1,65},{33,97},{65,1},{97,33},{2,66}... | collective-permute-start | bytes 12296 | tf_op jit(solution)/shard_map/ppermute | solution.py:63
  186.4 1.9 collective-permute-done.7
  (56 shorter events, 17.8 us)
Async XLA Ops:
  0.0 1.6 copy-start
  6.9 24.9 %all-to-all-start = ((bf16[32,32,512]{2,1,0:T(8,128)(2,1)}), bf16[32,32,512]{2,1,0:T(8,128)(2,1)}, u32[]{:S(2)}, u32[]{:S(2)}) async-start(bf16[32,32,512]{2,1,0:T(8,128)(2,1)} %copy.13), calls=%async_computation | async-start | bytes 2097152 | tf_op jit(solution)/shard_map/all_to_all | solution.py:29
  29.3 8.1 %copy-start.4 = (bf16[2,512,128]{2,1,0:T(8,128)(2,1)S(1)}, bf16[2,512,128]{2,1,0:T(8,128)(2,1)}, u32[]{:S(2)}) copy-start(bf16[2,512,128]{2,1,0:T(8,128)(2,1)} %param.10) | copy-start | bytes 786436
  31.8 68.8 %all-to-all-start.1 = ((bf16[32,96,512]{2,1,0:T(8,128)(2,1)}), bf16[32,96,512]{2,1,0:T(8,128)(2,1)S(1)}, u32[]{:S(2)}, u32[]{:S(2)}) async-start(bf16[32,96,512]{2,1,0:T(8,128)(2,1)} %copy.14), calls=%async_computation.1 | async-start | bytes 6291456 | tf_op jit(solution)/shard_map/all_to_all | solution.py:29
  37.4 45.4 %collective-permute-start = (bf16[2,512,128]{2,1,0:T(8,128)(2,1)S(1)}, bf16[2,512,128]{2,1,0:T(8,128)(2,1)}, u32[]{:S(2)}, u32[]{:S(2)}) collective-permute-start(bf16[2,512,128]{2,1,0:T(8,128)(2,1)S(1)} %copy-done.4), channel_id=1, source_target_pairs={{0,96},{32,0},{64,32},{96,64},{1,97},{33,1},{65,33},{97,65},{2,98}... | collective-permute-start | bytes 786440 | tf_op jit(solution)/shard_map/ppermute | solution.py:35
  39.2 47.4 %collective-permute-start.2 = (bf16[2,512,128]{2,1,0:T(8,128)(2,1)S(1)}, bf16[2,512,128]{2,1,0:T(8,128)(2,1)}, u32[]{:S(2)}, u32[]{:S(2)}) collective-permute-start(bf16[2,512,128]{2,1,0:T(8,128)(2,1)S(1)} %copy-done.4), channel_id=1, source_target_pairs={{0,32},{32,64},{64,96},{96,0},{1,33},{33,65},{65,97},{97,1},{2,34}... | collective-permute-start | bytes 786440 | tf_op jit(solution)/shard_map/ppermute | solution.py:35
  41.6 43.3 %collective-permute-start.1 = (bf16[2,512,128]{2,1,0:T(8,128)(2,1)S(1)}, bf16[2,512,128]{2,1,0:T(8,128)(2,1)}, u32[]{:S(2)}, u32[]{:S(2)}) collective-permute-start(bf16[2,512,128]{2,1,0:T(8,128)(2,1)S(1)} %copy-done.4), channel_id=1, source_target_pairs={{0,64},{32,96},{64,0},{96,32},{1,65},{33,97},{65,1},{97,33},{2,66}... | collective-permute-start | bytes 786440 | tf_op jit(solution)/shard_map/ppermute | solution.py:35
  95.4 1.0 copy-start.1
  100.6 1.0 copy-start.3
  101.1 10.3 %copy-start.2 = (bf16[2,512,512]{2,1,0:T(8,128)(2,1)S(1)}, bf16[2,512,512]{2,1,0:T(8,128)(2,1)}, u32[]{:S(2)}) copy-start(bf16[2,512,512]{2,1,0:T(8,128)(2,1)} %copy-done.1) | copy-start | bytes 3145732
  102.4 5.3 %collective-permute-start.3 = (f32[128,128]{1,0:T(8,128)S(1)}, f32[128,128]{1,0:T(8,128)S(1)}, u32[]{:S(2)}, u32[]{:S(2)}) collective-permute-start(f32[128,128]{1,0:T(8,128)S(1)} %get-tuple-element.38), channel_id=1, source_target_pairs={{0,96},{32,0},{64,32},{96,64},{1,97},{33,1},{65,33},{97,65},{2,98}... | collective-permute-start | bytes 196616 | tf_op jit(solution)/shard_map/ppermute | solution.py:63
  104.7 6.6 %collective-permute-start.5 = (f32[128,128]{1,0:T(8,128)S(1)}, f32[128,128]{1,0:T(8,128)S(1)}, u32[]{:S(2)}, u32[]{:S(2)}) collective-permute-start(f32[128,128]{1,0:T(8,128)S(1)} %get-tuple-element.35), channel_id=1, source_target_pairs={{0,32},{32,64},{64,96},{96,0},{1,33},{33,65},{65,97},{97,1},{2,34}... | collective-permute-start | bytes 196616 | tf_op jit(solution)/shard_map/ppermute | solution.py:63
  105.7 5.6 %collective-permute-start.4 = (f32[128,128]{1,0:T(8,128)S(1)}, f32[128,128]{1,0:T(8,128)S(1)}, u32[]{:S(2)}, u32[]{:S(2)}) collective-permute-start(f32[128,128]{1,0:T(8,128)S(1)} %get-tuple-element.37), channel_id=1, source_target_pairs={{0,64},{32,96},{64,0},{96,32},{1,65},{33,97},{65,1},{97,33},{2,66}... | collective-permute-start | bytes 196616 | tf_op jit(solution)/shard_map/ppermute | solution.py:63
  179.8 6.6 %collective-permute-start.6 = (f32[8,128]{1,0:T(8,128)S(1)}, f32[8,128]{1,0:T(8,128)S(1)}, u32[]{:S(2)}, u32[]{:S(2)}) collective-permute-start(f32[8,128]{1,0:T(8,128)S(1)} %get-tuple-element.42), channel_id=1, source_target_pairs={{0,96},{32,0},{64,32},{96,64},{1,97},{33,1},{65,33},{97,65},{2,98}... | collective-permute-start | bytes 12296 | tf_op jit(solution)/shard_map/ppermute | solution.py:63
  182.3 6.1 %collective-permute-start.8 = (f32[8,128]{1,0:T(8,128)S(1)}, f32[8,128]{1,0:T(8,128)S(1)}, u32[]{:S(2)}, u32[]{:S(2)}) collective-permute-start(f32[8,128]{1,0:T(8,128)S(1)} %get-tuple-element.39), channel_id=1, source_target_pairs={{0,32},{32,64},{64,96},{96,0},{1,33},{33,65},{65,97},{97,1},{2,34}... | collective-permute-start | bytes 12296 | tf_op jit(solution)/shard_map/ppermute | solution.py:63
  184.0 4.3 %collective-permute-start.7 = (f32[8,128]{1,0:T(8,128)S(1)}, f32[8,128]{1,0:T(8,128)S(1)}, u32[]{:S(2)}, u32[]{:S(2)}) collective-permute-start(f32[8,128]{1,0:T(8,128)S(1)} %get-tuple-element.41), channel_id=1, source_target_pairs={{0,64},{32,96},{64,0},{96,32},{1,65},{33,97},{65,1},{97,33},{2,66}... | collective-permute-start | bytes 12296 | tf_op jit(solution)/shard_map/ppermute | solution.py:63

commit v10 on v7

--- a/solution.py
+++ b/solution.py
@@ -48,11 +48,16 @@
     z_copies = jnp.broadcast_to(z_rows.astype(jnp.bfloat16)[None], (aux_count,) + z_rows.shape)
     z_all = lax.all_to_all(z_copies, "aux", split_axis=0, concat_axis=0, tiled=True)
     z_all = jnp.where(keep[None], z_all, jnp.zeros_like(z_all))
-    terms = jnp.einsum(
-        "nsp,kns->kp", tensor, z_all, preferred_element_type=jnp.float32
-    )
-    terms = terms.reshape((group_count, -1) + terms.shape[1:])
-    return jnp.sum(_blk_exchange(terms, group_count), axis=0)
+    half = shard_rows // 2
+    total = None
+    for rows in (slice(0, half), slice(half, shard_rows)):
+        terms = jnp.einsum(
+            "nsp,kns->kp", tensor[rows], z_all[:, rows], preferred_element_type=jnp.float32
+        )
+        terms = terms.reshape((group_count, -1) + terms.shape[1:])
+        part = jnp.sum(_blk_exchange(terms, group_count), axis=0)
+        total = part if total is None else total + part
+    return total
 
 
 def _blk_exchange(blocks, group_count):

time: 177 us -> 182 us (1.028)
  starting transfers between devices: 36.6 us -> 40.5 us
  waiting for transfers between devices: 38.3 us -> 40.9 us
    ppermute x6 -> x9, starting transfers between devices: 12.7 us -> 16.6 us  [_blk_exchange(): lax.ppermute(sent, 'blk', [(i, (i + s) % group_count) for i in range(grou...]
    ppermute x6 -> x9, waiting for transfers between devices: 5.08 us -> 7.68 us  [_blk_exchange(): lax.ppermute(sent, 'blk', [(i, (i + s) % group_count) for i in range(grou...]
    dot_general x1 -> x2, matrix products: 9.4 us -> 7.88 us  [per_device(): jnp.einsum('nsp,kns->kp', tensor[rows], z_all[:, rows], preferred_element...]
    unnamed x23 -> x26, local copies, waits for them, and re-layouts: 5.15 us -> 5.13 us
  transfers between devices with their start and end apart: 11 -> 14, of which waited for: 4 -> 5; matrix products, arithmetic and copies ran while one was open for 13% -> 14% of each run, Pallas kernels for 0% -> 0%
where the time goes in v10:
time: 182 us
  blocking collectives  55 us (30%)
  waiting for transfers between devices  40.9 us (22%)
  starting transfers between devices  40.5 us (22%)
  matrix products  23.3 us (13%)
  local copies, waits for them, and re-layouts  17.1 us (9%)
  other arithmetic  4.73 us (3%)
    all_to_all x1, blocking collectives, per_device(): lax.all_to_all(z_copies, 'aux', split_axis=0, concat_axis=0, tiled=True)  55 us
    all_to_all x2, waiting for transfers between devices, per_device(): lax.all_to_all(part.astype(jnp.bfloat16), 'aux', split_axis=0, concat_axi...  19 us
    all_to_all x2, starting transfers between devices, per_device(): lax.all_to_all(part.astype(jnp.bfloat16), 'aux', split_axis=0, concat_axi...  18.1 us
    ppermute x9, starting transfers between devices, _blk_exchange(): lax.ppermute(sent, 'blk', [(i, (i + s) % group_count) for i in range(grou...  16.6 us
    ppermute x3, waiting for transfers between devices, per_device(): lax.ppermute(greens, 'blk', [(i, (i - s) % group_count) for i in range(gr...  14.3 us
    dot_general x2, matrix products, per_device(): jnp.einsum('rsp,pk->krs', tensor[rows], trial_vectors, preferred_element_...  14.1 us
    dot_general x2, matrix products, per_device(): jnp.einsum('nsp,kns->kp', tensor[rows], z_all[:, rows], preferred_element...  7.88 us
    ppermute x9, waiting for transfers between devices, _blk_exchange(): lax.ppermute(sent, 'blk', [(i, (i + s) % group_count) for i in range(grou...  7.68 us
  transfers between devices with their start and end apart: 14, of which 5 were waited for; matrix products, arithmetic and copies ran while one was open for 14% of the time, Pallas kernels for 0%

profile of v10, /device:TPU:1, one launch (start us, length us, event | category | flops | bytes accessed | tf_op | source)
XLA Modules:
  0.0 181.8 jit_solution(2467870383594562724)
XLA Ops:
  1.6 6.4 %select_convert_fusion.1 = bf16[32,64,512]{2,0,1:T(8,128)(2,1)S(1)} fusion(pred[64,512]{1,0:T(8,128)(4,1)S(1)} %get-tuple-element.40, bf16[128,512,128]{2,1,0:T(8,128)(2,1)} %param.11, bf16[128,32]{0,1:T(8,128)(2,1)S(1)} %copy-done), kind=kOutput, calls=%fused_computation.12 | convolution fusion | flops 270532608 | bytes 10526720 | tf_op jit(solution)/shard_map/rsp,pk->krs/dot_general | solution.py:26
  8.0 2.5 %copy.13 = bf16[32,64,512]{2,1,0:T(8,128)(2,1)} copy(bf16[32,64,512]{2,0,1:T(8,128)(2,1)S(1)} %select_convert_fusion.1) | data formatting | bytes 4194304 | tf_op jit(solution)/shard_map/convert_element_type | solution.py:31
  10.5 9.9 %all-to-all-start = ((bf16[32,64,512]{2,1,0:T(8,128)(2,1)}), bf16[32,64,512]{2,1,0:T(8,128)(2,1)S(1)}, u32[]{:S(2)}, u32[]{:S(2)}) async-start(bf16[32,64,512]{2,1,0:T(8,128)(2,1)} %copy.13), calls=%async_computation | async-start | bytes 4194304 | tf_op jit(solution)/shard_map/all_to_all | solution.py:30
  21.4 2.4 %collective-permute-start.2 = (bf16[2,512,128]{2,1,0:T(8,128)(2,1)S(1)}, bf16[2,512,128]{2,1,0:T(8,128)(2,1)S(1)}, u32[]{:S(2)}, u32[]{:S(2)}) collective-permute-start(bf16[2,512,128]{2,1,0:T(8,128)(2,1)S(1)} %copy-done.2), channel_id=1, source_target_pairs={{0,32},{32,64},{64,96},{96,0},{1,33},{33,65},{65,97},{97,1},{2,34}... | collective-permute-start | bytes 786440 | tf_op jit(solution)/shard_map/ppermute | solution.py:36
  23.8 2.3 %collective-permute-start.1 = (bf16[2,512,128]{2,1,0:T(8,128)(2,1)S(1)}, bf16[2,512,128]{2,1,0:T(8,128)(2,1)S(1)}, u32[]{:S(2)}, u32[]{:S(2)}) collective-permute-start(bf16[2,512,128]{2,1,0:T(8,128)(2,1)S(1)} %copy-done.2), channel_id=1, source_target_pairs={{0,64},{32,96},{64,0},{96,32},{1,65},{33,97},{65,1},{97,33},{2,66}... | collective-permute-start | bytes 786440 | tf_op jit(solution)/shard_map/ppermute | solution.py:36
  26.2 7.7 %select_convert_fusion = bf16[32,64,512]{2,0,1:T(8,128)(2,1)} fusion(pred[64,512]{1,0:T(8,128)(4,1)S(1)} %get-tuple-element.41, bf16[128,512,128]{2,1,0:T(8,128)(2,1)} %param.11, bf16[128,32]{0,1:T(8,128)(2,1)S(1)} %copy-done), kind=kOutput, calls=%fused_computation.10 | convolution fusion | flops 270532608 | bytes 10526720 | tf_op jit(solution)/shard_map/rsp,pk->krs/dot_general | solution.py:26
  34.6 4.1 %copy.14 = bf16[32,64,512]{2,1,0:T(8,128)(2,1)} copy(bf16[32,64,512]{2,0,1:T(8,128)(2,1)} %select_convert_fusion) | data formatting | bytes 4194304 | tf_op jit(solution)/shard_map/convert_element_type | solution.py:31
  38.7 14.3 %collective-permute-done = bf16[2,512,128]{2,1,0:T(8,128)(2,1)S(1)} collective-permute-done((bf16[2,512,128]{2,1,0:T(8,128)(2,1)S(1)}, bf16[2,512,128]{2,1,0:T(8,128)(2,1)S(1)}, u32[]{:S(2)}, u32[]{:S(2)}) %collective-permute-start) | collective-permute-done | bytes 262176 | tf_op jit(solution)/shard_map/ppermute | solution.py:36
  53.7 8.2 %all-to-all-start.1 = ((bf16[32,64,512]{2,1,0:T(8,128)(2,1)}), bf16[32,64,512]{2,1,0:T(8,128)(2,1)}, u32[]{:S(2)}, u32[]{:S(2)}) async-start(bf16[32,64,512]{2,1,0:T(8,128)(2,1)} %copy.14), calls=%async_computation.1 | async-start | bytes 4194304 | tf_op jit(solution)/shard_map/all_to_all | solution.py:30
  66.2 1.3 dynamic-slice_bitcast_fusion.3
  68.4 2.1 %copy.15 = bf16[512,512]{1,0:T(8,128)(2,1)} copy(bf16[512,512]{0,1:T(8,128)(2,1)} %slice_bitcast_fusion.2) | data formatting | bytes 1048576 | tf_op jit(solution)/shard_map/dot_general | solution.py:43
  70.8 19.0 %all-to-all-done.1 = bf16[32,64,512]{2,1,0:T(8,128)(2,1)} async-done(((bf16[32,64,512]{2,1,0:T(8,128)(2,1)}), bf16[32,64,512]{2,1,0:T(8,128)(2,1)}, u32[]{:S(2)}, u32[]{:S(2)}) %all-to-all-start.1) | async-done | bytes 2097184 | tf_op jit(solution)/shard_map/all_to_all | solution.py:30
  89.8 2.0 %convert_reduce_fusion = f32[64,512]{1,0:T(8,128)S(1)} fusion(bf16[32,64,512]{2,1,0:T(8,128)(2,1)} %all-to-all-done.1), kind=kLoop, calls=%fused_computation.9 | loop fusion | flops 2064384 | bytes 2228224 | tf_op jit(solution)/shard_map/reduce_sum | solution.py:33
  92.6 3.2 %collective-permute-start.5 = (f32[128,128]{1,0:T(8,128)S(1)}, f32[128,128]{1,0:T(8,128)S(1)}, u32[]{:S(2)}, u32[]{:S(2)}) collective-permute-start(f32[128,128]{1,0:T(8,128)S(1)} %get-tuple-element.36), channel_id=1, source_target_pairs={{0,32},{32,64},{64,96},{96,0},{1,33},{33,65},{65,97},{97,1},{2,34}... | collective-permute-start | bytes 196616 | tf_op jit(solution)/shard_map/ppermute | solution.py:69
  95.9 2.4 %collective-permute-start.4 = (f32[128,128]{1,0:T(8,128)S(1)}, f32[128,128]{1,0:T(8,128)S(1)}, u32[]{:S(2)}, u32[]{:S(2)}) collective-permute-start(f32[128,128]{1,0:T(8,128)S(1)} %get-tuple-element.38), channel_id=1, source_target_pairs={{0,64},{32,96},{64,0},{96,32},{1,65},{33,97},{65,1},{97,33},{2,66}... | collective-permute-start | bytes 196616 | tf_op jit(solution)/shard_map/ppermute | solution.py:69
  98.3 3.2 %collective-permute-done.4 = f32[128,128]{1,0:T(8,128)S(1)} collective-permute-done((f32[128,128]{1,0:T(8,128)S(1)}, f32[128,128]{1,0:T(8,128)S(1)}, u32[]{:S(2)}, u32[]{:S(2)}) %collective-permute-start.4) | collective-permute-done | bytes 65568 | tf_op jit(solution)/shard_map/ppermute | solution.py:69
  102.8 55.0 %all_to_all.15 = bf16[32,128,512]{2,1,0:T(8,128)(2,1)S(1)} all-to-all(bf16[32,128,512]{2,1,0:T(8,128)(2,1)S(1)} %broadcast_in_dim.70), channel_id=1, replica_groups=mesh['blk'=4,'aux'=32] {'aux'}, dimensions={0} | all-to-all | bytes 8388608 | tf_op jit(solution)/shard_map/all_to_all | solution.py:49
  157.8 5.5 %fusion.14 = f32[4,8,128]{2,1,0:T(8,128)S(1)} fusion(bf16[128,512,128]{2,1,0:T(8,128)(2,1)} %param.11, bf16[32,128,512]{2,1,0:T(8,128)(2,1)S(1)} %all_to_all.15, pred[128,512]{1,0:T(8,128)(4,1)S(1)} %broadcast_and_fusion), kind=kOutput, calls=%fused_computation.17 | convolution fusion | flops 270532608 | bytes 12664832 | tf_op jit(solution)/shard_map/nsp,kns->kp/dot_general | solution.py:54
  163.3 4.6 %collective-permute-start.8 = (f32[8,128]{1,0:T(8,128)S(1)}, f32[8,128]{1,0:T(8,128)S(1)}, u32[]{:S(2)}, u32[]{:S(2)}) collective-permute-start(f32[8,128]{1,0:T(8,128)S(1)} %get-tuple-element.46), channel_id=1, source_target_pairs={{0,32},{32,64},{64,96},{96,0},{1,33},{33,65},{65,97},{97,1},{2,34}... | collective-permute-start | bytes 12296 | tf_op jit(solution)/shard_map/ppermute | solution.py:69
  168.4 2.4 %fusion.17 = f32[4,8,128]{2,1,0:T(8,128)S(1)} fusion(bf16[128,512,128]{2,1,0:T(8,128)(2,1)S(1)} %bitcast.93, bf16[32,128,512]{2,1,0:T(8,128)(2,1)S(1)} %all_to_all.15, pred[128,512]{1,0:T(8,128)(4,1)S(1)} %broadcast_and_fusion), kind=kOutput, calls=%fused_computation.18 | convolution fusion | flops 270532608 | bytes 12664832 | tf_op jit(solution)/shard_map/nsp,kns->kp/dot_general | solution.py:54
  170.8 3.1 %collective-permute-start.11 = (f32[8,128]{1,0:T(8,128)S(1)}, f32[8,128]{1,0:T(8,128)S(1)}, u32[]{:S(2)}, u32[]{:S(2)}) collective-permute-start(f32[8,128]{1,0:T(8,128)S(1)} %get-tuple-element.42), channel_id=1, source_target_pairs={{0,32},{32,64},{64,96},{96,0},{1,33},{33,65},{65,97},{97,1},{2,34}... | collective-permute-start | bytes 12296 | tf_op jit(solution)/shard_map/ppermute | solution.py:69
  174.0 2.7 %collective-permute-start.10 = (f32[8,128]{1,0:T(8,128)S(1)}, f32[8,128]{1,0:T(8,128)S(1)}, u32[]{:S(2)}, u32[]{:S(2)}) collective-permute-start(f32[8,128]{1,0:T(8,128)S(1)} %get-tuple-element.43), channel_id=1, source_target_pairs={{0,64},{32,96},{64,0},{96,32},{1,65},{33,97},{65,1},{97,33},{2,66}... | collective-permute-start | bytes 12296 | tf_op jit(solution)/shard_map/ppermute | solution.py:69
  176.7 1.2 collective-permute-done.10
  177.9 3.2 %collective-permute-done.9 = f32[8,128]{1,0:T(8,128)S(1)} collective-permute-done((f32[8,128]{1,0:T(8,128)S(1)}, f32[8,128]{1,0:T(8,128)S(1)}, u32[]{:S(2)}, u32[]{:S(2)}) %collective-permute-start.9) | collective-permute-done | bytes 4128 | tf_op jit(solution)/shard_map/ppermute | solution.py:69
  (62 shorter events, 12.9 us)
Async XLA Ops:
  0.0 1.6 copy-start
  10.5 9.9 %copy-start.2 = (bf16[2,512,128]{2,1,0:T(8,128)(2,1)S(1)}, bf16[2,512,128]{2,1,0:T(8,128)(2,1)}, u32[]{:S(2)}) copy-start(bf16[2,512,128]{2,1,0:T(8,128)(2,1)} %param.12) | copy-start | bytes 786436
  10.5 43.3 %all-to-all-start = ((bf16[32,64,512]{2,1,0:T(8,128)(2,1)}), bf16[32,64,512]{2,1,0:T(8,128)(2,1)S(1)}, u32[]{:S(2)}, u32[]{:S(2)}) async-start(bf16[32,64,512]{2,1,0:T(8,128)(2,1)} %copy.13), calls=%async_computation | async-start | bytes 4194304 | tf_op jit(solution)/shard_map/all_to_all | solution.py:30
  20.4 32.6 %collective-permute-start = (bf16[2,512,128]{2,1,0:T(8,128)(2,1)S(1)}, bf16[2,512,128]{2,1,0:T(8,128)(2,1)S(1)}, u32[]{:S(2)}, u32[]{:S(2)}) collective-permute-start(bf16[2,512,128]{2,1,0:T(8,128)(2,1)S(1)} %copy-done.2), channel_id=1, source_target_pairs={{0,96},{32,0},{64,32},{96,64},{1,97},{33,1},{65,33},{97,65},{2,98}... | collective-permute-start | bytes 786440 | tf_op jit(solution)/shard_map/ppermute | solution.py:36
  21.4 41.2 %collective-permute-start.2 = (bf16[2,512,128]{2,1,0:T(8,128)(2,1)S(1)}, bf16[2,512,128]{2,1,0:T(8,128)(2,1)S(1)}, u32[]{:S(2)}, u32[]{:S(2)}) collective-permute-start(bf16[2,512,128]{2,1,0:T(8,128)(2,1)S(1)} %copy-done.2), channel_id=1, source_target_pairs={{0,32},{32,64},{64,96},{96,0},{1,33},{33,65},{65,97},{97,1},{2,34}... | collective-permute-start | bytes 786440 | tf_op jit(solution)/shard_map/ppermute | solution.py:36
  23.8 38.1 %collective-permute-start.1 = (bf16[2,512,128]{2,1,0:T(8,128)(2,1)S(1)}, bf16[2,512,128]{2,1,0:T(8,128)(2,1)S(1)}, u32[]{:S(2)}, u32[]{:S(2)}) collective-permute-start(bf16[2,512,128]{2,1,0:T(8,128)(2,1)S(1)} %copy-done.2), channel_id=1, source_target_pairs={{0,64},{32,96},{64,0},{96,32},{1,65},{33,97},{65,1},{97,33},{2,66}... | collective-permute-start | bytes 786440 | tf_op jit(solution)/shard_map/ppermute | solution.py:36
  53.7 36.1 %all-to-all-start.1 = ((bf16[32,64,512]{2,1,0:T(8,128)(2,1)}), bf16[32,64,512]{2,1,0:T(8,128)(2,1)}, u32[]{:S(2)}, u32[]{:S(2)}) async-start(bf16[32,64,512]{2,1,0:T(8,128)(2,1)} %copy.14), calls=%async_computation.1 | async-start | bytes 4194304 | tf_op jit(solution)/shard_map/all_to_all | solution.py:30
  70.8 21.0 %copy-start.1 = (bf16[512,512]{1,0:T(8,128)(2,1)S(1)}, bf16[512,512]{1,0:T(8,128)(2,1)}, u32[]{:S(2)}) copy-start(bf16[512,512]{1,0:T(8,128)(2,1)} %copy.15) | copy-start | bytes 1572868
  89.8 78.6 %slice-start = ((s8[16777216]{0:T(1024)(128)(4,1)}), s8[4194304]{0:T(1024)(128)(4,1)S(1)}, s32[]{:S(2)}) async-start(s8[16777216]{0:T(1024)(128)(4,1)} %bitcast.92), calls=%async_computation.3 | async-start | bytes 8388608
  92.5 5.7 %collective-permute-start.3 = (f32[128,128]{1,0:T(8,128)S(1)}, f32[128,128]{1,0:T(8,128)S(1)}, u32[]{:S(2)}, u32[]{:S(2)}) collective-permute-start(f32[128,128]{1,0:T(8,128)S(1)} %get-tuple-element.39), channel_id=1, source_target_pairs={{0,96},{32,0},{64,32},{96,64},{1,97},{33,1},{65,33},{97,65},{2,98}... | collective-permute-start | bytes 196616 | tf_op jit(solution)/shard_map/ppermute | solution.py:69
  92.6 8.9 %collective-permute-start.5 = (f32[128,128]{1,0:T(8,128)S(1)}, f32[128,128]{1,0:T(8,128)S(1)}, u32[]{:S(2)}, u32[]{:S(2)}) collective-permute-start(f32[128,128]{1,0:T(8,128)S(1)} %get-tuple-element.36), channel_id=1, source_target_pairs={{0,32},{32,64},{64,96},{96,0},{1,33},{33,65},{65,97},{97,1},{2,34}... | collective-permute-start | bytes 196616 | tf_op jit(solution)/shard_map/ppermute | solution.py:69
  95.9 5.6 %collective-permute-start.4 = (f32[128,128]{1,0:T(8,128)S(1)}, f32[128,128]{1,0:T(8,128)S(1)}, u32[]{:S(2)}, u32[]{:S(2)}) collective-permute-start(f32[128,128]{1,0:T(8,128)S(1)} %get-tuple-element.38), channel_id=1, source_target_pairs={{0,64},{32,96},{64,0},{96,32},{1,65},{33,97},{65,1},{97,33},{2,66}... | collective-permute-start | bytes 196616 | tf_op jit(solution)/shard_map/ppermute | solution.py:69
  102.3 66.1 %slice-start.1 = ((s8[16777216]{0:T(1024)(128)(4,1)}), s8[4194304]{0:T(1024)(128)(4,1)S(1)}, s32[]{:S(2)}) async-start(s8[16777216]{0:T(1024)(128)(4,1)} %bitcast.92), calls=%async_computation.4 | async-start | bytes 8388608
  102.8 65.6 %slice-start.2 = ((s8[16777216]{0:T(1024)(128)(4,1)}), s8[4194304]{0:T(1024)(128)(4,1)S(1)}, s32[]{:S(2)}) async-start(s8[16777216]{0:T(1024)(128)(4,1)} %bitcast.92), calls=%async_computation.5 | async-start | bytes 8388608
  157.8 10.6 %slice-start.3 = ((s8[16777216]{0:T(1024)(128)(4,1)}), s8[4194304]{0:T(1024)(128)(4,1)S(1)}, s32[]{:S(2)}) async-start(s8[16777216]{0:T(1024)(128)(4,1)} %bitcast.92), calls=%async_computation.6 | async-start | bytes 8388608
  163.3 13.3 %collective-permute-start.8 = (f32[8,128]{1,0:T(8,128)S(1)}, f32[8,128]{1,0:T(8,128)S(1)}, u32[]{:S(2)}, u32[]{:S(2)}) collective-permute-start(f32[8,128]{1,0:T(8,128)S(1)} %get-tuple-element.46), channel_id=1, source_target_pairs={{0,32},{32,64},{64,96},{96,0},{1,33},{33,65},{65,97},{97,1},{2,34}... | collective-permute-start | bytes 12296 | tf_op jit(solution)/shard_map/ppermute | solution.py:69
  167.9 8.7 %collective-permute-start.7 = (f32[8,128]{1,0:T(8,128)S(1)}, f32[8,128]{1,0:T(8,128)S(1)}, u32[]{:S(2)}, u32[]{:S(2)}) collective-permute-start(f32[8,128]{1,0:T(8,128)S(1)} %get-tuple-element.47), channel_id=1, source_target_pairs={{0,64},{32,96},{64,0},{96,32},{1,65},{33,97},{65,1},{97,33},{2,66}... | collective-permute-start | bytes 12296 | tf_op jit(solution)/shard_map/ppermute | solution.py:69
  168.2 8.4 %collective-permute-start.6 = (f32[8,128]{1,0:T(8,128)S(1)}, f32[8,128]{1,0:T(8,128)S(1)}, u32[]{:S(2)}, u32[]{:S(2)}) collective-permute-start(f32[8,128]{1,0:T(8,128)S(1)} %get-tuple-element.48), channel_id=1, source_target_pairs={{0,96},{32,0},{64,32},{96,64},{1,97},{33,1},{65,33},{97,65},{2,98}... | collective-permute-start | bytes 12296 | tf_op jit(solution)/shard_map/ppermute | solution.py:69
  170.8 5.9 %collective-permute-start.11 = (f32[8,128]{1,0:T(8,128)S(1)}, f32[8,128]{1,0:T(8,128)S(1)}, u32[]{:S(2)}, u32[]{:S(2)}) collective-permute-start(f32[8,128]{1,0:T(8,128)S(1)} %get-tuple-element.42), channel_id=1, source_target_pairs={{0,32},{32,64},{64,96},{96,0},{1,33},{33,65},{65,97},{97,1},{2,34}... | collective-permute-start | bytes 12296 | tf_op jit(solution)/shard_map/ppermute | solution.py:69
  174.0 4.0 %collective-permute-start.10 = (f32[8,128]{1,0:T(8,128)S(1)}, f32[8,128]{1,0:T(8,128)S(1)}, u32[]{:S(2)}, u32[]{:S(2)}) collective-permute-start(f32[8,128]{1,0:T(8,128)S(1)} %get-tuple-element.43), channel_id=1, source_target_pairs={{0,64},{32,96},{64,0},{96,32},{1,65},{33,97},{65,1},{97,33},{2,66}... | collective-permute-start | bytes 12296 | tf_op jit(solution)/shard_map/ppermute | solution.py:69
  176.6 4.5 %collective-permute-start.9 = (f32[8,128]{1,0:T(8,128)S(1)}, f32[8,128]{1,0:T(8,128)S(1)}, u32[]{:S(2)}, u32[]{:S(2)}) collective-permute-start(f32[8,128]{1,0:T(8,128)S(1)} %get-tuple-element.44), channel_id=1, source_target_pairs={{0,96},{32,0},{64,32},{96,64},{1,97},{33,1},{65,33},{97,65},{2,98}... | collective-permute-start | bytes 12296 | tf_op jit(solution)/shard_map/ppermute | solution.py:69

commit v11 on v7

--- a/solution.py
+++ b/solution.py
@@ -36,15 +36,18 @@
         lax.ppermute(greens, "blk", [(i, (i - s) % group_count) for i in range(group_count)])
         for s in range(1, group_count)
     ]
-    both = jnp.roll(jnp.stack(shifted), lax.axis_index("blk"), axis=0)
-    both = jnp.concatenate(list(both), axis=2).astype(jnp.float32)
-    occupied = both[0]
+    both = jnp.concatenate(shifted, axis=2).astype(jnp.float32)
     virtual = both[1]
     projected = jnp.dot(weighted, virtual, precision=HI)
     projected = projected.reshape(shard_rows, group_count, shard_rows).transpose(1, 0, 2)
-    projected = _blk_exchange(projected, group_count)
-    projected = projected.reshape(group_count * shard_rows, shard_rows)
-    z_rows = jnp.einsum("ln,sl->ns", projected, occupied, precision=HI)
+    got = [projected[0]]
+    for s in range(1, group_count):
+        got.append(
+            lax.ppermute(projected[s], "blk", [(i, (i + s) % group_count) for i in range(group_count)])
+        )
+    occupied = jnp.concatenate([shifted[(-s) % group_count][0] for s in range(group_count)], axis=1)
+    projected = jnp.concatenate(got, axis=0)
+    z_rows = jnp.einsum("ln,sl->ns", projected, occupied.astype(jnp.float32), precision=HI)
     z_copies = jnp.broadcast_to(z_rows.astype(jnp.bfloat16)[None], (aux_count,) + z_rows.shape)
     z_all = lax.all_to_all(z_copies, "aux", split_axis=0, concat_axis=0, tiled=True)
     z_all = jnp.where(keep[None], z_all, jnp.zeros_like(z_all))

time: 177 us -> 199 us (1.12)
  waiting for transfers between devices: 38.3 us -> 100 us
  blocking collectives: 54.7 us -> 0 us
  starting transfers between devices: 36.6 us -> 53.6 us
  local copies, waits for them, and re-layouts: 17.2 us -> 11.7 us
  other arithmetic: 4.79 us -> 6.88 us
    all_to_all x1 -> x0, blocking collectives: 54.7 us -> none  [per_device(): lax.all_to_all(z_copies, 'aux', split_axis=0, concat_axis=0, tiled=True)]
    all_to_all x0 -> x1, waiting for transfers between devices: none -> 51.6 us  [per_device(): lax.all_to_all(z_copies, 'aux', split_axis=0, concat_axis=0, tiled=True)]
    ppermute x3, waiting for transfers between devices: 14.3 us -> 26.2 us  [per_device(): lax.ppermute(greens, 'blk', [(i, (i - s) % group_count) for i in range(gr...]
    all_to_all x0 -> x1, starting transfers between devices: none -> 7.81 us  [per_device(): lax.all_to_all(z_copies, 'aux', split_axis=0, concat_axis=0, tiled=True)]
    ppermute x0 -> x3, starting transfers between devices: none -> 7.57 us  [per_device(): lax.ppermute(projected[s], 'blk', [(i, (i + s) % group_count) for i in ra...]
    ppermute x0 -> x3, waiting for transfers between devices: none -> 5.17 us  [per_device(): lax.ppermute(projected[s], 'blk', [(i, (i + s) % group_count) for i in ra...]
    unnamed x23 -> x15, local copies, waits for them, and re-layouts: 5.15 us -> 0.81 us
    ppermute x6 -> x3, waiting for transfers between devices: 5.08 us -> 0.74 us  [_blk_exchange(): lax.ppermute(sent, 'blk', [(i, (i + s) % group_count) for i in range(grou...]
  transfers between devices with their start and end apart: 11 -> 12, of which waited for: 4 -> 6; matrix products, arithmetic and copies ran while one was open for 13% -> 6% of each run, Pallas kernels for 0% -> 0%
where the time goes in v11:
time: 199 us; the launch traced here: 197 us
  waiting for transfers between devices  100 us (50%)
  starting transfers between devices  53.6 us (27%)
  matrix products  24.4 us (12%)
  local copies, waits for them, and re-layouts  11.7 us (6%)
  other arithmetic  6.88 us (3%)
    all_to_all x1, waiting for transfers between devices, per_device(): lax.all_to_all(z_copies, 'aux', split_axis=0, concat_axis=0, tiled=True)  51.6 us
    ppermute x3, waiting for transfers between devices, per_device(): lax.ppermute(greens, 'blk', [(i, (i - s) % group_count) for i in range(gr...  26.2 us
    all_to_all x2, starting transfers between devices, per_device(): lax.all_to_all(part.astype(jnp.bfloat16), 'aux', split_axis=0, concat_axi...  17.5 us
    all_to_all x2, waiting for transfers between devices, per_device(): lax.all_to_all(part.astype(jnp.bfloat16), 'aux', split_axis=0, concat_axi...  16.7 us
    ppermute x3, starting transfers between devices, _blk_exchange(): lax.ppermute(sent, 'blk', [(i, (i + s) % group_count) for i in range(grou...  14.6 us
    dot_general x2, matrix products, per_device(): jnp.einsum('rsp,pk->krs', tensor[rows], trial_vectors, preferred_element_...  12.7 us
    dot_general x1, matrix products, per_device(): jnp.einsum('nsp,kns->kp', tensor, z_all, preferred_element_type=jnp.float32)  9.4 us
    all_to_all x1, starting transfers between devices, per_device(): lax.all_to_all(z_copies, 'aux', split_axis=0, concat_axis=0, tiled=True)  7.81 us
  transfers between devices with their start and end apart: 12, of which 6 were waited for; matrix products, arithmetic and copies ran while one was open for 6% of the time, Pallas kernels for 0%

profile of v11, /device:TPU:1, one launch (start us, length us, event | category | flops | bytes accessed | tf_op | source)
XLA Modules:
  0.0 197.3 jit_solution(3625225430206140006)
XLA Ops:
  1.6 6.4 %select_convert_fusion = bf16[32,64,512]{2,0,1:T(8,128)(2,1)S(1)} fusion(pred[64,512]{1,0:T(8,128)(4,1)S(1)} %get-tuple-element.24, bf16[128,512,128]{2,1,0:T(8,128)(2,1)} %param.7, bf16[128,32]{0,1:T(8,128)(2,1)S(1)} %copy-done), kind=kOutput, calls=%fused_computation.7 | convolution fusion | flops 270532608 | bytes 10526720 | tf_op jit(solution)/shard_map/rsp,pk->krs/dot_general | solution.py:26
  8.0 2.5 %copy.14 = bf16[32,64,512]{2,1,0:T(8,128)(2,1)} copy(bf16[32,64,512]{2,0,1:T(8,128)(2,1)S(1)} %select_convert_fusion) | data formatting | bytes 4194304 | tf_op jit(solution)/shard_map/convert_element_type | solution.py:31
  10.5 9.8 %all-to-all-start.1 = ((bf16[32,64,512]{2,1,0:T(8,128)(2,1)}), bf16[32,64,512]{2,1,0:T(8,128)(2,1)S(1)}, u32[]{:S(2)}, u32[]{:S(2)}) async-start(bf16[32,64,512]{2,1,0:T(8,128)(2,1)} %copy.14), calls=%async_computation.1 | async-start | bytes 4194304 | tf_op jit(solution)/shard_map/all_to_all | solution.py:30
  20.3 6.4 %select_convert_fusion.1 = bf16[32,64,512]{2,0,1:T(8,128)(2,1)S(1)} fusion(pred[64,512]{1,0:T(8,128)(4,1)S(1)} %get-tuple-element.23, bf16[128,512,128]{2,1,0:T(8,128)(2,1)} %param.7, bf16[128,32]{0,1:T(8,128)(2,1)S(1)} %copy-done), kind=kOutput, calls=%fused_computation.9 | convolution fusion | flops 270532608 | bytes 10526720 | tf_op jit(solution)/shard_map/rsp,pk->krs/dot_general | solution.py:26
  26.6 2.5 %copy.13 = bf16[32,64,512]{2,1,0:T(8,128)(2,1)} copy(bf16[32,64,512]{2,0,1:T(8,128)(2,1)S(1)} %select_convert_fusion.1) | data formatting | bytes 4194304 | tf_op jit(solution)/shard_map/convert_element_type | solution.py:31
  29.1 16.7 %all-to-all-done.1 = bf16[32,64,512]{2,1,0:T(8,128)(2,1)S(1)} async-done(((bf16[32,64,512]{2,1,0:T(8,128)(2,1)}), bf16[32,64,512]{2,1,0:T(8,128)(2,1)S(1)}, u32[]{:S(2)}, u32[]{:S(2)}) %all-to-all-start.1) | async-done | bytes 2097184 | tf_op jit(solution)/shard_map/all_to_all | solution.py:30
  45.9 7.7 %all-to-all-start = ((bf16[32,64,512]{2,1,0:T(8,128)(2,1)}), bf16[32,64,512]{2,1,0:T(8,128)(2,1)}, u32[]{:S(2)}, u32[]{:S(2)}) async-start(bf16[32,64,512]{2,1,0:T(8,128)(2,1)} %copy.13), calls=%async_computation | async-start | bytes 4194304 | tf_op jit(solution)/shard_map/all_to_all | solution.py:30
  54.8 2.5 %collective-permute-start.1 = (bf16[2,512,128]{2,1,0:T(8,128)(2,1)S(1)}, bf16[2,512,128]{2,1,0:T(8,128)(2,1)S(1)}, u32[]{:S(2)}, u32[]{:S(2)}) collective-permute-start(bf16[2,512,128]{2,1,0:T(8,128)(2,1)S(1)} %copy-done.1), channel_id=1, source_target_pairs={{0,64},{32,96},{64,0},{96,32},{1,65},{33,97},{65,1},{97,33},{2,66}... | collective-permute-start | bytes 786440 | tf_op jit(solution)/shard_map/ppermute | solution.py:36
  57.2 2.4 %collective-permute-start.2 = (bf16[2,512,128]{2,1,0:T(8,128)(2,1)S(1)}, bf16[2,512,128]{2,1,0:T(8,128)(2,1)S(1)}, u32[]{:S(2)}, u32[]{:S(2)}) collective-permute-start(bf16[2,512,128]{2,1,0:T(8,128)(2,1)S(1)} %copy-done.1), channel_id=1, source_target_pairs={{0,32},{32,64},{64,96},{96,0},{1,33},{33,65},{65,97},{97,1},{2,34}... | collective-permute-start | bytes 786440 | tf_op jit(solution)/shard_map/ppermute | solution.py:36
  60.3 26.2 %collective-permute-done = bf16[2,512,128]{2,1,0:T(8,128)(2,1)S(1)} collective-permute-done((bf16[2,512,128]{2,1,0:T(8,128)(2,1)S(1)}, bf16[2,512,128]{2,1,0:T(8,128)(2,1)S(1)}, u32[]{:S(2)}, u32[]{:S(2)}) %collective-permute-start) | collective-permute-done | bytes 262176 | tf_op jit(solution)/shard_map/ppermute | solution.py:36
  88.6 1.6 slice_bitcast_fusion.1
  90.4 1.9 convert_reduce_fusion.1
  93.0 5.1 %collective-permute-start.3 = (f32[128,128]{1,0:T(8,128)S(1)}, f32[128,128]{1,0:T(8,128)S(1)}, u32[]{:S(2)}, u32[]{:S(2)}) collective-permute-start(f32[128,128]{1,0:T(8,128)S(1)} %get-tuple-element.22), channel_id=1, source_target_pairs={{0,32},{32,64},{64,96},{96,0},{1,33},{33,65},{65,97},{97,1},{2,34}... | collective-permute-start | bytes 196616 | tf_op jit(solution)/shard_map/ppermute | solution.py:46
  98.1 2.4 %collective-permute-start.4 = (f32[128,128]{1,0:T(8,128)S(1)}, f32[128,128]{1,0:T(8,128)S(1)}, u32[]{:S(2)}, u32[]{:S(2)}) collective-permute-start(f32[128,128]{1,0:T(8,128)S(1)} %get-tuple-element.21), channel_id=1, source_target_pairs={{0,64},{32,96},{64,0},{96,32},{1,65},{33,97},{65,1},{97,33},{2,66}... | collective-permute-start | bytes 196616 | tf_op jit(solution)/shard_map/ppermute | solution.py:46
  100.6 3.3 %collective-permute-done.4 = f32[128,128]{1,0:T(8,128)S(1)} collective-permute-done((f32[128,128]{1,0:T(8,128)S(1)}, f32[128,128]{1,0:T(8,128)S(1)}, u32[]{:S(2)}, u32[]{:S(2)}) %collective-permute-start.4) | collective-permute-done | bytes 65568 | tf_op jit(solution)/shard_map/ppermute | solution.py:46
  103.9 1.9 collective-permute-done.5
  105.8 1.6 convolution_convert_fusion
  107.4 2.4 %broadcast_in_dim.61 = bf16[32,128,512]{2,1,0:T(8,128)(2,1)} broadcast(bf16[128,512]{1,0:T(8,128)(2,1)S(1)} %convolution_convert_fusion), dimensions={1,2} | broadcast | bytes 4325376 | tf_op jit(solution)/shard_map/broadcast_in_dim | solution.py:51
  109.8 7.8 %all-to-all-start.2 = ((bf16[32,128,512]{2,1,0:T(8,128)(2,1)}), bf16[32,128,512]{2,1,0:T(8,128)(2,1)}, u32[]{:S(2)}, u32[]{:S(2)}) async-start(bf16[32,128,512]{2,1,0:T(8,128)(2,1)} %broadcast_in_dim.61), calls=%async_computation.2 | async-start | bytes 8388608 | tf_op jit(solution)/shard_map/all_to_all | solution.py:52
  117.7 51.6 %all-to-all-done.2 = bf16[32,128,512]{2,1,0:T(8,128)(2,1)} async-done(((bf16[32,128,512]{2,1,0:T(8,128)(2,1)}), bf16[32,128,512]{2,1,0:T(8,128)(2,1)}, u32[]{:S(2)}, u32[]{:S(2)}) %all-to-all-start.2) | async-done | bytes 4194336 | tf_op jit(solution)/shard_map/all_to_all | solution.py:52
  169.3 2.5 %broadcast_select_fusion = bf16[32,128,512]{2,1,0:T(8,128)(2,1)S(1)} fusion(bf16[32,128,512]{2,1,0:T(8,128)(2,1)} %all-to-all-done.2, pred[128,512]{1,0:T(8,128)(4,1)S(1)} %broadcast_and_fusion), kind=kLoop, calls=%fused_computation.10 | loop fusion | flops 2097152 | bytes 8454144 | tf_op jit(solution)/shard_map/jit(_where)/select_n | solution.py:53
  171.8 9.4 %fusion.10 = f32[4,8,128]{2,1,0:T(8,128)S(1)} fusion(bf16[128,512,128]{2,1,0:T(8,128)(2,1)} %param.7, bf16[32,128,512]{2,1,0:T(8,128)(2,1)S(1)} %broadcast_select_fusion), kind=kOutput, calls=%fused_computation.13 | convolution fusion | flops 536870912 | bytes 20987904 | tf_op jit(solution)/shard_map/nsp,kns->kp/dot_general | solution.py:54
  181.3 11.4 %collective-permute-start.7 = (f32[8,128]{1,0:T(8,128)S(1)}, f32[8,128]{1,0:T(8,128)S(1)}, u32[]{:S(2)}, u32[]{:S(2)}) collective-permute-start(f32[8,128]{1,0:T(8,128)S(1)} %get-tuple-element.27), channel_id=1, source_target_pairs={{0,64},{32,96},{64,0},{96,32},{1,65},{33,97},{65,1},{97,33},{2,66}... | collective-permute-start | bytes 12296 | tf_op jit(solution)/shard_map/ppermute | solution.py:67
  192.7 3.1 %collective-permute-start.8 = (f32[8,128]{1,0:T(8,128)S(1)}, f32[8,128]{1,0:T(8,128)S(1)}, u32[]{:S(2)}, u32[]{:S(2)}) collective-permute-start(f32[8,128]{1,0:T(8,128)S(1)} %get-tuple-element.25), channel_id=1, source_target_pairs={{0,32},{32,64},{64,96},{96,0},{1,33},{33,65},{65,97},{97,1},{2,34}... | collective-permute-start | bytes 12296 | tf_op jit(solution)/shard_map/ppermute | solution.py:67
  (42 shorter events, 7.9 us)
Async XLA Ops:
  0.0 1.6 copy-start
  10.5 35.4 %all-to-all-start.1 = ((bf16[32,64,512]{2,1,0:T(8,128)(2,1)}), bf16[32,64,512]{2,1,0:T(8,128)(2,1)S(1)}, u32[]{:S(2)}, u32[]{:S(2)}) async-start(bf16[32,64,512]{2,1,0:T(8,128)(2,1)} %copy.14), calls=%async_computation.1 | async-start | bytes 4194304 | tf_op jit(solution)/shard_map/all_to_all | solution.py:30
  26.6 27.0 %copy-start.1 = (bf16[2,512,128]{2,1,0:T(8,128)(2,1)S(1)}, bf16[2,512,128]{2,1,0:T(8,128)(2,1)}, u32[]{:S(2)}) copy-start(bf16[2,512,128]{2,1,0:T(8,128)(2,1)} %param.8) | copy-start | bytes 786436
  45.9 44.6 %all-to-all-start = ((bf16[32,64,512]{2,1,0:T(8,128)(2,1)}), bf16[32,64,512]{2,1,0:T(8,128)(2,1)}, u32[]{:S(2)}, u32[]{:S(2)}) async-start(bf16[32,64,512]{2,1,0:T(8,128)(2,1)} %copy.13), calls=%async_computation | async-start | bytes 4194304 | tf_op jit(solution)/shard_map/all_to_all | solution.py:30
  53.6 32.9 %collective-permute-start = (bf16[2,512,128]{2,1,0:T(8,128)(2,1)S(1)}, bf16[2,512,128]{2,1,0:T(8,128)(2,1)S(1)}, u32[]{:S(2)}, u32[]{:S(2)}) collective-permute-start(bf16[2,512,128]{2,1,0:T(8,128)(2,1)S(1)} %copy-done.1), channel_id=1, source_target_pairs={{0,96},{32,0},{64,32},{96,64},{1,97},{33,1},{65,33},{97,65},{2,98}... | collective-permute-start | bytes 786440 | tf_op jit(solution)/shard_map/ppermute | solution.py:36
  54.8 31.8 %collective-permute-start.1 = (bf16[2,512,128]{2,1,0:T(8,128)(2,1)S(1)}, bf16[2,512,128]{2,1,0:T(8,128)(2,1)S(1)}, u32[]{:S(2)}, u32[]{:S(2)}) collective-permute-start(bf16[2,512,128]{2,1,0:T(8,128)(2,1)S(1)} %copy-done.1), channel_id=1, source_target_pairs={{0,64},{32,96},{64,0},{96,32},{1,65},{33,97},{65,1},{97,33},{2,66}... | collective-permute-start | bytes 786440 | tf_op jit(solution)/shard_map/ppermute | solution.py:36
  57.2 29.3 %collective-permute-start.2 = (bf16[2,512,128]{2,1,0:T(8,128)(2,1)S(1)}, bf16[2,512,128]{2,1,0:T(8,128)(2,1)S(1)}, u32[]{:S(2)}, u32[]{:S(2)}) collective-permute-start(bf16[2,512,128]{2,1,0:T(8,128)(2,1)S(1)} %copy-done.1), channel_id=1, source_target_pairs={{0,32},{32,64},{64,96},{96,0},{1,33},{33,65},{65,97},{97,1},{2,34}... | collective-permute-start | bytes 786440 | tf_op jit(solution)/shard_map/ppermute | solution.py:36
  86.5 0.7 copy-start.2
  86.5 0.8 copy-start.3
  87.6 18.2 %copy-start.4 = (bf16[512,128]{1,0:T(8,128)(2,1)S(1)}, bf16[512,128]{1,0:T(8,128)(2,1)}, u32[]{:S(2)}) copy-start(bf16[512,128]{1,0:T(8,128)(2,1)} %slice_bitcast_fusion.3) | copy-start | bytes 393220
  93.0 7.6 %collective-permute-start.3 = (f32[128,128]{1,0:T(8,128)S(1)}, f32[128,128]{1,0:T(8,128)S(1)}, u32[]{:S(2)}, u32[]{:S(2)}) collective-permute-start(f32[128,128]{1,0:T(8,128)S(1)} %get-tuple-element.22), channel_id=1, source_target_pairs={{0,32},{32,64},{64,96},{96,0},{1,33},{33,65},{65,97},{97,1},{2,34}... | collective-permute-start | bytes 196616 | tf_op jit(solution)/shard_map/ppermute | solution.py:46
  98.1 5.8 %collective-permute-start.4 = (f32[128,128]{1,0:T(8,128)S(1)}, f32[128,128]{1,0:T(8,128)S(1)}, u32[]{:S(2)}, u32[]{:S(2)}) collective-permute-start(f32[128,128]{1,0:T(8,128)S(1)} %get-tuple-element.21), channel_id=1, source_target_pairs={{0,64},{32,96},{64,0},{96,32},{1,65},{33,97},{65,1},{97,33},{2,66}... | collective-permute-start | bytes 196616 | tf_op jit(solution)/shard_map/ppermute | solution.py:46
  100.6 5.2 %collective-permute-start.5 = (f32[128,128]{1,0:T(8,128)S(1)}, f32[128,128]{1,0:T(8,128)S(1)}, u32[]{:S(2)}, u32[]{:S(2)}) collective-permute-start(f32[128,128]{1,0:T(8,128)S(1)} %get-tuple-element.20), channel_id=1, source_target_pairs={{0,96},{32,0},{64,32},{96,64},{1,97},{33,1},{65,33},{97,65},{2,98}... | collective-permute-start | bytes 196616 | tf_op jit(solution)/shard_map/ppermute | solution.py:46
  109.8 59.5 %all-to-all-start.2 = ((bf16[32,128,512]{2,1,0:T(8,128)(2,1)}), bf16[32,128,512]{2,1,0:T(8,128)(2,1)}, u32[]{:S(2)}, u32[]{:S(2)}) async-start(bf16[32,128,512]{2,1,0:T(8,128)(2,1)} %broadcast_in_dim.61), calls=%async_computation.2 | async-start | bytes 8388608 | tf_op jit(solution)/shard_map/all_to_all | solution.py:52
  181.2 14.6 %collective-permute-start.6 = (f32[8,128]{1,0:T(8,128)S(1)}, f32[8,128]{1,0:T(8,128)S(1)}, u32[]{:S(2)}, u32[]{:S(2)}) collective-permute-start(f32[8,128]{1,0:T(8,128)S(1)} %get-tuple-element.28), channel_id=1, source_target_pairs={{0,96},{32,0},{64,32},{96,64},{1,97},{33,1},{65,33},{97,65},{2,98}... | collective-permute-start | bytes 12296 | tf_op jit(solution)/shard_map/ppermute | solution.py:67
  181.3 14.5 %collective-permute-start.7 = (f32[8,128]{1,0:T(8,128)S(1)}, f32[8,128]{1,0:T(8,128)S(1)}, u32[]{:S(2)}, u32[]{:S(2)}) collective-permute-start(f32[8,128]{1,0:T(8,128)S(1)} %get-tuple-element.27), channel_id=1, source_target_pairs={{0,64},{32,96},{64,0},{96,32},{1,65},{33,97},{65,1},{97,33},{2,66}... | collective-permute-start | bytes 12296 | tf_op jit(solution)/shard_map/ppermute | solution.py:67
  192.7 3.9 %collective-permute-start.8 = (f32[8,128]{1,0:T(8,128)S(1)}, f32[8,128]{1,0:T(8,128)S(1)}, u32[]{:S(2)}, u32[]{:S(2)}) collective-permute-start(f32[8,128]{1,0:T(8,128)S(1)} %get-tuple-element.25), channel_id=1, source_target_pairs={{0,32},{32,64},{64,96},{96,0},{1,33},{33,65},{65,97},{97,1},{2,34}... | collective-permute-start | bytes 12296 | tf_op jit(solution)/shard_map/ppermute | solution.py:67

commit v12 on v7

--- a/solution.py
+++ b/solution.py
@@ -52,7 +52,14 @@
         "nsp,kns->kp", tensor, z_all, preferred_element_type=jnp.float32
     )
     terms = terms.reshape((group_count, -1) + terms.shape[1:])
-    return jnp.sum(_blk_exchange(terms, group_count), axis=0)
+    me = lax.axis_index("blk")
+    total = jnp.take(terms, me, axis=0)
+    for s in range(1, group_count):
+        sent = jnp.take(terms, (me + s) % group_count, axis=0)
+        total = total + lax.ppermute(
+            sent, "blk", [(i, (i + s) % group_count) for i in range(group_count)]
+        )
+    return total
 
 
 def _blk_exchange(blocks, group_count):

time: 177 us -> 178 us (level)
  waiting for transfers between devices: 38.3 us -> 40.5 us
  starting transfers between devices: 36.6 us -> 34.5 us
    ppermute x6 -> x3, starting transfers between devices: 12.7 us -> 5.71 us  [_blk_exchange(): lax.ppermute(sent, 'blk', [(i, (i + s) % group_count) for i in range(grou...]
    ppermute x0 -> x3, starting transfers between devices: none -> 4.92 us  [per_device(): lax.ppermute(sent, 'blk', [(i, (i + s) % group_count) for i in range(grou...]
    ppermute x0 -> x3, waiting for transfers between devices: none -> 4.09 us  [per_device(): lax.ppermute(sent, 'blk', [(i, (i + s) % group_count) for i in range(grou...]
    ppermute x6 -> x3, waiting for transfers between devices: 5.08 us -> 3.22 us  [_blk_exchange(): lax.ppermute(sent, 'blk', [(i, (i + s) % group_count) for i in range(grou...]
    unnamed x23 -> x18, local copies, waits for them, and re-layouts: 5.15 us -> 5.14 us
  transfers between devices with their start and end apart: 11 -> 11, of which waited for: 4 -> 5; matrix products, arithmetic and copies ran while one was open for 13% -> 13% of each run, Pallas kernels for 0% -> 0%
where the time goes in v12:
time: 178 us; the launch traced here: 177 us
  blocking collectives  54.7 us (31%)
  waiting for transfers between devices  40.5 us (23%)
  starting transfers between devices  34.5 us (19%)
  matrix products  24.8 us (14%)
  local copies, waits for them, and re-layouts  17.2 us (10%)
  other arithmetic  4.78 us (3%)
    all_to_all x1, blocking collectives, per_device(): lax.all_to_all(z_copies, 'aux', split_axis=0, concat_axis=0, tiled=True)  54.7 us
    all_to_all x2, waiting for transfers between devices, per_device(): lax.all_to_all(part.astype(jnp.bfloat16), 'aux', split_axis=0, concat_axi...  18.9 us
    all_to_all x2, starting transfers between devices, per_device(): lax.all_to_all(part.astype(jnp.bfloat16), 'aux', split_axis=0, concat_axi...  18.1 us
    ppermute x3, waiting for transfers between devices, per_device(): lax.ppermute(greens, 'blk', [(i, (i - s) % group_count) for i in range(gr...  14.3 us
    dot_general x2, matrix products, per_device(): jnp.einsum('rsp,pk->krs', tensor[rows], trial_vectors, preferred_element_...  14.1 us
    dot_general x1, matrix products, per_device(): jnp.einsum('nsp,kns->kp', tensor, z_all, preferred_element_type=jnp.float32)  9.4 us
    convert_element_type x2, local copies, waits for them, and re-layouts, per_device(): part.astype(jnp.bfloat16)  6.58 us
    ppermute x3, starting transfers between devices, per_device(): lax.ppermute(greens, 'blk', [(i, (i - s) % group_count) for i in range(gr...  5.77 us
  transfers between devices with their start and end apart: 11, of which 5 were waited for; matrix products, arithmetic and copies ran while one was open for 13% of the time, Pallas kernels for 0%

profile of v12, /device:TPU:1, one launch (start us, length us, event | category | flops | bytes accessed | tf_op | source)
XLA Modules:
  0.0 176.7 jit_solution(1463044289085058171)
XLA Ops:
  1.6 6.4 %select_convert_fusion.1 = bf16[32,64,512]{2,0,1:T(8,128)(2,1)S(1)} fusion(pred[64,512]{1,0:T(8,128)(4,1)S(1)} %get-tuple-element.39, bf16[128,512,128]{2,1,0:T(8,128)(2,1)} %param.9, bf16[128,32]{0,1:T(8,128)(2,1)S(1)} %copy-done), kind=kOutput, calls=%fused_computation.9 | convolution fusion | flops 270532608 | bytes 10526720 | tf_op jit(solution)/shard_map/rsp,pk->krs/dot_general | solution.py:26
  8.0 2.5 %copy.13 = bf16[32,64,512]{2,1,0:T(8,128)(2,1)} copy(bf16[32,64,512]{2,0,1:T(8,128)(2,1)S(1)} %select_convert_fusion.1) | data formatting | bytes 4194304 | tf_op jit(solution)/shard_map/convert_element_type | solution.py:31
  10.5 9.9 %all-to-all-start = ((bf16[32,64,512]{2,1,0:T(8,128)(2,1)}), bf16[32,64,512]{2,1,0:T(8,128)(2,1)S(1)}, u32[]{:S(2)}, u32[]{:S(2)}) async-start(bf16[32,64,512]{2,1,0:T(8,128)(2,1)} %copy.13), calls=%async_computation | async-start | bytes 4194304 | tf_op jit(solution)/shard_map/all_to_all | solution.py:30
  20.4 1.0 collective-permute-start
  21.4 2.4 %collective-permute-start.2 = (bf16[2,512,128]{2,1,0:T(8,128)(2,1)S(1)}, bf16[2,512,128]{2,1,0:T(8,128)(2,1)S(1)}, u32[]{:S(2)}, u32[]{:S(2)}) collective-permute-start(bf16[2,512,128]{2,1,0:T(8,128)(2,1)S(1)} %copy-done.2), channel_id=1, source_target_pairs={{0,32},{32,64},{64,96},{96,0},{1,33},{33,65},{65,97},{97,1},{2,34}... | collective-permute-start | bytes 786440 | tf_op jit(solution)/shard_map/ppermute | solution.py:36
  23.9 2.3 %collective-permute-start.1 = (bf16[2,512,128]{2,1,0:T(8,128)(2,1)S(1)}, bf16[2,512,128]{2,1,0:T(8,128)(2,1)S(1)}, u32[]{:S(2)}, u32[]{:S(2)}) collective-permute-start(bf16[2,512,128]{2,1,0:T(8,128)(2,1)S(1)} %copy-done.2), channel_id=1, source_target_pairs={{0,64},{32,96},{64,0},{96,32},{1,65},{33,97},{65,1},{97,33},{2,66}... | collective-permute-start | bytes 786440 | tf_op jit(solution)/shard_map/ppermute | solution.py:36
  26.2 7.7 %select_convert_fusion = bf16[32,64,512]{2,0,1:T(8,128)(2,1)} fusion(pred[64,512]{1,0:T(8,128)(4,1)S(1)} %get-tuple-element.40, bf16[128,512,128]{2,1,0:T(8,128)(2,1)} %param.9, bf16[128,32]{0,1:T(8,128)(2,1)S(1)} %copy-done), kind=kOutput, calls=%fused_computation.7 | convolution fusion | flops 270532608 | bytes 10526720 | tf_op jit(solution)/shard_map/rsp,pk->krs/dot_general | solution.py:26
  34.6 4.1 %copy.14 = bf16[32,64,512]{2,1,0:T(8,128)(2,1)} copy(bf16[32,64,512]{2,0,1:T(8,128)(2,1)} %select_convert_fusion) | data formatting | bytes 4194304 | tf_op jit(solution)/shard_map/convert_element_type | solution.py:31
  38.7 14.3 %collective-permute-done = bf16[2,512,128]{2,1,0:T(8,128)(2,1)S(1)} collective-permute-done((bf16[2,512,128]{2,1,0:T(8,128)(2,1)S(1)}, bf16[2,512,128]{2,1,0:T(8,128)(2,1)S(1)}, u32[]{:S(2)}, u32[]{:S(2)}) %collective-permute-start) | collective-permute-done | bytes 262176 | tf_op jit(solution)/shard_map/ppermute | solution.py:36
  53.7 8.2 %all-to-all-start.1 = ((bf16[32,64,512]{2,1,0:T(8,128)(2,1)}), bf16[32,64,512]{2,1,0:T(8,128)(2,1)}, u32[]{:S(2)}, u32[]{:S(2)}) async-start(bf16[32,64,512]{2,1,0:T(8,128)(2,1)} %copy.14), calls=%async_computation.1 | async-start | bytes 4194304 | tf_op jit(solution)/shard_map/all_to_all | solution.py:30
  61.9 0.7 bitcast_dynamic-update-slice_fusion.2
  63.4 0.7 bitcast_dynamic-update-slice_fusion.7
  66.3 1.3 dynamic-slice_bitcast_fusion.3
  67.7 0.8 slice_bitcast_fusion.2
  68.5 2.0 %copy.15 = bf16[512,512]{1,0:T(8,128)(2,1)} copy(bf16[512,512]{0,1:T(8,128)(2,1)} %slice_bitcast_fusion.2) | data formatting | bytes 1048576 | tf_op jit(solution)/shard_map/dot_general | solution.py:43
  70.9 18.9 %all-to-all-done.1 = bf16[32,64,512]{2,1,0:T(8,128)(2,1)} async-done(((bf16[32,64,512]{2,1,0:T(8,128)(2,1)}), bf16[32,64,512]{2,1,0:T(8,128)(2,1)}, u32[]{:S(2)}, u32[]{:S(2)}) %all-to-all-start.1) | async-done | bytes 2097184 | tf_op jit(solution)/shard_map/all_to_all | solution.py:30
  89.8 1.9 %convert_reduce_fusion = f32[64,512]{1,0:T(8,128)S(1)} fusion(bf16[32,64,512]{2,1,0:T(8,128)(2,1)} %all-to-all-done.1), kind=kLoop, calls=%fused_computation.6 | loop fusion | flops 2064384 | bytes 2228224 | tf_op jit(solution)/shard_map/reduce_sum | solution.py:33
  92.5 3.2 %collective-permute-start.5 = (f32[128,128]{1,0:T(8,128)S(1)}, f32[128,128]{1,0:T(8,128)S(1)}, u32[]{:S(2)}, u32[]{:S(2)}) collective-permute-start(f32[128,128]{1,0:T(8,128)S(1)} %get-tuple-element.35), channel_id=1, source_target_pairs={{0,32},{32,64},{64,96},{96,0},{1,33},{33,65},{65,97},{97,1},{2,34}... | collective-permute-start | bytes 196616 | tf_op jit(solution)/shard_map/ppermute | solution.py:71
  95.7 2.4 %collective-permute-start.4 = (f32[128,128]{1,0:T(8,128)S(1)}, f32[128,128]{1,0:T(8,128)S(1)}, u32[]{:S(2)}, u32[]{:S(2)}) collective-permute-start(f32[128,128]{1,0:T(8,128)S(1)} %get-tuple-element.37), channel_id=1, source_target_pairs={{0,64},{32,96},{64,0},{96,32},{1,65},{33,97},{65,1},{97,33},{2,66}... | collective-permute-start | bytes 196616 | tf_op jit(solution)/shard_map/ppermute | solution.py:71
  98.1 3.2 %collective-permute-done.4 = f32[128,128]{1,0:T(8,128)S(1)} collective-permute-done((f32[128,128]{1,0:T(8,128)S(1)}, f32[128,128]{1,0:T(8,128)S(1)}, u32[]{:S(2)}, u32[]{:S(2)}) %collective-permute-start.4) | collective-permute-done | bytes 65568 | tf_op jit(solution)/shard_map/ppermute | solution.py:71
  102.6 54.7 %all_to_all.15 = bf16[32,128,512]{2,1,0:T(8,128)(2,1)S(1)} all-to-all(bf16[32,128,512]{2,1,0:T(8,128)(2,1)S(1)} %broadcast_in_dim.70), channel_id=1, replica_groups=mesh['blk'=4,'aux'=32] {'aux'}, dimensions={0} | all-to-all | bytes 8388608 | tf_op jit(solution)/shard_map/all_to_all | solution.py:49
  157.6 9.4 %fusion.10 = f32[4,8,128]{2,1,0:T(8,128)S(1)} fusion(bf16[128,512,128]{2,1,0:T(8,128)(2,1)} %param.9, bf16[32,128,512]{2,1,0:T(8,128)(2,1)S(1)} %broadcast_select_fusion), kind=kOutput, calls=%fused_computation.13 | convolution fusion | flops 536870912 | bytes 20987904 | tf_op jit(solution)/shard_map/nsp,kns->kp/dot_general | solution.py:51
  167.1 4.5 %collective-permute-start.6 = (f32[8,128]{1,0:T(8,128)S(1)}, f32[8,128]{1,0:T(8,128)S(1)}, u32[]{:S(2)}, u32[]{:S(2)}) collective-permute-start(f32[8,128]{1,0:T(8,128)S(1)} %get-tuple-element.41), channel_id=1, source_target_pairs={{0,32},{32,64},{64,96},{96,0},{1,33},{33,65},{65,97},{97,1},{2,34}... | collective-permute-start | bytes 12296 | tf_op jit(solution)/shard_map/ppermute | solution.py:59
  172.3 3.8 %collective-permute-done.8 = f32[8,128]{1,0:T(8,128)S(1)} collective-permute-done((f32[8,128]{1,0:T(8,128)S(1)}, f32[8,128]{1,0:T(8,128)S(1)}, u32[]{:S(2)}, u32[]{:S(2)}) %collective-permute-start.8) | collective-permute-done | bytes 4128 | tf_op jit(solution)/shard_map/ppermute | solution.py:59
  (44 shorter events, 10.0 us)
Async XLA Ops:
  0.0 1.6 copy-start
  10.5 9.9 %copy-start.2 = (bf16[2,512,128]{2,1,0:T(8,128)(2,1)S(1)}, bf16[2,512,128]{2,1,0:T(8,128)(2,1)}, u32[]{:S(2)}) copy-start(bf16[2,512,128]{2,1,0:T(8,128)(2,1)} %param.10) | copy-start | bytes 786436
  10.5 43.3 %all-to-all-start = ((bf16[32,64,512]{2,1,0:T(8,128)(2,1)}), bf16[32,64,512]{2,1,0:T(8,128)(2,1)S(1)}, u32[]{:S(2)}, u32[]{:S(2)}) async-start(bf16[32,64,512]{2,1,0:T(8,128)(2,1)} %copy.13), calls=%async_computation | async-start | bytes 4194304 | tf_op jit(solution)/shard_map/all_to_all | solution.py:30
  20.4 32.6 %collective-permute-start = (bf16[2,512,128]{2,1,0:T(8,128)(2,1)S(1)}, bf16[2,512,128]{2,1,0:T(8,128)(2,1)S(1)}, u32[]{:S(2)}, u32[]{:S(2)}) collective-permute-start(bf16[2,512,128]{2,1,0:T(8,128)(2,1)S(1)} %copy-done.2), channel_id=1, source_target_pairs={{0,96},{32,0},{64,32},{96,64},{1,97},{33,1},{65,33},{97,65},{2,98}... | collective-permute-start | bytes 786440 | tf_op jit(solution)/shard_map/ppermute | solution.py:36
  21.4 41.2 %collective-permute-start.2 = (bf16[2,512,128]{2,1,0:T(8,128)(2,1)S(1)}, bf16[2,512,128]{2,1,0:T(8,128)(2,1)S(1)}, u32[]{:S(2)}, u32[]{:S(2)}) collective-permute-start(bf16[2,512,128]{2,1,0:T(8,128)(2,1)S(1)} %copy-done.2), channel_id=1, source_target_pairs={{0,32},{32,64},{64,96},{96,0},{1,33},{33,65},{65,97},{97,1},{2,34}... | collective-permute-start | bytes 786440 | tf_op jit(solution)/shard_map/ppermute | solution.py:36
  23.9 38.1 %collective-permute-start.1 = (bf16[2,512,128]{2,1,0:T(8,128)(2,1)S(1)}, bf16[2,512,128]{2,1,0:T(8,128)(2,1)S(1)}, u32[]{:S(2)}, u32[]{:S(2)}) collective-permute-start(bf16[2,512,128]{2,1,0:T(8,128)(2,1)S(1)} %copy-done.2), channel_id=1, source_target_pairs={{0,64},{32,96},{64,0},{96,32},{1,65},{33,97},{65,1},{97,33},{2,66}... | collective-permute-start | bytes 786440 | tf_op jit(solution)/shard_map/ppermute | solution.py:36
  53.7 36.1 %all-to-all-start.1 = ((bf16[32,64,512]{2,1,0:T(8,128)(2,1)}), bf16[32,64,512]{2,1,0:T(8,128)(2,1)}, u32[]{:S(2)}, u32[]{:S(2)}) async-start(bf16[32,64,512]{2,1,0:T(8,128)(2,1)} %copy.14), calls=%async_computation.1 | async-start | bytes 4194304 | tf_op jit(solution)/shard_map/all_to_all | solution.py:30
  70.9 20.8 %copy-start.1 = (bf16[512,512]{1,0:T(8,128)(2,1)S(1)}, bf16[512,512]{1,0:T(8,128)(2,1)}, u32[]{:S(2)}) copy-start(bf16[512,512]{1,0:T(8,128)(2,1)} %copy.15) | copy-start | bytes 1572868
  92.4 5.7 %collective-permute-start.3 = (f32[128,128]{1,0:T(8,128)S(1)}, f32[128,128]{1,0:T(8,128)S(1)}, u32[]{:S(2)}, u32[]{:S(2)}) collective-permute-start(f32[128,128]{1,0:T(8,128)S(1)} %get-tuple-element.38), channel_id=1, source_target_pairs={{0,96},{32,0},{64,32},{96,64},{1,97},{33,1},{65,33},{97,65},{2,98}... | collective-permute-start | bytes 196616 | tf_op jit(solution)/shard_map/ppermute | solution.py:71
  92.5 8.9 %collective-permute-start.5 = (f32[128,128]{1,0:T(8,128)S(1)}, f32[128,128]{1,0:T(8,128)S(1)}, u32[]{:S(2)}, u32[]{:S(2)}) collective-permute-start(f32[128,128]{1,0:T(8,128)S(1)} %get-tuple-element.35), channel_id=1, source_target_pairs={{0,32},{32,64},{64,96},{96,0},{1,33},{33,65},{65,97},{97,1},{2,34}... | collective-permute-start | bytes 196616 | tf_op jit(solution)/shard_map/ppermute | solution.py:71
  95.7 5.6 %collective-permute-start.4 = (f32[128,128]{1,0:T(8,128)S(1)}, f32[128,128]{1,0:T(8,128)S(1)}, u32[]{:S(2)}, u32[]{:S(2)}) collective-permute-start(f32[128,128]{1,0:T(8,128)S(1)} %get-tuple-element.37), channel_id=1, source_target_pairs={{0,64},{32,96},{64,0},{96,32},{1,65},{33,97},{65,1},{97,33},{2,66}... | collective-permute-start | bytes 196616 | tf_op jit(solution)/shard_map/ppermute | solution.py:71
  167.1 5.2 %collective-permute-start.6 = (f32[8,128]{1,0:T(8,128)S(1)}, f32[8,128]{1,0:T(8,128)S(1)}, u32[]{:S(2)}, u32[]{:S(2)}) collective-permute-start(f32[8,128]{1,0:T(8,128)S(1)} %get-tuple-element.41), channel_id=1, source_target_pairs={{0,32},{32,64},{64,96},{96,0},{1,33},{33,65},{65,97},{97,1},{2,34}... | collective-permute-start | bytes 12296 | tf_op jit(solution)/shard_map/ppermute | solution.py:59
  171.6 4.5 %collective-permute-start.8 = (f32[8,128]{1,0:T(8,128)S(1)}, f32[8,128]{1,0:T(8,128)S(1)}, u32[]{:S(2)}, u32[]{:S(2)}) collective-permute-start(f32[8,128]{1,0:T(8,128)S(1)} %get-tuple-element.42), channel_id=1, source_target_pairs={{0,96},{32,0},{64,32},{96,64},{1,97},{33,1},{65,33},{97,65},{2,98}... | collective-permute-start | bytes 12296 | tf_op jit(solution)/shard_map/ppermute | solution.py:59
  171.6 4.5 %collective-permute-start.7 = (f32[8,128]{1,0:T(8,128)S(1)}, f32[8,128]{1,0:T(8,128)S(1)}, u32[]{:S(2)}, u32[]{:S(2)}) collective-permute-start(f32[8,128]{1,0:T(8,128)S(1)} %get-tuple-element.43), channel_id=1, source_target_pairs={{0,64},{32,96},{64,0},{96,32},{1,65},{33,97},{65,1},{97,33},{2,66}... | collective-permute-start | bytes 12296 | tf_op jit(solution)/shard_map/ppermute | solution.py:59

commit v13 on v7

--- a/solution.py
+++ b/solution.py
@@ -31,7 +31,6 @@
             part.astype(jnp.bfloat16), "aux", split_axis=0, concat_axis=0, tiled=True
         )
         pieces.append(jnp.sum(part.astype(jnp.float32), axis=0))
-    weighted = jnp.concatenate(pieces, axis=0)
     shifted = [greens] + [
         lax.ppermute(greens, "blk", [(i, (i - s) % group_count) for i in range(group_count)])
         for s in range(1, group_count)
@@ -40,10 +39,12 @@
     both = jnp.concatenate(list(both), axis=2).astype(jnp.float32)
     occupied = both[0]
     virtual = both[1]
-    projected = jnp.dot(weighted, virtual, precision=HI)
-    projected = projected.reshape(shard_rows, group_count, shard_rows).transpose(1, 0, 2)
-    projected = _blk_exchange(projected, group_count)
-    projected = projected.reshape(group_count * shard_rows, shard_rows)
+    moved = []
+    for piece in pieces:
+        part = jnp.dot(piece, virtual, precision=HI)
+        part = part.reshape(piece.shape[0], group_count, shard_rows).transpose(1, 0, 2)
+        moved.append(_blk_exchange(part, group_count))
+    projected = jnp.concatenate(moved, axis=1).reshape(group_count * shard_rows, shard_rows)
     z_rows = jnp.einsum("ln,sl->ns", projected, occupied, precision=HI)
     z_copies = jnp.broadcast_to(z_rows.astype(jnp.bfloat16)[None], (aux_count,) + z_rows.shape)
     z_all = lax.all_to_all(z_copies, "aux", split_axis=0, concat_axis=0, tiled=True)

time: 177 us -> 183 us (1.034)
  waiting for transfers between devices: 38.3 us -> 42.2 us
  starting transfers between devices: 36.6 us -> 39.4 us
    ppermute x6 -> x9, starting transfers between devices: 12.7 us -> 16.1 us  [_blk_exchange(): lax.ppermute(sent, 'blk', [(i, (i + s) % group_count) for i in range(grou...]
    ppermute x3, waiting for transfers between devices: 14.3 us -> 17.2 us  [per_device(): lax.ppermute(greens, 'blk', [(i, (i - s) % group_count) for i in range(gr...]
    dot_general x2, local copies, waits for them, and re-layouts: 2.88 us -> 0.25 us  [per_device(): part = jnp.dot(piece, virtual, precision=HI)]
    ppermute x6 -> x9, waiting for transfers between devices: 5.08 us -> 7.3 us  [_blk_exchange(): lax.ppermute(sent, 'blk', [(i, (i + s) % group_count) for i in range(grou...]
    unnamed x23 -> x20, local copies, waits for them, and re-layouts: 5.15 us -> 6.09 us
  transfers between devices with their start and end apart: 11 -> 14, of which waited for: 4 -> 6; matrix products, arithmetic and copies ran while one was open for 13% -> 11% of each run, Pallas kernels for 0% -> 0%
where the time goes in v13:
time: 183 us
  blocking collectives  54.9 us (30%)
  waiting for transfers between devices  42.2 us (23%)
  starting transfers between devices  39.4 us (22%)
  matrix products  25.4 us (14%)
  local copies, waits for them, and re-layouts  15.5 us (8%)
  other arithmetic  4.98 us (3%)
    all_to_all x1, blocking collectives, per_device(): lax.all_to_all(z_copies, 'aux', split_axis=0, concat_axis=0, tiled=True)  54.9 us
    all_to_all x2, waiting for transfers between devices, per_device(): lax.all_to_all(part.astype(jnp.bfloat16), 'aux', split_axis=0, concat_axi...  17.7 us
    all_to_all x2, starting transfers between devices, per_device(): lax.all_to_all(part.astype(jnp.bfloat16), 'aux', split_axis=0, concat_axi...  17.6 us
    ppermute x3, waiting for transfers between devices, per_device(): lax.ppermute(greens, 'blk', [(i, (i - s) % group_count) for i in range(gr...  17.2 us
    ppermute x9, starting transfers between devices, _blk_exchange(): lax.ppermute(sent, 'blk', [(i, (i + s) % group_count) for i in range(grou...  16.1 us
    dot_general x2, matrix products, per_device(): jnp.einsum('rsp,pk->krs', tensor[rows], trial_vectors, preferred_element_...  14.1 us
    dot_general x1, matrix products, per_device(): jnp.einsum('nsp,kns->kp', tensor, z_all, preferred_element_type=jnp.float32)  9.4 us
    ppermute x9, waiting for transfers between devices, _blk_exchange(): lax.ppermute(sent, 'blk', [(i, (i + s) % group_count) for i in range(grou...  7.3 us
  transfers between devices with their start and end apart: 14, of which 6 were waited for; matrix products, arithmetic and copies ran while one was open for 11% of the time, Pallas kernels for 0%

profile of v13, /device:TPU:1, one launch (start us, length us, event | category | flops | bytes accessed | tf_op | source)
XLA Modules:
  0.0 182.6 jit_solution(4343318677681774107)
XLA Ops:
  1.6 6.4 %select_convert_fusion = bf16[32,64,512]{2,0,1:T(8,128)(2,1)S(1)} fusion(pred[64,512]{1,0:T(8,128)(4,1)S(1)} %get-tuple-element.45, bf16[128,512,128]{2,1,0:T(8,128)(2,1)} %param.11, bf16[128,32]{0,1:T(8,128)(2,1)S(1)} %copy-done), kind=kOutput, calls=%fused_computation.7 | convolution fusion | flops 270532608 | bytes 10526720 | tf_op jit(solution)/shard_map/rsp,pk->krs/dot_general | solution.py:26
  8.0 2.5 %copy.15 = bf16[32,64,512]{2,1,0:T(8,128)(2,1)} copy(bf16[32,64,512]{2,0,1:T(8,128)(2,1)S(1)} %select_convert_fusion) | data formatting | bytes 4194304 | tf_op jit(solution)/shard_map/convert_element_type | solution.py:31
  10.5 9.9 %all-to-all-start.1 = ((bf16[32,64,512]{2,1,0:T(8,128)(2,1)}), bf16[32,64,512]{2,1,0:T(8,128)(2,1)S(1)}, u32[]{:S(2)}, u32[]{:S(2)}) async-start(bf16[32,64,512]{2,1,0:T(8,128)(2,1)} %copy.15), calls=%async_computation.1 | async-start | bytes 4194304 | tf_op jit(solution)/shard_map/all_to_all | solution.py:30
  21.5 2.4 %collective-permute-start.2 = (bf16[2,512,128]{2,1,0:T(8,128)(2,1)S(1)}, bf16[2,512,128]{2,1,0:T(8,128)(2,1)S(1)}, u32[]{:S(2)}, u32[]{:S(2)}) collective-permute-start(bf16[2,512,128]{2,1,0:T(8,128)(2,1)S(1)} %copy-done.3), channel_id=1, source_target_pairs={{0,32},{32,64},{64,96},{96,0},{1,33},{33,65},{65,97},{97,1},{2,34}... | collective-permute-start | bytes 786440 | tf_op jit(solution)/shard_map/ppermute | solution.py:35
  23.9 2.3 %collective-permute-start.1 = (bf16[2,512,128]{2,1,0:T(8,128)(2,1)S(1)}, bf16[2,512,128]{2,1,0:T(8,128)(2,1)S(1)}, u32[]{:S(2)}, u32[]{:S(2)}) collective-permute-start(bf16[2,512,128]{2,1,0:T(8,128)(2,1)S(1)} %copy-done.3), channel_id=1, source_target_pairs={{0,64},{32,96},{64,0},{96,32},{1,65},{33,97},{65,1},{97,33},{2,66}... | collective-permute-start | bytes 786440 | tf_op jit(solution)/shard_map/ppermute | solution.py:35
  26.2 7.7 %select_convert_fusion.1 = bf16[32,64,512]{2,0,1:T(8,128)(2,1)} fusion(pred[64,512]{1,0:T(8,128)(4,1)S(1)} %get-tuple-element.44, bf16[128,512,128]{2,1,0:T(8,128)(2,1)} %param.11, bf16[128,32]{0,1:T(8,128)(2,1)S(1)} %copy-done), kind=kOutput, calls=%fused_computation.9 | convolution fusion | flops 270532608 | bytes 10526720 | tf_op jit(solution)/shard_map/rsp,pk->krs/dot_general | solution.py:26
  34.6 4.1 %copy.13 = bf16[32,64,512]{2,1,0:T(8,128)(2,1)} copy(bf16[32,64,512]{2,0,1:T(8,128)(2,1)} %select_convert_fusion.1) | data formatting | bytes 4194304 | tf_op jit(solution)/shard_map/convert_element_type | solution.py:31
  38.7 14.3 %collective-permute-done = bf16[2,512,128]{2,1,0:T(8,128)(2,1)S(1)} collective-permute-done((bf16[2,512,128]{2,1,0:T(8,128)(2,1)S(1)}, bf16[2,512,128]{2,1,0:T(8,128)(2,1)S(1)}, u32[]{:S(2)}, u32[]{:S(2)}) %collective-permute-start) | collective-permute-done | bytes 262176 | tf_op jit(solution)/shard_map/ppermute | solution.py:35
  53.7 2.9 %collective-permute-done.1 = bf16[2,512,128]{2,1,0:T(8,128)(2,1)S(1)} collective-permute-done((bf16[2,512,128]{2,1,0:T(8,128)(2,1)S(1)}, bf16[2,512,128]{2,1,0:T(8,128)(2,1)S(1)}, u32[]{:S(2)}, u32[]{:S(2)}) %collective-permute-start.1) | collective-permute-done | bytes 262176 | tf_op jit(solution)/shard_map/ppermute | solution.py:35
  57.4 7.6 %all-to-all-start = ((bf16[32,64,512]{2,1,0:T(8,128)(2,1)}), bf16[32,64,512]{2,1,0:T(8,128)(2,1)}, u32[]{:S(2)}, u32[]{:S(2)}) async-start(bf16[32,64,512]{2,1,0:T(8,128)(2,1)} %copy.13), calls=%async_computation | async-start | bytes 4194304 | tf_op jit(solution)/shard_map/all_to_all | solution.py:30
  68.7 1.3 dynamic-slice_bitcast_fusion.3
  72.2 17.7 %all-to-all-done = bf16[32,64,512]{2,1,0:T(8,128)(2,1)} async-done(((bf16[32,64,512]{2,1,0:T(8,128)(2,1)}), bf16[32,64,512]{2,1,0:T(8,128)(2,1)}, u32[]{:S(2)}, u32[]{:S(2)}) %all-to-all-start) | async-done | bytes 2097184 | tf_op jit(solution)/shard_map/all_to_all | solution.py:30
  89.9 1.9 %convert_reduce_fusion.1 = f32[64,512]{1,0:T(8,128)S(1)} fusion(bf16[32,64,512]{2,1,0:T(8,128)(2,1)} %all-to-all-done), kind=kLoop, calls=%fused_computation.8 | loop fusion | flops 2064384 | bytes 2228224 | tf_op jit(solution)/shard_map/reduce_sum | solution.py:33
  92.4 5.1 %collective-permute-start.8 = (f32[64,128]{1,0:T(8,128)S(1)}, f32[64,128]{1,0:T(8,128)S(1)}, u32[]{:S(2)}, u32[]{:S(2)}) collective-permute-start(f32[64,128]{1,0:T(8,128)S(1)} %get-tuple-element.40), channel_id=1, source_target_pairs={{0,32},{32,64},{64,96},{96,0},{1,33},{33,65},{65,97},{97,1},{2,34}... | collective-permute-start | bytes 98312 | tf_op jit(solution)/shard_map/ppermute | solution.py:65
  97.5 1.2 collective-permute-start.7
  98.8 3.3 %collective-permute-start.5 = (f32[64,128]{1,0:T(8,128)S(1)}, f32[64,128]{1,0:T(8,128)S(1)}, u32[]{:S(2)}, u32[]{:S(2)}) collective-permute-start(f32[64,128]{1,0:T(8,128)S(1)} %get-tuple-element.36), channel_id=1, source_target_pairs={{0,32},{32,64},{64,96},{96,0},{1,33},{33,65},{65,97},{97,1},{2,34}... | collective-permute-start | bytes 98312 | tf_op jit(solution)/shard_map/ppermute | solution.py:65
  102.1 1.7 collective-permute-start.4
  104.0 2.4 %collective-permute-done.4 = f32[64,128]{1,0:T(8,128)S(1)} collective-permute-done((f32[64,128]{1,0:T(8,128)S(1)}, f32[64,128]{1,0:T(8,128)S(1)}, u32[]{:S(2)}, u32[]{:S(2)}) %collective-permute-start.4) | collective-permute-done | bytes 32800 | tf_op jit(solution)/shard_map/ppermute | solution.py:65
  106.4 2.3 %collective-permute-done.3 = f32[64,128]{1,0:T(8,128)S(1)} collective-permute-done((f32[64,128]{1,0:T(8,128)S(1)}, f32[64,128]{1,0:T(8,128)S(1)}, u32[]{:S(2)}, u32[]{:S(2)}) %collective-permute-start.3) | collective-permute-done | bytes 32800 | tf_op jit(solution)/shard_map/ppermute | solution.py:65
  110.0 54.9 %all_to_all.15 = bf16[32,128,512]{2,1,0:T(8,128)(2,1)S(1)} all-to-all(bf16[32,128,512]{2,1,0:T(8,128)(2,1)S(1)} %broadcast_in_dim.70), channel_id=1, replica_groups=mesh['blk'=4,'aux'=32] {'aux'}, dimensions={0} | all-to-all | bytes 8388608 | tf_op jit(solution)/shard_map/all_to_all | solution.py:50
  165.2 9.4 %fusion.10 = f32[4,8,128]{2,1,0:T(8,128)S(1)} fusion(bf16[128,512,128]{2,1,0:T(8,128)(2,1)} %param.11, bf16[32,128,512]{2,1,0:T(8,128)(2,1)S(1)} %broadcast_select_fusion), kind=kOutput, calls=%fused_computation.14 | convolution fusion | flops 536870912 | bytes 20987904 | tf_op jit(solution)/shard_map/nsp,kns->kp/dot_general | solution.py:52
  174.9 3.1 %collective-permute-start.11 = (f32[8,128]{1,0:T(8,128)S(1)}, f32[8,128]{1,0:T(8,128)S(1)}, u32[]{:S(2)}, u32[]{:S(2)}) collective-permute-start(f32[8,128]{1,0:T(8,128)S(1)} %get-tuple-element.46), channel_id=1, source_target_pairs={{0,32},{32,64},{64,96},{96,0},{1,33},{33,65},{65,97},{97,1},{2,34}... | collective-permute-start | bytes 12296 | tf_op jit(solution)/shard_map/ppermute | solution.py:65
  178.0 1.4 collective-permute-start.10
  179.4 2.6 %collective-permute-done.10 = f32[8,128]{1,0:T(8,128)S(1)} collective-permute-done((f32[8,128]{1,0:T(8,128)S(1)}, f32[8,128]{1,0:T(8,128)S(1)}, u32[]{:S(2)}, u32[]{:S(2)}) %collective-permute-start.10) | collective-permute-done | bytes 4128 | tf_op jit(solution)/shard_map/ppermute | solution.py:65
  (56 shorter events, 13.8 us)
Async XLA Ops:
  0.0 1.6 copy-start
  10.5 9.9 %copy-start.3 = (bf16[2,512,128]{2,1,0:T(8,128)(2,1)S(1)}, bf16[2,512,128]{2,1,0:T(8,128)(2,1)}, u32[]{:S(2)}) copy-start(bf16[2,512,128]{2,1,0:T(8,128)(2,1)} %param.12) | copy-start | bytes 786436
  10.5 46.9 %all-to-all-start.1 = ((bf16[32,64,512]{2,1,0:T(8,128)(2,1)}), bf16[32,64,512]{2,1,0:T(8,128)(2,1)S(1)}, u32[]{:S(2)}, u32[]{:S(2)}) async-start(bf16[32,64,512]{2,1,0:T(8,128)(2,1)} %copy.15), calls=%async_computation.1 | async-start | bytes 4194304 | tf_op jit(solution)/shard_map/all_to_all | solution.py:30
  20.4 32.6 %collective-permute-start = (bf16[2,512,128]{2,1,0:T(8,128)(2,1)S(1)}, bf16[2,512,128]{2,1,0:T(8,128)(2,1)S(1)}, u32[]{:S(2)}, u32[]{:S(2)}) collective-permute-start(bf16[2,512,128]{2,1,0:T(8,128)(2,1)S(1)} %copy-done.3), channel_id=1, source_target_pairs={{0,96},{32,0},{64,32},{96,64},{1,97},{33,1},{65,33},{97,65},{2,98}... | collective-permute-start | bytes 786440 | tf_op jit(solution)/shard_map/ppermute | solution.py:35
  21.5 43.6 %collective-permute-start.2 = (bf16[2,512,128]{2,1,0:T(8,128)(2,1)S(1)}, bf16[2,512,128]{2,1,0:T(8,128)(2,1)S(1)}, u32[]{:S(2)}, u32[]{:S(2)}) collective-permute-start(bf16[2,512,128]{2,1,0:T(8,128)(2,1)S(1)} %copy-done.3), channel_id=1, source_target_pairs={{0,32},{32,64},{64,96},{96,0},{1,33},{33,65},{65,97},{97,1},{2,34}... | collective-permute-start | bytes 786440 | tf_op jit(solution)/shard_map/ppermute | solution.py:35
  23.9 32.8 %collective-permute-start.1 = (bf16[2,512,128]{2,1,0:T(8,128)(2,1)S(1)}, bf16[2,512,128]{2,1,0:T(8,128)(2,1)S(1)}, u32[]{:S(2)}, u32[]{:S(2)}) collective-permute-start(bf16[2,512,128]{2,1,0:T(8,128)(2,1)S(1)} %copy-done.3), channel_id=1, source_target_pairs={{0,64},{32,96},{64,0},{96,32},{1,65},{33,97},{65,1},{97,33},{2,66}... | collective-permute-start | bytes 786440 | tf_op jit(solution)/shard_map/ppermute | solution.py:35
  57.4 32.5 %all-to-all-start = ((bf16[32,64,512]{2,1,0:T(8,128)(2,1)}), bf16[32,64,512]{2,1,0:T(8,128)(2,1)}, u32[]{:S(2)}, u32[]{:S(2)}) async-start(bf16[32,64,512]{2,1,0:T(8,128)(2,1)} %copy.13), calls=%async_computation | async-start | bytes 4194304 | tf_op jit(solution)/shard_map/all_to_all | solution.py:30
  70.1 1.0 copy-start.1
  72.2 36.6 %copy-start.2 = (bf16[2,512,512]{2,1,0:T(8,128)(2,1)S(1)}, bf16[2,512,512]{2,1,0:T(8,128)(2,1)}, u32[]{:S(2)}) copy-start(bf16[2,512,512]{2,1,0:T(8,128)(2,1)} %copy-done.1) | copy-start | bytes 3145732
  92.4 11.4 %collective-permute-start.8 = (f32[64,128]{1,0:T(8,128)S(1)}, f32[64,128]{1,0:T(8,128)S(1)}, u32[]{:S(2)}, u32[]{:S(2)}) collective-permute-start(f32[64,128]{1,0:T(8,128)S(1)} %get-tuple-element.40), channel_id=1, source_target_pairs={{0,32},{32,64},{64,96},{96,0},{1,33},{33,65},{65,97},{97,1},{2,34}... | collective-permute-start | bytes 98312 | tf_op jit(solution)/shard_map/ppermute | solution.py:65
  97.5 6.3 %collective-permute-start.7 = (f32[64,128]{1,0:T(8,128)S(1)}, f32[64,128]{1,0:T(8,128)S(1)}, u32[]{:S(2)}, u32[]{:S(2)}) collective-permute-start(f32[64,128]{1,0:T(8,128)S(1)} %get-tuple-element.41), channel_id=1, source_target_pairs={{0,64},{32,96},{64,0},{96,32},{1,65},{33,97},{65,1},{97,33},{2,66}... | collective-permute-start | bytes 98312 | tf_op jit(solution)/shard_map/ppermute | solution.py:65
  98.8 5.1 %collective-permute-start.6 = (f32[64,128]{1,0:T(8,128)S(1)}, f32[64,128]{1,0:T(8,128)S(1)}, u32[]{:S(2)}, u32[]{:S(2)}) collective-permute-start(f32[64,128]{1,0:T(8,128)S(1)} %get-tuple-element.42), channel_id=1, source_target_pairs={{0,96},{32,0},{64,32},{96,64},{1,97},{33,1},{65,33},{97,65},{2,98}... | collective-permute-start | bytes 98312 | tf_op jit(solution)/shard_map/ppermute | solution.py:65
  98.8 5.2 %collective-permute-start.5 = (f32[64,128]{1,0:T(8,128)S(1)}, f32[64,128]{1,0:T(8,128)S(1)}, u32[]{:S(2)}, u32[]{:S(2)}) collective-permute-start(f32[64,128]{1,0:T(8,128)S(1)} %get-tuple-element.36), channel_id=1, source_target_pairs={{0,32},{32,64},{64,96},{96,0},{1,33},{33,65},{65,97},{97,1},{2,34}... | collective-permute-start | bytes 98312 | tf_op jit(solution)/shard_map/ppermute | solution.py:65
  102.1 4.3 %collective-permute-start.4 = (f32[64,128]{1,0:T(8,128)S(1)}, f32[64,128]{1,0:T(8,128)S(1)}, u32[]{:S(2)}, u32[]{:S(2)}) collective-permute-start(f32[64,128]{1,0:T(8,128)S(1)} %get-tuple-element.37), channel_id=1, source_target_pairs={{0,64},{32,96},{64,0},{96,32},{1,65},{33,97},{65,1},{97,33},{2,66}... | collective-permute-start | bytes 98312 | tf_op jit(solution)/shard_map/ppermute | solution.py:65
  103.9 4.8 %collective-permute-start.3 = (f32[64,128]{1,0:T(8,128)S(1)}, f32[64,128]{1,0:T(8,128)S(1)}, u32[]{:S(2)}, u32[]{:S(2)}) collective-permute-start(f32[64,128]{1,0:T(8,128)S(1)} %get-tuple-element.38), channel_id=1, source_target_pairs={{0,96},{32,0},{64,32},{96,64},{1,97},{33,1},{65,33},{97,65},{2,98}... | collective-permute-start | bytes 98312 | tf_op jit(solution)/shard_map/ppermute | solution.py:65
  174.7 4.7 %collective-permute-start.9 = (f32[8,128]{1,0:T(8,128)S(1)}, f32[8,128]{1,0:T(8,128)S(1)}, u32[]{:S(2)}, u32[]{:S(2)}) collective-permute-start(f32[8,128]{1,0:T(8,128)S(1)} %get-tuple-element.49), channel_id=1, source_target_pairs={{0,96},{32,0},{64,32},{96,64},{1,97},{33,1},{65,33},{97,65},{2,98}... | collective-permute-start | bytes 12296 | tf_op jit(solution)/shard_map/ppermute | solution.py:65
  174.9 7.1 %collective-permute-start.11 = (f32[8,128]{1,0:T(8,128)S(1)}, f32[8,128]{1,0:T(8,128)S(1)}, u32[]{:S(2)}, u32[]{:S(2)}) collective-permute-start(f32[8,128]{1,0:T(8,128)S(1)} %get-tuple-element.46), channel_id=1, source_target_pairs={{0,32},{32,64},{64,96},{96,0},{1,33},{33,65},{65,97},{97,1},{2,34}... | collective-permute-start | bytes 12296 | tf_op jit(solution)/shard_map/ppermute | solution.py:65
  178.0 4.0 %collective-permute-start.10 = (f32[8,128]{1,0:T(8,128)S(1)}, f32[8,128]{1,0:T(8,128)S(1)}, u32[]{:S(2)}, u32[]{:S(2)}) collective-permute-start(f32[8,128]{1,0:T(8,128)S(1)} %get-tuple-element.48), channel_id=1, source_target_pairs={{0,64},{32,96},{64,0},{96,32},{1,65},{33,97},{65,1},{97,33},{2,66}... | collective-permute-start | bytes 12296 | tf_op jit(solution)/shard_map/ppermute | solution.py:65
